TPU v7x, 512 devices: a whole 4x8x8 slice. The times are simulated.
512 devices in a mesh: row: 64 (over x, y, core), col: 8 (over z).
Axes of the slice: x: 4, y: 8, z: 8, core: 2. Of those that a mesh axis runs over, the one named last changes fastest.
Arguments:
- grad_out: bfloat16 [2048, 12288], P('row', 'col'), may hold values from -3.5 to 3.5
- pre_act: bfloat16 [2048, 24576], P('col', 'row'), may hold values from -6 to 6
- down_weight: bfloat16 [24576, 12288], P('row', 'col'), may hold values from -0.0546875 to 0.0546875
Outputs:
- grad_pre: bfloat16 [2048, 24576], P('col', 'row')
- grad_weight: bfloat16 [24576, 12288], P('row', 'col')
All inputs are finite; a program needn't handle non-finite values.
Results may differ from a plain program's by a relative error of at most 0.015.
Values may be sent and summed in bfloat16 or wider, within the bound.
No kernel may reach another device: no remote copies, remote signals or barrier semaphores. Data moves between devices by JAX's collectives and lax.ppermute only.
A program may use at most 64 MiB of HBM per device.

v0:
```python
import jax
import jax.numpy as jnp
from jax import lax
from jax.sharding import PartitionSpec as P

coef = 0.7978845608
cubic = 0.044715


def gelu_fwd(x):
    return 0.5 * x * (1.0 + jnp.tanh(coef * (x + cubic * x * x * x)))


def gelu_grad(x):
    inner = coef * (x + cubic * x * x * x)
    tangent = jnp.tanh(inner)
    return 0.5 * (1.0 + tangent) + 0.5 * x * (1.0 - tangent * tangent) * coef * (
        1.0 + 3.0 * cubic * x * x
    )


def body(grad_out, pre_act, down_weight):
    grad_all = lax.all_gather(grad_out, "row", axis=0, tiled=True)
    pre_all = lax.all_gather(pre_act, "col", axis=0, tiled=True)
    hidden = gelu_fwd(pre_all.astype(jnp.float32)).astype(jnp.bfloat16)
    grad_weight = lax.dot_general(
        hidden, grad_all, (((0,), (0,)), ((), ())), preferred_element_type=jnp.float32
    ).astype(jnp.bfloat16)
    share_rows = pre_act.shape[0]
    partial_term = lax.dot_general(
        grad_all, down_weight, (((1,), (1,)), ((), ())), preferred_element_type=jnp.float32
    )
    summed = lax.psum(partial_term.astype(jnp.bfloat16), "col").astype(jnp.float32)
    offset = lax.axis_index("col") * share_rows
    grad_hidden = lax.dynamic_slice_in_dim(summed, offset, share_rows, 0)
    grad_pre = (grad_hidden * gelu_grad(pre_act.astype(jnp.float32))).astype(jnp.bfloat16)
    return (grad_pre, grad_weight)


def solution(mesh):
    in_specs = (P("row", "col"), P("col", "row"), P("row", "col"))
    out_specs = (P("col", "row"), P("row", "col"))
    return jax.shard_map(body, mesh=mesh, in_specs=in_specs, out_specs=out_specs, check_vma=False)
```

profile of v0, /device:TPU:6, one launch (start us, length us, event | category | flops | bytes accessed | tf_op | source)
XLA Modules:
  0.0 237.7 jit_solution(11160524972806360876)
XLA Ops:
  7.2 0.0 copy-start
  7.2 0.0 all-gather.3.cloned.1.call-start
  7.2 0.7 all-gather.3.cloned.1.call-update
  7.9 0.0 all-gather.5.cloned.1.call-start
  8.0 0.7 all-gather.5.cloned.1.call-update
  8.7 0.0 all-reduce.2.cloned.1.call-start
  8.7 91.4 %all-gather.3.cloned.1.call-done = bf16[2048,1536]{1,0:T(8,128)(2,1)} async-done(((bf16[32,1536]{1,0:T(8,128)(2,1)}), bf16[2048,1536]{1,0:T(8,128)(2,1)}) %all-gather.3.cloned.1.call-update) | async-done | bytes 6291472 | tf_op jit(solution)/shard_map/all_gather | solution.py:23
  100.1 0.0 copy-done
  100.1 7.4 %convolution_convert_fusion.1 = bf16[2048,384]{1,0:T(8,128)(2,1)} fusion(bf16[2048,1536]{1,0:T(8,128)(2,1)} %all-gather.3.cloned.1.call-done, bf16[384,1536]{1,0:T(8,128)(2,1)S(1)} %copy-done), kind=kOutput, calls=%fused_computation.11 | convolution fusion | flops 2416705536 | bytes 9043968 | tf_op jit(solution)/shard_map/dot_general | solution.py:30
  107.5 0.0 all-reduce.2.cloned.1.call-update
  107.5 0.0 copy-start.1
  107.6 36.3 %all-gather.5.cloned.1.call-done = bf16[2048,384]{1,0:T(8,128)(2,1)} async-done(((bf16[256,384]{1,0:T(8,128)(2,1)}), bf16[2048,384]{1,0:T(8,128)(2,1)}) %all-gather.5.cloned.1.call-update) | async-done | bytes 1572880 | tf_op jit(solution)/shard_map/all_gather | solution.py:24
  143.9 7.0 %convolution_convert_fusion = bf16[384,1536]{1,0:T(8,128)(2,1)} fusion(bf16[2048,1536]{1,0:T(8,128)(2,1)} %all-gather.3.cloned.1.call-done, bf16[2048,384]{1,0:T(8,128)(2,1)} %all-gather.5.cloned.1.call-done), kind=kOutput, calls=%fused_computation.10 | convolution fusion | flops 2424373248 | bytes 9043968 | tf_op jit(solution)/shard_map/dot_general | solution.py:26
  150.9 78.4 %all-reduce.2.cloned.1.call-done = bf16[2048,384]{1,0:T(8,128)(2,1)} async-done(((bf16[2048,384]{1,0:T(8,128)(2,1)}), bf16[2048,384]{1,0:T(8,128)(2,1)}) %all-reduce.2.cloned.1.call-update) | async-done | bytes 1572880 | tf_op jit(solution)/shard_map/psum | solution.py:33
  229.3 0.0 copy-done.1
  229.3 1.9 fusion.17
Async XLA Ops:
  7.2 92.9 %copy-start = (bf16[384,1536]{1,0:T(8,128)(2,1)S(1)}, bf16[384,1536]{1,0:T(8,128)(2,1)}, u32[]{:S(2)}) copy-start(bf16[384,1536]{1,0:T(8,128)(2,1)} %param.5) | copy-start | bytes 3538948
  7.2 92.9 %all-gather.3.cloned.1.call-start = ((), (), s32[]{:S(2)}) async-start(), calls=%async_computation | async-start | bytes 6389760 | tf_op jit(solution)/shard_map/all_gather | solution.py:23
  7.9 136.0 %all-gather.5.cloned.1.call-start = ((), (), s32[]{:S(2)}) async-start(), calls=%async_computation.2 | async-start | bytes 1769472 | tf_op jit(solution)/shard_map/all_gather | solution.py:24
  8.7 220.6 %all-reduce.2.cloned.1.call-start = ((), (), s32[]{:S(2)}) async-start(), calls=%async_computation.1 | async-start | bytes 3145728 | tf_op jit(solution)/shard_map/psum | solution.py:33
  107.5 121.7 %copy-start.1 = (bf16[256,384]{1,0:T(8,128)(2,1)S(1)}, bf16[256,384]{1,0:T(8,128)(2,1)}, u32[]{:S(2)}) copy-start(bf16[256,384]{1,0:T(8,128)(2,1)} %param.4) | copy-start | bytes 589828
Sparse Core Ops, SparseCore 0:
  11.3 88.7 all-gather.2
  102.2 41.6 all-gather.4
  146.3 82.9 all-reduce.1
where the time goes:
time: 238 us
  waiting for transfers between devices  208 us (87%)
  matrix products  14.4 us (6%)
  between operations  13.8 us (6%)
    all_gather x1, waiting for transfers between devices, body(): grad_all = lax.all_gather(grad_out, 'row', axis=0, tiled=True)  91.4 us
    psum x1, waiting for transfers between devices, body(): lax.psum(partial_term.astype(jnp.bfloat16), 'col').astype(jnp.float32)  78.4 us
    all_gather x1, waiting for transfers between devices, body(): pre_all = lax.all_gather(pre_act, 'col', axis=0, tiled=True)  36.3 us
    dot_general x1, matrix products, body(): lax.dot_general(grad_all, down_weight, (((1,), (1,)), ((), ())), preferre...  7.4 us
    dot_general x1, matrix products, body(): lax.dot_general(hidden, grad_all, (((0,), (0,)), ((), ())), preferred_ele...  6.99 us
  transfers between devices with their start and end apart: 3, of which 3 were waited for; matrix products, arithmetic and copies ran while one was open for 6% of the time, Pallas kernels for 0%

commit v1 on v0

--- a/solution.py
+++ b/solution.py
@@ -26,13 +26,12 @@
     grad_weight = lax.dot_general(
         hidden, grad_all, (((0,), (0,)), ((), ())), preferred_element_type=jnp.float32
     ).astype(jnp.bfloat16)
-    share_rows = pre_act.shape[0]
     partial_term = lax.dot_general(
         grad_all, down_weight, (((1,), (1,)), ((), ())), preferred_element_type=jnp.float32
     )
-    summed = lax.psum(partial_term.astype(jnp.bfloat16), "col").astype(jnp.float32)
-    offset = lax.axis_index("col") * share_rows
-    grad_hidden = lax.dynamic_slice_in_dim(summed, offset, share_rows, 0)
+    grad_hidden = lax.psum_scatter(
+        partial_term.astype(jnp.bfloat16), "col", scatter_dimension=0, tiled=True
+    ).astype(jnp.float32)
     grad_pre = (grad_hidden * gelu_grad(pre_act.astype(jnp.float32))).astype(jnp.bfloat16)
     return (grad_pre, grad_weight)
 

time: 238 us -> 198 us (0.83)
  waiting for transfers between devices: 208 us -> 167 us
    psum x1 -> x0, waiting for transfers between devices: 78.4 us -> none  [body(): lax.psum(partial_term.astype(jnp.bfloat16), 'col').astype(jnp.float32)]
    reduce_scatter x0 -> x1, waiting for transfers between devices: none -> 38.1 us  [body(): lax.psum_scatter(partial_term.astype(jnp.bfloat16), 'col', scatter_dimens...]
  transfers between devices with their start and end apart: 3 -> 3, of which waited for: 3 -> 3; matrix products, arithmetic and copies ran while one was open for 6% -> 7% of each run, Pallas kernels for 0% -> 0%
where the time goes in v1:
time: 198 us; the launch traced here: 197 us
  waiting for transfers between devices  167 us (84%)
  matrix products  14.5 us (7%)
  between operations  13.8 us (7%)
    all_gather x1, waiting for transfers between devices, body(): grad_all = lax.all_gather(grad_out, 'row', axis=0, tiled=True)  91.4 us
    reduce_scatter x1, waiting for transfers between devices, body(): lax.psum_scatter(partial_term.astype(jnp.bfloat16), 'col', scatter_dimens...  38.1 us
    all_gather x1, waiting for transfers between devices, body(): pre_all = lax.all_gather(pre_act, 'col', axis=0, tiled=True)  36.3 us
    dot_general x1, matrix products, body(): lax.dot_general(grad_all, down_weight, (((1,), (1,)), ((), ())), preferre...  7.48 us
    dot_general x1, matrix products, body(): lax.dot_general(hidden, grad_all, (((0,), (0,)), ((), ())), preferred_ele...  6.99 us
  transfers between devices with their start and end apart: 3, of which 3 were waited for; matrix products, arithmetic and copies ran while one was open for 7% of the time, Pallas kernels for 0%

profile of v1, /device:TPU:6, one launch (start us, length us, event | category | flops | bytes accessed | tf_op | source)
XLA Modules:
  0.0 197.4 jit_solution(17193629523569997921)
XLA Ops:
  7.2 0.0 copy-start
  7.2 0.0 all-gather.3.cloned.1.call-start
  7.2 0.7 all-gather.3.cloned.1.call-update
  7.9 0.0 all-gather.5.cloned.1.call-start
  8.0 0.7 all-gather.5.cloned.1.call-update
  8.7 0.0 reduce-scatter.2.cloned.1.call-start
  8.7 91.4 %all-gather.3.cloned.1.call-done = bf16[2048,1536]{1,0:T(8,128)(2,1)} async-done(((bf16[32,1536]{1,0:T(8,128)(2,1)}), bf16[2048,1536]{1,0:T(8,128)(2,1)}) %all-gather.3.cloned.1.call-update) | async-done | bytes 6291472 | tf_op jit(solution)/shard_map/all_gather | solution.py:23
  100.1 0.0 copy-done
  100.1 7.5 %convolution_convert_fusion.1 = bf16[2048,384]{1,0:T(8,128)(2,1)} fusion(bf16[2048,1536]{1,0:T(8,128)(2,1)} %all-gather.3.cloned.1.call-done, bf16[384,1536]{1,0:T(8,128)(2,1)S(1)} %copy-done), kind=kOutput, calls=%fused_computation.11 | convolution fusion | flops 2416705536 | bytes 9043968 | tf_op jit(solution)/shard_map/dot_general | solution.py:29
  107.6 0.0 reduce-scatter.2.cloned.1.call-update
  107.6 0.0 copy-start.1
  107.6 36.3 %all-gather.5.cloned.1.call-done = bf16[2048,384]{1,0:T(8,128)(2,1)} async-done(((bf16[256,384]{1,0:T(8,128)(2,1)}), bf16[2048,384]{1,0:T(8,128)(2,1)}) %all-gather.5.cloned.1.call-update) | async-done | bytes 1572880 | tf_op jit(solution)/shard_map/all_gather | solution.py:24
  143.9 7.0 %convolution_convert_fusion = bf16[384,1536]{1,0:T(8,128)(2,1)} fusion(bf16[2048,1536]{1,0:T(8,128)(2,1)} %all-gather.3.cloned.1.call-done, bf16[2048,384]{1,0:T(8,128)(2,1)} %all-gather.5.cloned.1.call-done), kind=kOutput, calls=%fused_computation.10 | convolution fusion | flops 2424373248 | bytes 9043968 | tf_op jit(solution)/shard_map/dot_general | solution.py:26
  150.9 38.1 %reduce-scatter.2.cloned.1.call-done = bf16[256,384]{1,0:T(8,128)(2,1)} async-done(((bf16[2048,384]{1,0:T(8,128)(2,1)}), bf16[256,384]{1,0:T(8,128)(2,1)}) %reduce-scatter.2.cloned.1.call-update) | async-done | bytes 196624 | tf_op jit(solution)/shard_map/reduce_scatter | solution.py:32
  189.0 0.0 copy-done.1
  189.0 1.9 fusion.17
Async XLA Ops:
  7.2 92.9 %copy-start = (bf16[384,1536]{1,0:T(8,128)(2,1)S(1)}, bf16[384,1536]{1,0:T(8,128)(2,1)}, u32[]{:S(2)}) copy-start(bf16[384,1536]{1,0:T(8,128)(2,1)} %param.5) | copy-start | bytes 3538948
  7.2 92.9 %all-gather.3.cloned.1.call-start = ((), (), s32[]{:S(2)}) async-start(), calls=%async_computation.1 | async-start | bytes 6389760 | tf_op jit(solution)/shard_map/all_gather | solution.py:23
  7.9 136.0 %all-gather.5.cloned.1.call-start = ((), (), s32[]{:S(2)}) async-start(), calls=%async_computation.3 | async-start | bytes 1769472 | tf_op jit(solution)/shard_map/all_gather | solution.py:24
  8.7 180.3 %reduce-scatter.2.cloned.1.call-start = ((), (), s32[]{:S(2)}) async-start(), calls=%async_computation.2 | async-start | bytes 1769472 | tf_op jit(solution)/shard_map/reduce_scatter | solution.py:32
  107.6 81.4 %copy-start.1 = (bf16[256,384]{1,0:T(8,128)(2,1)S(1)}, bf16[256,384]{1,0:T(8,128)(2,1)}, u32[]{:S(2)}) copy-start(bf16[256,384]{1,0:T(8,128)(2,1)} %param.4) | copy-start | bytes 589828
Sparse Core Ops, SparseCore 0:
  11.3 88.7 all-gather.2
  102.2 41.6 all-gather.4
  146.7 42.2 reduce-scatter.1

commit v2 on v1

v2 whole, which is shorter than its diff:
```python
import jax
import jax.numpy as jnp
import numpy as np
from jax import lax
from jax.sharding import Mesh
from jax.sharding import PartitionSpec as P

coef = 0.7978845608
cubic = 0.044715


def gelu_fwd(x):
    return 0.5 * x * (1.0 + jnp.tanh(coef * (x + cubic * x * x * x)))


def gelu_grad(x):
    inner = coef * (x + cubic * x * x * x)
    tangent = jnp.tanh(inner)
    return 0.5 * (1.0 + tangent) + 0.5 * x * (1.0 - tangent * tangent) * coef * (
        1.0 + 3.0 * cubic * x * x
    )


def ring_gather(block, axis, n):
    fwd = block
    bwd = block
    got = {0: block}
    for k in range(1, n // 2 + 1):
        fwd = lax.ppermute(fwd, axis, [(i, (i + 1) % n) for i in range(n)])
        got[(n - k) % n] = fwd
        if k < n - k:
            bwd = lax.ppermute(bwd, axis, [(i, (i - 1) % n) for i in range(n)])
            got[k] = bwd
    return jnp.stack([got[k] for k in range(n)])


def make_body(n_col, n_core):
    def body(grad_out, pre_act, down_weight):
        rc = lax.axis_index("rc")
        c = lax.axis_index("col")
        tok_blk = grad_out.shape[0]
        g_own = lax.all_gather(grad_out, "rp", axis=0, tiled=True)
        rel = ring_gather(pre_act, "col", n_col)
        g_own, rel = lax.optimization_barrier((g_own, rel))
        g_other = lax.ppermute(g_own, "rc", [(i, (i + 1) % n_core) for i in range(n_core)])
        both = jnp.concatenate([rel, rel], axis=0)
        pre_abs = lax.dynamic_slice_in_dim(both, (n_col - c) % n_col, n_col, 0)
        hidden = gelu_fwd(pre_abs.astype(jnp.float32)).astype(jnp.bfloat16)
        sub = pre_act.shape[0] // (tok_blk * n_core)
        h5 = hidden.reshape(n_col, sub, n_core, tok_blk, hidden.shape[-1])
        h_own = lax.dynamic_index_in_dim(h5, rc, 2, keepdims=False).reshape(-1, hidden.shape[-1])
        h_other = lax.dynamic_index_in_dim(h5, (rc + 1) % n_core, 2, keepdims=False).reshape(
            -1, hidden.shape[-1]
        )
        dn = (((0,), (0,)), ((), ()))
        gw = lax.dot_general(h_own, g_own, dn, preferred_element_type=jnp.float32)
        gw = gw + lax.dot_general(h_other, g_other, dn, preferred_element_type=jnp.float32)
        grad_weight = gw.astype(jnp.bfloat16)
        dn2 = (((1,), (1,)), ((), ()))
        p_own = lax.dot_general(g_own, down_weight, dn2, preferred_element_type=jnp.float32)
        p_other = lax.dot_general(g_other, down_weight, dn2, preferred_element_type=jnp.float32)
        stacked = jnp.stack([p_own, p_other]).astype(jnp.bfloat16)
        red = lax.psum_scatter(stacked, "col", scatter_dimension=1, tiled=True)
        red = red.astype(jnp.float32).reshape(n_core, sub, tok_blk, -1)
        first = jnp.where(rc == 0, red[0], red[1])
        second = jnp.where(rc == 0, red[1], red[0])
        grad_hidden = jnp.stack([first, second], axis=1).reshape(pre_act.shape)
        grad_pre = (grad_hidden * gelu_grad(pre_act.astype(jnp.float32))).astype(jnp.bfloat16)
        return (grad_pre, grad_weight)

    return body


def solution(mesh):
    devs = mesh.devices
    n_row, n_col = devs.shape
    chips = {tuple(getattr(d, "coords", (i,))) for i, d in enumerate(devs.flat)}
    n_core = max(1, devs.size // len(chips))
    split = Mesh(np.asarray(devs).reshape(n_row // n_core, n_core, n_col), ("rp", "rc", "col"))
    row = ("rp", "rc")
    in_specs = (P(row, "col"), P("col", row), P(row, "col"))
    out_specs = (P("col", row), P(row, "col"))
    return jax.shard_map(
        make_body(n_col, n_core), mesh=split, in_specs=in_specs, out_specs=out_specs, check_vma=False
    )
```

time: 198 us -> 162 us (0.82)
  waiting for transfers between devices: 167 us -> 97.8 us
  starting transfers between devices: 0.11 us -> 31.7 us
  matrix products: 14.5 us -> 9.37 us
  local copies, waits for them, and re-layouts: 0.02 us -> 3.58 us
  other arithmetic: 1.89 us -> 4.81 us
    all_gather x2 -> x1, waiting for transfers between devices: 128 us -> 43.3 us  [body(): g_own = lax.all_gather(grad_out, 'rp', axis=0, tiled=True)]
    ppermute x0 -> x8, starting transfers between devices: none -> 31.6 us  [the longest x3 22 us: ring_gather(): bwd = lax.ppermute(bwd, axis, [(i, (i - 1) % n) for i in range(n)])]
    ppermute x0 -> x8, waiting for transfers between devices: none -> 18.6 us  [the longest x4 13.6 us: ring_gather(): fwd = lax.ppermute(fwd, axis, [(i, (i + 1) % n) for i in range(n)])]
    dot_general x2 -> x4, matrix products: 14.5 us -> 9.37 us  [the longest x1 3.69 us: body(): lax.dot_general(g_own, down_weight, dn2, preferred_element_type=jnp.float32)]
    unnamed x4 -> x17, local copies, waits for them, and re-layouts: 0.02 us -> 3.27 us
    reduce_scatter x1, waiting for transfers between devices: 38.1 us -> 35.2 us  [body(): red = lax.psum_scatter(stacked, 'col', scatter_dimension=1, tiled=True)]
    convert_element_type x0 -> x2, other arithmetic: none -> 2.47 us  [the longest x1 1.51 us: body(): hidden = gelu_fwd(pre_abs.astype(jnp.float32)).astype(jnp.bfloat16)]
  transfers between devices with their start and end apart: 3 -> 10, of which waited for: 3 -> 7; matrix products, arithmetic and copies ran while one was open for 7% -> 7% of each run, Pallas kernels for 0% -> 0%
where the time goes in v2:
time: 162 us
  waiting for transfers between devices  97.8 us (60%)
  starting transfers between devices  31.7 us (20%)
  between operations  14.3 us (9%)
  matrix products  9.37 us (6%)
  other arithmetic  4.81 us (3%)
  local copies, waits for them, and re-layouts  3.58 us (2%)
    all_gather x1, waiting for transfers between devices, body(): g_own = lax.all_gather(grad_out, 'rp', axis=0, tiled=True)  43.3 us
    reduce_scatter x1, waiting for transfers between devices, body(): red = lax.psum_scatter(stacked, 'col', scatter_dimension=1, tiled=True)  35.2 us
    ppermute x3, starting transfers between devices, ring_gather(): bwd = lax.ppermute(bwd, axis, [(i, (i - 1) % n) for i in range(n)])  22 us
    ppermute x4, waiting for transfers between devices, ring_gather(): fwd = lax.ppermute(fwd, axis, [(i, (i + 1) % n) for i in range(n)])  13.6 us
    ppermute x4, starting transfers between devices, ring_gather(): fwd = lax.ppermute(fwd, axis, [(i, (i + 1) % n) for i in range(n)])  7.67 us
    dot_general x1, matrix products, body(): lax.dot_general(g_own, down_weight, dn2, preferred_element_type=jnp.float32)  3.69 us
    unnamed x17, local copies, waits for them, and re-layouts  3.27 us
  transfers between devices with their start and end apart: 10, of which 7 were waited for; matrix products, arithmetic and copies ran while one was open for 7% of the time, Pallas kernels for 0%

profile of v2, /device:TPU:6, one launch (start us, length us, event | category | flops | bytes accessed | tf_op | source)
XLA Modules:
  0.0 161.6 jit_solution(332515710004886059)
XLA Ops:
  8.0 10.9 %collective-permute-start = (bf16[256,384]{1,0:T(8,128)(2,1)}, bf16[256,384]{1,0:T(8,128)(2,1)S(1)}, u32[]{:S(2)}, u32[]{:S(2)}) collective-permute-start(bf16[256,384]{1,0:T(8,128)(2,1)} %param.4), channel_id=1, source_target_pairs={{0,7},{1,0},{2,1},{3,2},{4,3},{5,4},{6,5},{7,6},{8,15},{9,8},{10,9... | collective-permute-start | bytes 589832 | tf_op jit(solution)/shard_map/ppermute | solution.py:32
  18.9 1.9 %collective-permute-start.3 = (bf16[256,384]{1,0:T(8,128)(2,1)}, bf16[256,384]{1,0:T(8,128)(2,1)S(1)}, u32[]{:S(2)}, u32[]{:S(2)}) collective-permute-start(bf16[256,384]{1,0:T(8,128)(2,1)} %param.4), channel_id=1, source_target_pairs={{0,1},{1,2},{2,3},{3,4},{4,5},{5,6},{6,7},{7,0},{8,9},{9,10},{10,1... | collective-permute-start | bytes 589832 | tf_op jit(solution)/shard_map/ppermute | solution.py:29
  20.8 1.0 bitcast_dynamic-update-slice_fusion.7
  21.8 1.6 collective-permute-done
  23.4 5.5 %collective-permute-start.1 = (bf16[256,384]{1,0:T(8,128)(2,1)S(1)}, bf16[256,384]{1,0:T(8,128)(2,1)S(1)}, u32[]{:S(2)}, u32[]{:S(2)}) collective-permute-start(bf16[256,384]{1,0:T(8,128)(2,1)S(1)} %collective-permute-done), channel_id=1, source_target_pairs={{0,7},{1,0},{2,1},{3,2},{4,3},{5,4},{6,5},{7,6},{8,15},{9,8},{10,9... | collective-permute-start | bytes 589832 | tf_op jit(solution)/shard_map/ppermute | solution.py:32
  28.9 1.9 %collective-permute-start.4 = (bf16[256,384]{1,0:T(8,128)(2,1)S(1)}, bf16[256,384]{1,0:T(8,128)(2,1)S(1)}, u32[]{:S(2)}, u32[]{:S(2)}) collective-permute-start(bf16[256,384]{1,0:T(8,128)(2,1)S(1)} %collective-permute-done.3), channel_id=1, source_target_pairs={{0,1},{1,2},{2,3},{3,4},{4,5},{5,6},{6,7},{7,0},{8,9},{9,10},{10,1... | collective-permute-start | bytes 589832 | tf_op jit(solution)/shard_map/ppermute | solution.py:29
  30.8 1.3 collective-permute-done.1
  32.1 5.6 %collective-permute-start.2 = (bf16[256,384]{1,0:T(8,128)(2,1)S(1)}, bf16[256,384]{1,0:T(8,128)(2,1)S(1)}, u32[]{:S(2)}, u32[]{:S(2)}) collective-permute-start(bf16[256,384]{1,0:T(8,128)(2,1)S(1)} %collective-permute-done.1), channel_id=1, source_target_pairs={{0,7},{1,0},{2,1},{3,2},{4,3},{5,4},{6,5},{7,6},{8,15},{9,8},{10,9... | collective-permute-start | bytes 589832 | tf_op jit(solution)/shard_map/ppermute | solution.py:32
  37.8 1.9 %collective-permute-start.5 = (bf16[256,384]{1,0:T(8,128)(2,1)S(1)}, bf16[256,384]{1,0:T(8,128)(2,1)S(1)}, u32[]{:S(2)}, u32[]{:S(2)}) collective-permute-start(bf16[256,384]{1,0:T(8,128)(2,1)S(1)} %collective-permute-done.4), channel_id=1, source_target_pairs={{0,1},{1,2},{2,3},{3,4},{4,5},{5,6},{6,7},{7,0},{8,9},{9,10},{10,1... | collective-permute-start | bytes 589832 | tf_op jit(solution)/shard_map/ppermute | solution.py:29
  39.7 6.8 %collective-permute-done.5 = bf16[256,384]{1,0:T(8,128)(2,1)S(1)} collective-permute-done((bf16[256,384]{1,0:T(8,128)(2,1)S(1)}, bf16[256,384]{1,0:T(8,128)(2,1)S(1)}, u32[]{:S(2)}, u32[]{:S(2)}) %collective-permute-start.5) | collective-permute-done | bytes 196640 | tf_op jit(solution)/shard_map/ppermute | solution.py:29
  46.5 1.9 %collective-permute-start.6 = (bf16[256,384]{1,0:T(8,128)(2,1)S(1)}, bf16[256,384]{1,0:T(8,128)(2,1)S(1)}, u32[]{:S(2)}, u32[]{:S(2)}) collective-permute-start(bf16[256,384]{1,0:T(8,128)(2,1)S(1)} %collective-permute-done.5), channel_id=1, source_target_pairs={{0,1},{1,2},{2,3},{3,4},{4,5},{5,6},{6,7},{7,0},{8,9},{9,10},{10,1... | collective-permute-start | bytes 589832 | tf_op jit(solution)/shard_map/ppermute | solution.py:29
  48.5 6.8 %collective-permute-done.6 = bf16[256,384]{1,0:T(8,128)(2,1)S(1)} collective-permute-done((bf16[256,384]{1,0:T(8,128)(2,1)S(1)}, bf16[256,384]{1,0:T(8,128)(2,1)S(1)}, u32[]{:S(2)}, u32[]{:S(2)}) %collective-permute-start.6) | collective-permute-done | bytes 196640 | tf_op jit(solution)/shard_map/ppermute | solution.py:29
  55.4 43.3 %all-gather.2.cloned.1.call-done = bf16[1024,1536]{1,0:T(8,128)(2,1)} async-done(((bf16[32,1536]{1,0:T(8,128)(2,1)}), bf16[1024,1536]{1,0:T(8,128)(2,1)}) %all-gather.2.cloned.1.call-update) | async-done | bytes 3145744 | tf_op jit(solution)/shard_map/all_gather | solution.py:42
  98.8 1.9 %collective-permute-start.7 = (bf16[1024,1536]{1,0:T(8,128)(2,1)}, bf16[1024,1536]{1,0:T(8,128)(2,1)S(1)}, u32[]{:S(2)}, u32[]{:S(2)}) collective-permute-start(bf16[1024,1536]{1,0:T(8,128)(2,1)} %all-gather.2.cloned.1.call-done), channel_id=1, source_target_pairs={{0,8},{8,0},{1,9},{9,1},{2,10},{10,2},{3,11},{11,3},{4,12},{12,4},... | collective-permute-start | bytes 9437192 | tf_op jit(solution)/shard_map/ppermute | solution.py:45
  100.7 3.7 %fusion.7 = bf16[1,1024,384]{2,1,0:T(8,128)(2,1)S(1)} fusion(bf16[1024,1536]{1,0:T(8,128)(2,1)} %all-gather.2.cloned.1.call-done, bf16[384,1536]{1,0:T(8,128)(2,1)S(1)} %copy-done), kind=kOutput, calls=%fused_computation.18 | convolution fusion | flops 1208352768 | bytes 5111808 | tf_op jit(solution)/shard_map/dot_general | solution.py:60
  104.4 2.1 %collective-permute-done.7 = bf16[1024,1536]{1,0:T(8,128)(2,1)S(1)} collective-permute-done((bf16[1024,1536]{1,0:T(8,128)(2,1)}, bf16[1024,1536]{1,0:T(8,128)(2,1)S(1)}, u32[]{:S(2)}, u32[]{:S(2)}) %collective-permute-start.7) | collective-permute-done | bytes 3145760 | tf_op jit(solution)/shard_map/ppermute | solution.py:45
  106.5 1.8 %fusion.8 = bf16[1,1024,384]{2,1,0:T(8,128)(2,1)S(1)} fusion(bf16[1024,1536]{1,0:T(8,128)(2,1)S(1)} %collective-permute-done.7, bf16[384,1536]{1,0:T(8,128)(2,1)S(1)} %copy-done), kind=kOutput, calls=%fused_computation.19 | convolution fusion | flops 1208352768 | bytes 5111808 | tf_op jit(solution)/shard_map/dot_general | solution.py:61
  108.4 1.3 pad_maximum_fusion
  109.7 1.5 fusion.1
  111.5 1.6 %copy-done.4 = bf16[1024,1536]{1,0:T(8,128)(2,1)S(1)} copy-done((bf16[1024,1536]{1,0:T(8,128)(2,1)S(1)}, bf16[1024,1536]{1,0:T(8,128)(2,1)}, u32[]{:S(2)}) %copy-start.4) | copy-done | bytes 3145752
  113.2 1.4 fusion.18
  115.0 2.5 %fusion.5 = bf16[384,1536]{1,0:T(8,128)(2,1)} fusion(f32[384,1536]{1,0:T(8,128)S(1)} %fusion.18, bf16[1024,384]{1,0:T(8,128)(2,1)S(1)} %bitcast.36, bf16[1024,1536]{1,0:T(8,128)(2,1)S(1)} %copy-done.2), kind=kOutput, calls=%fused_computation.13 | convolution fusion | flops 1209139200 | bytes 7471104 | tf_op jit(solution)/shard_map/dot_general | solution.py:57
  117.5 35.2 %reduce-scatter.2.cloned.1.call-done = bf16[2,128,384]{2,1,0:T(8,128)(2,1)} async-done(((bf16[2,1024,384]{2,1,0:T(8,128)(2,1)}), bf16[2,128,384]{2,1,0:T(8,128)(2,1)}) %reduce-scatter.2.cloned.1.call-update) | async-done | bytes 196624 | tf_op jit(solution)/shard_map/reduce_scatter | solution.py:63
  152.7 1.0 convert_element_type.19
  (28 shorter events, 2.8 us)
Async XLA Ops:
  7.2 93.5 %copy-start = (bf16[384,1536]{1,0:T(8,128)(2,1)S(1)}, bf16[384,1536]{1,0:T(8,128)(2,1)}, u32[]{:S(2)}) copy-start(bf16[384,1536]{1,0:T(8,128)(2,1)} %param.5) | copy-start | bytes 3538948
  7.2 91.6 %all-gather.2.cloned.1.call-start = ((), (), s32[]{:S(2)}) async-start(), calls=%async_computation.1 | async-start | bytes 3244032 | tf_op jit(solution)/shard_map/all_gather | solution.py:42
  7.9 144.8 %reduce-scatter.2.cloned.1.call-start = ((), (), s32[]{:S(2)}) async-start(), calls=%async_computation.2 | async-start | bytes 1769472 | tf_op jit(solution)/shard_map/reduce_scatter | solution.py:63
  8.0 15.4 %collective-permute-start = (bf16[256,384]{1,0:T(8,128)(2,1)}, bf16[256,384]{1,0:T(8,128)(2,1)S(1)}, u32[]{:S(2)}, u32[]{:S(2)}) collective-permute-start(bf16[256,384]{1,0:T(8,128)(2,1)} %param.4), channel_id=1, source_target_pairs={{0,7},{1,0},{2,1},{3,2},{4,3},{5,4},{6,5},{7,6},{8,15},{9,8},{10,9... | collective-permute-start | bytes 589832 | tf_op jit(solution)/shard_map/ppermute | solution.py:32
  18.9 9.9 %collective-permute-start.3 = (bf16[256,384]{1,0:T(8,128)(2,1)}, bf16[256,384]{1,0:T(8,128)(2,1)S(1)}, u32[]{:S(2)}, u32[]{:S(2)}) collective-permute-start(bf16[256,384]{1,0:T(8,128)(2,1)} %param.4), channel_id=1, source_target_pairs={{0,1},{1,2},{2,3},{3,4},{4,5},{5,6},{6,7},{7,0},{8,9},{9,10},{10,1... | collective-permute-start | bytes 589832 | tf_op jit(solution)/shard_map/ppermute | solution.py:29
  23.4 8.8 %collective-permute-start.1 = (bf16[256,384]{1,0:T(8,128)(2,1)S(1)}, bf16[256,384]{1,0:T(8,128)(2,1)S(1)}, u32[]{:S(2)}, u32[]{:S(2)}) collective-permute-start(bf16[256,384]{1,0:T(8,128)(2,1)S(1)} %collective-permute-done), channel_id=1, source_target_pairs={{0,7},{1,0},{2,1},{3,2},{4,3},{5,4},{6,5},{7,6},{8,15},{9,8},{10,9... | collective-permute-start | bytes 589832 | tf_op jit(solution)/shard_map/ppermute | solution.py:32
  28.9 8.9 %collective-permute-start.4 = (bf16[256,384]{1,0:T(8,128)(2,1)S(1)}, bf16[256,384]{1,0:T(8,128)(2,1)S(1)}, u32[]{:S(2)}, u32[]{:S(2)}) collective-permute-start(bf16[256,384]{1,0:T(8,128)(2,1)S(1)} %collective-permute-done.3), channel_id=1, source_target_pairs={{0,1},{1,2},{2,3},{3,4},{4,5},{5,6},{6,7},{7,0},{8,9},{9,10},{10,1... | collective-permute-start | bytes 589832 | tf_op jit(solution)/shard_map/ppermute | solution.py:29
  32.1 16.3 %collective-permute-start.2 = (bf16[256,384]{1,0:T(8,128)(2,1)S(1)}, bf16[256,384]{1,0:T(8,128)(2,1)S(1)}, u32[]{:S(2)}, u32[]{:S(2)}) collective-permute-start(bf16[256,384]{1,0:T(8,128)(2,1)S(1)} %collective-permute-done.1), channel_id=1, source_target_pairs={{0,7},{1,0},{2,1},{3,2},{4,3},{5,4},{6,5},{7,6},{8,15},{9,8},{10,9... | collective-permute-start | bytes 589832 | tf_op jit(solution)/shard_map/ppermute | solution.py:32
  37.8 8.8 %collective-permute-start.5 = (bf16[256,384]{1,0:T(8,128)(2,1)S(1)}, bf16[256,384]{1,0:T(8,128)(2,1)S(1)}, u32[]{:S(2)}, u32[]{:S(2)}) collective-permute-start(bf16[256,384]{1,0:T(8,128)(2,1)S(1)} %collective-permute-done.4), channel_id=1, source_target_pairs={{0,1},{1,2},{2,3},{3,4},{4,5},{5,6},{6,7},{7,0},{8,9},{9,10},{10,1... | collective-permute-start | bytes 589832 | tf_op jit(solution)/shard_map/ppermute | solution.py:29
  46.5 8.8 %collective-permute-start.6 = (bf16[256,384]{1,0:T(8,128)(2,1)S(1)}, bf16[256,384]{1,0:T(8,128)(2,1)S(1)}, u32[]{:S(2)}, u32[]{:S(2)}) collective-permute-start(bf16[256,384]{1,0:T(8,128)(2,1)S(1)} %collective-permute-done.5), channel_id=1, source_target_pairs={{0,1},{1,2},{2,3},{3,4},{4,5},{5,6},{6,7},{7,0},{8,9},{9,10},{10,1... | collective-permute-start | bytes 589832 | tf_op jit(solution)/shard_map/ppermute | solution.py:29
  98.8 7.8 %collective-permute-start.7 = (bf16[1024,1536]{1,0:T(8,128)(2,1)}, bf16[1024,1536]{1,0:T(8,128)(2,1)S(1)}, u32[]{:S(2)}, u32[]{:S(2)}) collective-permute-start(bf16[1024,1536]{1,0:T(8,128)(2,1)} %all-gather.2.cloned.1.call-done), channel_id=1, source_target_pairs={{0,8},{8,0},{1,9},{9,1},{2,10},{10,2},{3,11},{11,3},{4,12},{12,4},... | collective-permute-start | bytes 9437192 | tf_op jit(solution)/shard_map/ppermute | solution.py:45
  106.5 1.8 %copy-start.1 = (bf16[1024,1536]{1,0:T(8,128)(2,1)}, bf16[1024,1536]{1,0:T(8,128)(2,1)S(1)}, u32[]{:S(2)}) copy-start(bf16[1024,1536]{1,0:T(8,128)(2,1)S(1)} %collective-permute-done.7) | copy-start | bytes 9437188
  111.3 1.9 %copy-start.4 = (bf16[1024,1536]{1,0:T(8,128)(2,1)S(1)}, bf16[1024,1536]{1,0:T(8,128)(2,1)}, u32[]{:S(2)}) copy-start(bf16[1024,1536]{1,0:T(8,128)(2,1)} %all-gather.2.cloned.1.call-done) | copy-start | bytes 9437188
  113.2 1.9 %copy-start.2 = (bf16[1024,1536]{1,0:T(8,128)(2,1)S(1)}, bf16[1024,1536]{1,0:T(8,128)(2,1)}, u32[]{:S(2)}) copy-start(bf16[1024,1536]{1,0:T(8,128)(2,1)} %copy-done.1) | copy-start | bytes 9437188
  117.5 36.3 %copy-start.3 = (bf16[256,384]{1,0:T(8,128)(2,1)S(1)}, bf16[256,384]{1,0:T(8,128)(2,1)}, u32[]{:S(2)}) copy-start(bf16[256,384]{1,0:T(8,128)(2,1)} %param.4) | copy-start | bytes 589828
Sparse Core Ops, SparseCore 0:
  11.1 87.5 all-gather.1
  109.8 42.8 reduce-scatter.1

commit v3 on v2

v3 whole, which is shorter than its diff:
```python
import jax
import jax.numpy as jnp
import numpy as np
from jax import lax
from jax.sharding import Mesh
from jax.sharding import PartitionSpec as P

coef = 0.7978845608
cubic = 0.044715


def gelu_fwd(x):
    return 0.5 * x * (1.0 + jnp.tanh(coef * (x + cubic * x * x * x)))


def gelu_grad(x):
    inner = coef * (x + cubic * x * x * x)
    tangent = jnp.tanh(inner)
    return 0.5 * (1.0 + tangent) + 0.5 * x * (1.0 - tangent * tangent) * coef * (
        1.0 + 3.0 * cubic * x * x
    )


def ring_gather(block, axis, n):
    fwd = block
    bwd = block
    got = {0: block}
    for k in range(1, n // 2 + 1):
        fwd = lax.ppermute(fwd, axis, [(i, (i + 1) % n) for i in range(n)])
        got[(n - k) % n] = fwd
        if k < n - k:
            bwd = lax.ppermute(bwd, axis, [(i, (i - 1) % n) for i in range(n)])
            got[k] = bwd
    return jnp.stack([got[k] for k in range(n)])


def shift_pairs(n, s):
    return [(i, (i + s) % n) for i in range(n)]


def make_body(n_x, n_col, n_core):
    def body(grad_out, pre_act, down_weight):
        rc = lax.axis_index("rc")
        c = lax.axis_index("col")
        ix = lax.axis_index("rx")
        tok_blk, width = grad_out.shape
        rel_x = [grad_out] + [
            lax.ppermute(grad_out, "rx", shift_pairs(n_x, n_x - k)) for k in range(1, n_x)
        ]
        stack_x = jnp.stack(rel_x)
        twice_x = jnp.concatenate([stack_x, stack_x], axis=0)
        abs_x = lax.dynamic_slice_in_dim(twice_x, (n_x - ix) % n_x, n_x, 0)
        g_own = lax.all_gather(abs_x, "ry", axis=0, tiled=False)
        rel = ring_gather(pre_act, "col", n_col)
        g_own, rel = lax.optimization_barrier((g_own, rel))
        g_other = lax.ppermute(g_own, "rc", shift_pairs(n_core, 1))
        n_y = g_own.shape[0]
        both = jnp.concatenate([rel, rel], axis=0)
        pre_abs = lax.dynamic_slice_in_dim(both, (n_col - c) % n_col, n_col, 0)
        hidden = gelu_fwd(pre_abs.astype(jnp.float32)).astype(jnp.bfloat16)
        hid = hidden.shape[-1]
        h5 = hidden.reshape(n_x, n_y, n_core, tok_blk, hid)
        h5 = jnp.transpose(h5, (2, 1, 0, 3, 4))
        h_own = lax.dynamic_index_in_dim(h5, rc, 0, keepdims=False).reshape(-1, hid)
        h_other = lax.dynamic_index_in_dim(h5, (rc + 1) % n_core, 0, keepdims=False).reshape(-1, hid)
        go = g_own.reshape(-1, width)
        gt = g_other.reshape(-1, width)
        dn = (((0,), (0,)), ((), ()))
        gw = lax.dot_general(h_own, go, dn, preferred_element_type=jnp.float32)
        gw = gw + lax.dot_general(h_other, gt, dn, preferred_element_type=jnp.float32)
        grad_weight = gw.astype(jnp.bfloat16)
        dn2 = (((1,), (1,)), ((), ()))
        p_own = lax.dot_general(go, down_weight, dn2, preferred_element_type=jnp.float32)
        p_other = lax.dot_general(gt, down_weight, dn2, preferred_element_type=jnp.float32)
        stacked = jnp.stack([p_own, p_other]).astype(jnp.bfloat16)
        stacked = jnp.transpose(stacked.reshape(n_core, n_y, n_x, tok_blk, hid), (0, 2, 1, 3, 4))
        stacked = stacked.reshape(n_core, n_x * n_y * tok_blk, hid)
        red = lax.psum_scatter(stacked, "col", scatter_dimension=1, tiled=True)
        sub = pre_act.shape[0] // (tok_blk * n_core)
        red = red.astype(jnp.float32).reshape(n_core, sub, tok_blk, hid)
        first = jnp.where(rc == 0, red[0], red[1])
        second = jnp.where(rc == 0, red[1], red[0])
        grad_hidden = jnp.stack([first, second], axis=1).reshape(pre_act.shape)
        grad_pre = (grad_hidden * gelu_grad(pre_act.astype(jnp.float32))).astype(jnp.bfloat16)
        return (grad_pre, grad_weight)

    return body


def solution(mesh):
    devs = np.asarray(mesh.devices)
    n_row, n_col = devs.shape
    flat = list(devs.flat)
    chips = {tuple(getattr(d, "coords", (i,))) for i, d in enumerate(flat)}
    n_core = max(1, devs.size // len(chips))
    xs = {tuple(getattr(d, "coords", (i,)))[0] for i, d in enumerate(flat)}
    n_x = len(xs)
    split = Mesh(devs.reshape(n_x, n_row // (n_x * n_core), n_core, n_col), ("rx", "ry", "rc", "col"))
    row = ("rx", "ry", "rc")
    in_specs = (P(row, "col"), P("col", row), P(row, "col"))
    out_specs = (P("col", row), P(row, "col"))
    return jax.shard_map(
        make_body(n_x, n_col, n_core), mesh=split, in_specs=in_specs, out_specs=out_specs, check_vma=False
    )
```

time: 162 us -> 140 us (0.86)
  waiting for transfers between devices: 97.8 us -> 63 us
  starting transfers between devices: 31.7 us -> 42.3 us
  local copies, waits for them, and re-layouts: 3.58 us -> 6.85 us
    all_gather x1, waiting for transfers between devices: 43.3 us -> 5.74 us  [body(): g_own = lax.all_gather(abs_x, 'ry', axis=0, tiled=False)]
    ppermute x1 -> x4, starting transfers between devices: 1.91 us -> 15.1 us  [the longest x3 13.2 us: body(): lax.ppermute(grad_out, 'rx', shift_pairs(n_x, n_x - k))]
    ppermute x1 -> x4, waiting for transfers between devices: 2.13 us -> 6.05 us  [the longest x3 3.92 us: body(): lax.ppermute(grad_out, 'rx', shift_pairs(n_x, n_x - k))]
    ppermute x3, starting transfers between devices: 22 us -> 19.5 us  [ring_gather(): bwd = lax.ppermute(bwd, axis, [(i, (i - 1) % n) for i in range(n)])]
    unnamed x17 -> x24, local copies, waits for them, and re-layouts: 3.27 us -> 4.22 us
  transfers between devices with their start and end apart: 10 -> 13, of which waited for: 7 -> 8; matrix products, arithmetic and copies ran while one was open for 7% -> 8% of each run, Pallas kernels for 0% -> 0%
where the time goes in v3:
time: 140 us
  waiting for transfers between devices  63 us (45%)
  starting transfers between devices  42.3 us (30%)
  between operations  14.4 us (10%)
  matrix products  9.37 us (7%)
  local copies, waits for them, and re-layouts  6.85 us (5%)
  other arithmetic  3.65 us (3%)
    reduce_scatter x1, waiting for transfers between devices, body(): red = lax.psum_scatter(stacked, 'col', scatter_dimension=1, tiled=True)  35.2 us
    ppermute x3, starting transfers between devices, ring_gather(): bwd = lax.ppermute(bwd, axis, [(i, (i - 1) % n) for i in range(n)])  19.5 us
    ppermute x4, waiting for transfers between devices, ring_gather(): fwd = lax.ppermute(fwd, axis, [(i, (i + 1) % n) for i in range(n)])  13.6 us
    ppermute x3, starting transfers between devices, body(): lax.ppermute(grad_out, 'rx', shift_pairs(n_x, n_x - k))  13.2 us
    ppermute x4, starting transfers between devices, ring_gather(): fwd = lax.ppermute(fwd, axis, [(i, (i + 1) % n) for i in range(n)])  7.66 us
    all_gather x1, waiting for transfers between devices, body(): g_own = lax.all_gather(abs_x, 'ry', axis=0, tiled=False)  5.74 us
    unnamed x24, local copies, waits for them, and re-layouts  4.22 us
    ppermute x3, waiting for transfers between devices, body(): lax.ppermute(grad_out, 'rx', shift_pairs(n_x, n_x - k))  3.92 us
  transfers between devices with their start and end apart: 13, of which 8 were waited for; matrix products, arithmetic and copies ran while one was open for 8% of the time, Pallas kernels for 0%

profile of v3, /device:TPU:6, one launch (start us, length us, event | category | flops | bytes accessed | tf_op | source)
XLA Modules:
  0.0 139.6 jit_solution(10396267338108206240)
XLA Ops:
  7.2 2.9 %collective-permute-start = (bf16[32,1536]{1,0:T(8,128)(2,1)}, bf16[32,1536]{1,0:T(8,128)(2,1)S(1)}, u32[]{:S(2)}, u32[]{:S(2)}) collective-permute-start(bf16[32,1536]{1,0:T(8,128)(2,1)} %param.3), channel_id=1, source_target_pairs={{0,384},{128,0},{256,128},{384,256},{1,385},{129,1},{257,129},{385... | collective-permute-start | bytes 294920 | tf_op jit(solution)/shard_map/ppermute | solution.py:48
  10.1 6.9 %collective-permute-start.2 = (bf16[32,1536]{1,0:T(8,128)(2,1)}, bf16[32,1536]{1,0:T(8,128)(2,1)S(1)}, u32[]{:S(2)}, u32[]{:S(2)}) collective-permute-start(bf16[32,1536]{1,0:T(8,128)(2,1)} %param.3), channel_id=1, source_target_pairs={{0,128},{128,256},{256,384},{384,0},{1,129},{129,257},{257,385},{3... | collective-permute-start | bytes 294920 | tf_op jit(solution)/shard_map/ppermute | solution.py:48
  17.0 3.4 %collective-permute-start.1 = (bf16[32,1536]{1,0:T(8,128)(2,1)}, bf16[32,1536]{1,0:T(8,128)(2,1)S(1)}, u32[]{:S(2)}, u32[]{:S(2)}) collective-permute-start(bf16[32,1536]{1,0:T(8,128)(2,1)} %param.3), channel_id=1, source_target_pairs={{0,256},{128,384},{256,0},{384,128},{1,257},{129,385},{257,1},{385... | collective-permute-start | bytes 294920 | tf_op jit(solution)/shard_map/ppermute | solution.py:48
  21.4 3.9 %collective-permute-done.1 = bf16[32,1536]{1,0:T(8,128)(2,1)S(1)} collective-permute-done((bf16[32,1536]{1,0:T(8,128)(2,1)}, bf16[32,1536]{1,0:T(8,128)(2,1)S(1)}, u32[]{:S(2)}, u32[]{:S(2)}) %collective-permute-start.1) | collective-permute-done | bytes 98336 | tf_op jit(solution)/shard_map/ppermute | solution.py:48
  27.1 8.3 %collective-permute-start.3 = (bf16[256,384]{1,0:T(8,128)(2,1)S(1)}, bf16[256,384]{1,0:T(8,128)(2,1)S(1)}, u32[]{:S(2)}, u32[]{:S(2)}) collective-permute-start(bf16[256,384]{1,0:T(8,128)(2,1)S(1)} %copy-done.3), channel_id=1, source_target_pairs={{0,7},{1,0},{2,1},{3,2},{4,3},{5,4},{6,5},{7,6},{8,15},{9,8},{10,9... | collective-permute-start | bytes 589832 | tf_op jit(solution)/shard_map/ppermute | solution.py:32
  35.5 1.9 %collective-permute-start.6 = (bf16[256,384]{1,0:T(8,128)(2,1)S(1)}, bf16[256,384]{1,0:T(8,128)(2,1)S(1)}, u32[]{:S(2)}, u32[]{:S(2)}) collective-permute-start(bf16[256,384]{1,0:T(8,128)(2,1)S(1)} %copy-done.3), channel_id=1, source_target_pairs={{0,1},{1,2},{2,3},{3,4},{4,5},{5,6},{6,7},{7,0},{8,9},{9,10},{10,1... | collective-permute-start | bytes 589832 | tf_op jit(solution)/shard_map/ppermute | solution.py:29
  38.6 5.6 %collective-permute-start.4 = (bf16[256,384]{1,0:T(8,128)(2,1)S(1)}, bf16[256,384]{1,0:T(8,128)(2,1)S(1)}, u32[]{:S(2)}, u32[]{:S(2)}) collective-permute-start(bf16[256,384]{1,0:T(8,128)(2,1)S(1)} %collective-permute-done.3), channel_id=1, source_target_pairs={{0,7},{1,0},{2,1},{3,2},{4,3},{5,4},{6,5},{7,6},{8,15},{9,8},{10,9... | collective-permute-start | bytes 589832 | tf_op jit(solution)/shard_map/ppermute | solution.py:32
  44.2 1.9 %collective-permute-start.7 = (bf16[256,384]{1,0:T(8,128)(2,1)S(1)}, bf16[256,384]{1,0:T(8,128)(2,1)S(1)}, u32[]{:S(2)}, u32[]{:S(2)}) collective-permute-start(bf16[256,384]{1,0:T(8,128)(2,1)S(1)} %collective-permute-done.6), channel_id=1, source_target_pairs={{0,1},{1,2},{2,3},{3,4},{4,5},{5,6},{6,7},{7,0},{8,9},{9,10},{10,1... | collective-permute-start | bytes 589832 | tf_op jit(solution)/shard_map/ppermute | solution.py:29
  47.4 5.6 %collective-permute-start.5 = (bf16[256,384]{1,0:T(8,128)(2,1)S(1)}, bf16[256,384]{1,0:T(8,128)(2,1)S(1)}, u32[]{:S(2)}, u32[]{:S(2)}) collective-permute-start(bf16[256,384]{1,0:T(8,128)(2,1)S(1)} %collective-permute-done.4), channel_id=1, source_target_pairs={{0,7},{1,0},{2,1},{3,2},{4,3},{5,4},{6,5},{7,6},{8,15},{9,8},{10,9... | collective-permute-start | bytes 589832 | tf_op jit(solution)/shard_map/ppermute | solution.py:32
  53.0 1.9 %collective-permute-start.8 = (bf16[256,384]{1,0:T(8,128)(2,1)S(1)}, bf16[256,384]{1,0:T(8,128)(2,1)S(1)}, u32[]{:S(2)}, u32[]{:S(2)}) collective-permute-start(bf16[256,384]{1,0:T(8,128)(2,1)S(1)} %collective-permute-done.7), channel_id=1, source_target_pairs={{0,1},{1,2},{2,3},{3,4},{4,5},{5,6},{6,7},{7,0},{8,9},{9,10},{10,1... | collective-permute-start | bytes 589832 | tf_op jit(solution)/shard_map/ppermute | solution.py:29
  55.0 6.8 %collective-permute-done.8 = bf16[256,384]{1,0:T(8,128)(2,1)S(1)} collective-permute-done((bf16[256,384]{1,0:T(8,128)(2,1)S(1)}, bf16[256,384]{1,0:T(8,128)(2,1)S(1)}, u32[]{:S(2)}, u32[]{:S(2)}) %collective-permute-start.8) | collective-permute-done | bytes 196640 | tf_op jit(solution)/shard_map/ppermute | solution.py:29
  61.8 1.9 %collective-permute-start.9 = (bf16[256,384]{1,0:T(8,128)(2,1)S(1)}, bf16[256,384]{1,0:T(8,128)(2,1)S(1)}, u32[]{:S(2)}, u32[]{:S(2)}) collective-permute-start(bf16[256,384]{1,0:T(8,128)(2,1)S(1)} %collective-permute-done.8), channel_id=1, source_target_pairs={{0,1},{1,2},{2,3},{3,4},{4,5},{5,6},{6,7},{7,0},{8,9},{9,10},{10,1... | collective-permute-start | bytes 589832 | tf_op jit(solution)/shard_map/ppermute | solution.py:29
  63.8 6.8 %collective-permute-done.9 = bf16[256,384]{1,0:T(8,128)(2,1)S(1)} collective-permute-done((bf16[256,384]{1,0:T(8,128)(2,1)S(1)}, bf16[256,384]{1,0:T(8,128)(2,1)S(1)}, u32[]{:S(2)}, u32[]{:S(2)}) %collective-permute-start.9) | collective-permute-done | bytes 196640 | tf_op jit(solution)/shard_map/ppermute | solution.py:29
  70.7 5.7 %all-gather.3.cloned.1.call-done = bf16[32,32,1536]{2,1,0:T(8,128)(2,1)} async-done(((bf16[4,32,1536]{2,1,0:T(8,128)(2,1)}), bf16[32,32,1536]{2,1,0:T(8,128)(2,1)}) %all-gather.3.cloned.1.call-update) | async-done | bytes 3145744 | tf_op jit(solution)/shard_map/all_gather | solution.py:53
  76.4 1.9 %collective-permute-start.10 = (bf16[8,4,32,1536]{3,2,1,0:T(8,128)(2,1)}, bf16[8,4,32,1536]{3,2,1,0:T(8,128)(2,1)S(1)}, u32[]{:S(2)}, u32[]{:S(2)}) collective-permute-start(bf16[8,4,32,1536]{3,2,1,0:T(8,128)(2,1)} %bitcast.69), channel_id=1, source_target_pairs={{0,8},{8,0},{1,9},{9,1},{2,10},{10,2},{3,11},{11,3},{4,12},{12,4},... | collective-permute-start | bytes 9437192 | tf_op jit(solution)/shard_map/ppermute | solution.py:56
  78.4 3.7 %fusion.7 = bf16[1,8,4,32,384]{4,3,2,1,0:T(8,128)(2,1)S(1)} fusion(bf16[8,4,32,1536]{3,2,1,0:T(8,128)(2,1)} %bitcast.70, bf16[384,1536]{1,0:T(8,128)(2,1)S(1)} %copy-done), kind=kOutput, calls=%fused_computation.18 | convolution fusion | flops 1208352768 | bytes 5111808 | tf_op jit(solution)/shard_map/dot_general | solution.py:73
  82.1 2.1 %collective-permute-done.10 = bf16[8,4,32,1536]{3,2,1,0:T(8,128)(2,1)S(1)} collective-permute-done((bf16[8,4,32,1536]{3,2,1,0:T(8,128)(2,1)}, bf16[8,4,32,1536]{3,2,1,0:T(8,128)(2,1)S(1)}, u32[]{:S(2)}, u32[]{:S(2)}) %collective-permute-start.10) | collective-permute-done | bytes 3145760 | tf_op jit(solution)/shard_map/ppermute | solution.py:56
  84.2 1.8 %fusion.8 = bf16[1,8,4,32,384]{4,3,2,1,0:T(8,128)(2,1)S(1)} fusion(bf16[8,4,32,1536]{3,2,1,0:T(8,128)(2,1)S(1)} %collective-permute-done.10, bf16[384,1536]{1,0:T(8,128)(2,1)S(1)} %copy-done), kind=kOutput, calls=%fused_computation.19 | convolution fusion | flops 1208352768 | bytes 5111808 | tf_op jit(solution)/shard_map/dot_general | solution.py:74
  86.2 1.3 copy.11
  87.6 1.5 %fusion.1 = bf16[8,256,384]{2,1,0:T(8,128)(2,1)S(1)} fusion(s32[]{:T(128)S(6)} %select_n.68, bf16[8,256,384]{2,1,0:T(8,128)(2,1)S(1)} %bitcast_dynamic-update-slice_fusion), kind=kLoop, calls=%fused_computation.6 | loop fusion | flops 8650752 | bytes 3145732 | tf_op jit(solution)/shard_map/convert_element_type | solution.py:60
  89.6 1.7 %copy-done.4 = bf16[32,32,1536]{2,1,0:T(8,128)(2,1)S(1)} copy-done((bf16[32,32,1536]{2,1,0:T(8,128)(2,1)S(1)}, bf16[32,32,1536]{2,1,0:T(8,128)(2,1)}, u32[]{:S(2)}) %copy-start.4) | copy-done | bytes 3145752
  91.3 1.4 %fusion.20 = f32[384,1536]{1,0:T(8,128)S(1)} fusion(bf16[1024,384]{1,0:T(8,128)(2,1)S(1)} %bitcast.66, bf16[1024,1536]{1,0:T(8,128)(2,1)S(1)} %bitcast.71), kind=kOutput, calls=%fused_computation.60 | convolution fusion | flops 1207959552 | bytes 6291456 | tf_op jit(solution)/shard_map/dot_general | solution.py:69
  93.1 2.5 %fusion.5 = bf16[384,1536]{1,0:T(8,128)(2,1)} fusion(f32[384,1536]{1,0:T(8,128)S(1)} %fusion.20, bf16[1024,384]{1,0:T(8,128)(2,1)S(1)} %bitcast.65, bf16[1024,1536]{1,0:T(8,128)(2,1)S(1)} %bitcast.64), kind=kOutput, calls=%fused_computation.13 | convolution fusion | flops 1209139200 | bytes 7471104 | tf_op jit(solution)/shard_map/dot_general | solution.py:70
  95.6 35.2 %reduce-scatter.2.cloned.1.call-done = bf16[2,128,384]{2,1,0:T(8,128)(2,1)} async-done(((bf16[2,1024,384]{2,1,0:T(8,128)(2,1)}), bf16[2,128,384]{2,1,0:T(8,128)(2,1)}) %reduce-scatter.2.cloned.1.call-update) | async-done | bytes 196624 | tf_op jit(solution)/shard_map/reduce_scatter | solution.py:78
  (46 shorter events, 8.5 us)
Async XLA Ops:
  7.2 71.2 %copy-start = (bf16[384,1536]{1,0:T(8,128)(2,1)S(1)}, bf16[384,1536]{1,0:T(8,128)(2,1)}, u32[]{:S(2)}) copy-start(bf16[384,1536]{1,0:T(8,128)(2,1)} %param.5) | copy-start | bytes 3538948
  7.2 19.9 %copy-start.3 = (bf16[256,384]{1,0:T(8,128)(2,1)S(1)}, bf16[256,384]{1,0:T(8,128)(2,1)}, u32[]{:S(2)}) copy-start(bf16[256,384]{1,0:T(8,128)(2,1)} %param.4) | copy-start | bytes 589828
  7.2 69.3 %all-gather.3.cloned.1.call-start = ((), (), s32[]{:S(2)}) async-start(), calls=%async_computation.2 | async-start | bytes 3538944 | tf_op jit(solution)/shard_map/all_gather | solution.py:53
  7.2 14.1 %collective-permute-start = (bf16[32,1536]{1,0:T(8,128)(2,1)}, bf16[32,1536]{1,0:T(8,128)(2,1)S(1)}, u32[]{:S(2)}, u32[]{:S(2)}) collective-permute-start(bf16[32,1536]{1,0:T(8,128)(2,1)} %param.3), channel_id=1, source_target_pairs={{0,384},{128,0},{256,128},{384,256},{1,385},{129,1},{257,129},{385... | collective-permute-start | bytes 294920 | tf_op jit(solution)/shard_map/ppermute | solution.py:48
  10.1 15.2 %collective-permute-start.2 = (bf16[32,1536]{1,0:T(8,128)(2,1)}, bf16[32,1536]{1,0:T(8,128)(2,1)S(1)}, u32[]{:S(2)}, u32[]{:S(2)}) collective-permute-start(bf16[32,1536]{1,0:T(8,128)(2,1)} %param.3), channel_id=1, source_target_pairs={{0,128},{128,256},{256,384},{384,0},{1,129},{129,257},{257,385},{3... | collective-permute-start | bytes 294920 | tf_op jit(solution)/shard_map/ppermute | solution.py:48
  17.0 8.2 %collective-permute-start.1 = (bf16[32,1536]{1,0:T(8,128)(2,1)}, bf16[32,1536]{1,0:T(8,128)(2,1)S(1)}, u32[]{:S(2)}, u32[]{:S(2)}) collective-permute-start(bf16[32,1536]{1,0:T(8,128)(2,1)} %param.3), channel_id=1, source_target_pairs={{0,256},{128,384},{256,0},{384,128},{1,257},{129,385},{257,1},{385... | collective-permute-start | bytes 294920 | tf_op jit(solution)/shard_map/ppermute | solution.py:48
  27.1 103.7 %reduce-scatter.2.cloned.1.call-start = ((), (), s32[]{:S(2)}) async-start(), calls=%async_computation.1 | async-start | bytes 1769472 | tf_op jit(solution)/shard_map/reduce_scatter | solution.py:78
  27.1 11.5 %collective-permute-start.3 = (bf16[256,384]{1,0:T(8,128)(2,1)S(1)}, bf16[256,384]{1,0:T(8,128)(2,1)S(1)}, u32[]{:S(2)}, u32[]{:S(2)}) collective-permute-start(bf16[256,384]{1,0:T(8,128)(2,1)S(1)} %copy-done.3), channel_id=1, source_target_pairs={{0,7},{1,0},{2,1},{3,2},{4,3},{5,4},{6,5},{7,6},{8,15},{9,8},{10,9... | collective-permute-start | bytes 589832 | tf_op jit(solution)/shard_map/ppermute | solution.py:32
  35.5 8.8 %collective-permute-start.6 = (bf16[256,384]{1,0:T(8,128)(2,1)S(1)}, bf16[256,384]{1,0:T(8,128)(2,1)S(1)}, u32[]{:S(2)}, u32[]{:S(2)}) collective-permute-start(bf16[256,384]{1,0:T(8,128)(2,1)S(1)} %copy-done.3), channel_id=1, source_target_pairs={{0,1},{1,2},{2,3},{3,4},{4,5},{5,6},{6,7},{7,0},{8,9},{9,10},{10,1... | collective-permute-start | bytes 589832 | tf_op jit(solution)/shard_map/ppermute | solution.py:29
  38.6 8.8 %collective-permute-start.4 = (bf16[256,384]{1,0:T(8,128)(2,1)S(1)}, bf16[256,384]{1,0:T(8,128)(2,1)S(1)}, u32[]{:S(2)}, u32[]{:S(2)}) collective-permute-start(bf16[256,384]{1,0:T(8,128)(2,1)S(1)} %collective-permute-done.3), channel_id=1, source_target_pairs={{0,7},{1,0},{2,1},{3,2},{4,3},{5,4},{6,5},{7,6},{8,15},{9,8},{10,9... | collective-permute-start | bytes 589832 | tf_op jit(solution)/shard_map/ppermute | solution.py:32
  44.2 8.8 %collective-permute-start.7 = (bf16[256,384]{1,0:T(8,128)(2,1)S(1)}, bf16[256,384]{1,0:T(8,128)(2,1)S(1)}, u32[]{:S(2)}, u32[]{:S(2)}) collective-permute-start(bf16[256,384]{1,0:T(8,128)(2,1)S(1)} %collective-permute-done.6), channel_id=1, source_target_pairs={{0,1},{1,2},{2,3},{3,4},{4,5},{5,6},{6,7},{7,0},{8,9},{9,10},{10,1... | collective-permute-start | bytes 589832 | tf_op jit(solution)/shard_map/ppermute | solution.py:29
  47.4 16.3 %collective-permute-start.5 = (bf16[256,384]{1,0:T(8,128)(2,1)S(1)}, bf16[256,384]{1,0:T(8,128)(2,1)S(1)}, u32[]{:S(2)}, u32[]{:S(2)}) collective-permute-start(bf16[256,384]{1,0:T(8,128)(2,1)S(1)} %collective-permute-done.4), channel_id=1, source_target_pairs={{0,7},{1,0},{2,1},{3,2},{4,3},{5,4},{6,5},{7,6},{8,15},{9,8},{10,9... | collective-permute-start | bytes 589832 | tf_op jit(solution)/shard_map/ppermute | solution.py:32
  53.0 8.8 %collective-permute-start.8 = (bf16[256,384]{1,0:T(8,128)(2,1)S(1)}, bf16[256,384]{1,0:T(8,128)(2,1)S(1)}, u32[]{:S(2)}, u32[]{:S(2)}) collective-permute-start(bf16[256,384]{1,0:T(8,128)(2,1)S(1)} %collective-permute-done.7), channel_id=1, source_target_pairs={{0,1},{1,2},{2,3},{3,4},{4,5},{5,6},{6,7},{7,0},{8,9},{9,10},{10,1... | collective-permute-start | bytes 589832 | tf_op jit(solution)/shard_map/ppermute | solution.py:29
  61.8 8.8 %collective-permute-start.9 = (bf16[256,384]{1,0:T(8,128)(2,1)S(1)}, bf16[256,384]{1,0:T(8,128)(2,1)S(1)}, u32[]{:S(2)}, u32[]{:S(2)}) collective-permute-start(bf16[256,384]{1,0:T(8,128)(2,1)S(1)} %collective-permute-done.8), channel_id=1, source_target_pairs={{0,1},{1,2},{2,3},{3,4},{4,5},{5,6},{6,7},{7,0},{8,9},{9,10},{10,1... | collective-permute-start | bytes 589832 | tf_op jit(solution)/shard_map/ppermute | solution.py:29
  76.4 7.8 %collective-permute-start.10 = (bf16[8,4,32,1536]{3,2,1,0:T(8,128)(2,1)}, bf16[8,4,32,1536]{3,2,1,0:T(8,128)(2,1)S(1)}, u32[]{:S(2)}, u32[]{:S(2)}) collective-permute-start(bf16[8,4,32,1536]{3,2,1,0:T(8,128)(2,1)} %bitcast.69), channel_id=1, source_target_pairs={{0,8},{8,0},{1,9},{9,1},{2,10},{10,2},{3,11},{11,3},{4,12},{12,4},... | collective-permute-start | bytes 9437192 | tf_op jit(solution)/shard_map/ppermute | solution.py:56
  84.2 1.8 %copy-start.1 = (bf16[8,4,32,1536]{3,2,1,0:T(8,128)(2,1)}, bf16[8,4,32,1536]{3,2,1,0:T(8,128)(2,1)S(1)}, u32[]{:S(2)}) copy-start(bf16[8,4,32,1536]{3,2,1,0:T(8,128)(2,1)S(1)} %collective-permute-done.10) | copy-start | bytes 9437188
  89.4 1.9 %copy-start.4 = (bf16[32,32,1536]{2,1,0:T(8,128)(2,1)S(1)}, bf16[32,32,1536]{2,1,0:T(8,128)(2,1)}, u32[]{:S(2)}) copy-start(bf16[32,32,1536]{2,1,0:T(8,128)(2,1)} %all-gather.3.cloned.1.call-done) | copy-start | bytes 9437188
  91.2 1.9 %copy-start.2 = (bf16[8,4,32,1536]{3,2,1,0:T(8,128)(2,1)S(1)}, bf16[8,4,32,1536]{3,2,1,0:T(8,128)(2,1)}, u32[]{:S(2)}) copy-start(bf16[8,4,32,1536]{3,2,1,0:T(8,128)(2,1)} %copy-done.1) | copy-start | bytes 9437188
Sparse Core Ops, SparseCore 0:
  27.2 49.2 all-gather.2
  87.7 43.0 reduce-scatter.1

commit v4 on v3

--- a/solution.py
+++ b/solution.py
@@ -42,14 +42,9 @@
     def body(grad_out, pre_act, down_weight):
         rc = lax.axis_index("rc")
         c = lax.axis_index("col")
-        ix = lax.axis_index("rx")
         tok_blk, width = grad_out.shape
-        rel_x = [grad_out] + [
-            lax.ppermute(grad_out, "rx", shift_pairs(n_x, n_x - k)) for k in range(1, n_x)
-        ]
-        stack_x = jnp.stack(rel_x)
-        twice_x = jnp.concatenate([stack_x, stack_x], axis=0)
-        abs_x = lax.dynamic_slice_in_dim(twice_x, (n_x - ix) % n_x, n_x, 0)
+        w_partner = lax.ppermute(down_weight, "rc", shift_pairs(n_core, 1))
+        abs_x = lax.all_gather(grad_out, "rx", axis=0, tiled=False)
         g_own = lax.all_gather(abs_x, "ry", axis=0, tiled=False)
         rel = ring_gather(pre_act, "col", n_col)
         g_own, rel = lax.optimization_barrier((g_own, rel))
@@ -69,12 +64,12 @@
         gw = lax.dot_general(h_own, go, dn, preferred_element_type=jnp.float32)
         gw = gw + lax.dot_general(h_other, gt, dn, preferred_element_type=jnp.float32)
         grad_weight = gw.astype(jnp.bfloat16)
+        go_t = jnp.transpose(g_own, (1, 0, 2, 3)).reshape(-1, width)
         dn2 = (((1,), (1,)), ((), ()))
-        p_own = lax.dot_general(go, down_weight, dn2, preferred_element_type=jnp.float32)
-        p_other = lax.dot_general(gt, down_weight, dn2, preferred_element_type=jnp.float32)
-        stacked = jnp.stack([p_own, p_other]).astype(jnp.bfloat16)
-        stacked = jnp.transpose(stacked.reshape(n_core, n_y, n_x, tok_blk, hid), (0, 2, 1, 3, 4))
-        stacked = stacked.reshape(n_core, n_x * n_y * tok_blk, hid)
+        p_mine = lax.dot_general(go_t, down_weight, dn2, preferred_element_type=jnp.float32)
+        p_part = lax.dot_general(go_t, w_partner, dn2, preferred_element_type=jnp.float32)
+        p_recv = lax.ppermute(p_part.astype(jnp.bfloat16), "rc", shift_pairs(n_core, 1))
+        stacked = jnp.stack([p_mine.astype(jnp.bfloat16), p_recv])
         red = lax.psum_scatter(stacked, "col", scatter_dimension=1, tiled=True)
         sub = pre_act.shape[0] // (tok_blk * n_core)
         red = red.astype(jnp.float32).reshape(n_core, sub, tok_blk, hid)

time: 140 us -> 137 us (0.979)
  blocking collectives: 0 us -> 17.9 us
  waiting for transfers between devices: 63 us -> 48.2 us
  starting transfers between devices: 42.3 us -> 31.2 us
  other arithmetic: 3.65 us -> 6.21 us
  local copies, waits for them, and re-layouts: 6.85 us -> 9.21 us
    all_gather x0 -> x1, blocking collectives: none -> 17.9 us  [body(): abs_x = lax.all_gather(grad_out, 'rx', axis=0, tiled=False)]
    ppermute x3 -> x2, starting transfers between devices: 13.2 us -> 3.84 us  [the longest x1 1.92 us: body(): w_partner = lax.ppermute(down_weight, 'rc', shift_pairs(n_core, 1))]
    all_gather x1, waiting for transfers between devices: 5.74 us -> 0.01 us  [body(): g_own = lax.all_gather(abs_x, 'ry', axis=0, tiled=False)]
    ppermute x3 -> x2, waiting for transfers between devices: 3.92 us -> 0.01 us  [the longest x1 0.01 us: body(): lax.ppermute(p_part.astype(jnp.bfloat16), 'rc', shift_pairs(n_core, 1))]
    ppermute x3, starting transfers between devices: 19.5 us -> 17.2 us  [ring_gather(): bwd = lax.ppermute(bwd, axis, [(i, (i - 1) % n) for i in range(n)])]
    ppermute x1, waiting for transfers between devices: 2.13 us -> 0.01 us  [body(): g_other = lax.ppermute(g_own, 'rc', shift_pairs(n_core, 1))]
    reduce_scatter x1, waiting for transfers between devices: 35.2 us -> 33.1 us  [body(): red = lax.psum_scatter(stacked, 'col', scatter_dimension=1, tiled=True)]
    dot_general x1, matrix products: 1.42 us -> 3.31 us  [body(): gw = lax.dot_general(h_own, go, dn, preferred_element_type=jnp.float32)]
  transfers between devices with their start and end apart: 13 -> 12, of which waited for: 8 -> 4; matrix products, arithmetic and copies ran while one was open for 8% -> 15% of each run, Pallas kernels for 0% -> 0%
where the time goes in v4:
time: 137 us; the launch traced here: 136 us
  waiting for transfers between devices  48.2 us (35%)
  starting transfers between devices  31.2 us (23%)
  blocking collectives  17.9 us (13%)
  between operations  14.3 us (10%)
  matrix products  9.37 us (7%)
  local copies, waits for them, and re-layouts  9.21 us (7%)
  other arithmetic  6.21 us (5%)
    reduce_scatter x1, waiting for transfers between devices, body(): red = lax.psum_scatter(stacked, 'col', scatter_dimension=1, tiled=True)  33.1 us
    all_gather x1, blocking collectives, body(): abs_x = lax.all_gather(grad_out, 'rx', axis=0, tiled=False)  17.9 us
    ppermute x3, starting transfers between devices, ring_gather(): bwd = lax.ppermute(bwd, axis, [(i, (i - 1) % n) for i in range(n)])  17.2 us
    ppermute x4, waiting for transfers between devices, ring_gather(): fwd = lax.ppermute(fwd, axis, [(i, (i + 1) % n) for i in range(n)])  12.9 us
    ppermute x4, starting transfers between devices, ring_gather(): fwd = lax.ppermute(fwd, axis, [(i, (i + 1) % n) for i in range(n)])  7.67 us
    unnamed x11, local copies, waits for them, and re-layouts  5.83 us
    dot_general x1, matrix products, body(): gw = lax.dot_general(h_own, go, dn, preferred_element_type=jnp.float32)  3.31 us
    convert_element_type x1, other arithmetic, body(): hidden = gelu_fwd(pre_abs.astype(jnp.float32)).astype(jnp.bfloat16)  2.91 us
  transfers between devices with their start and end apart: 12, of which 4 were waited for; matrix products, arithmetic and copies ran while one was open for 15% of the time, Pallas kernels for 0%

profile of v4, /device:TPU:6, one launch (start us, length us, event | category | flops | bytes accessed | tf_op | source)
XLA Modules:
  0.0 136.4 jit_solution(5215588971916077260)
XLA Ops:
  7.2 17.9 %all-gather = bf16[128,1536]{1,0:T(8,128)(2,1)} all-gather(bf16[32,1536]{1,0:T(8,128)(2,1)} %param.3), channel_id=2, replica_groups=mesh['rx'=4,'ry'=8,'rc'=2,'col'=8] {'rx'}, dimensions={0}, use_global_device_ids=true | all-gather | bytes 491520 | tf_op jit(solution)/shard_map/all_gather | solution.py:47
  25.2 6.5 %collective-permute-start = (bf16[256,384]{1,0:T(8,128)(2,1)}, bf16[256,384]{1,0:T(8,128)(2,1)S(1)}, u32[]{:S(2)}, u32[]{:S(2)}) collective-permute-start(bf16[256,384]{1,0:T(8,128)(2,1)} %param.4), channel_id=1, source_target_pairs={{0,7},{1,0},{2,1},{3,2},{4,3},{5,4},{6,5},{7,6},{8,15},{9,8},{10,9... | collective-permute-start | bytes 589832 | tf_op jit(solution)/shard_map/ppermute | solution.py:32
  31.7 1.9 %collective-permute-start.3 = (bf16[256,384]{1,0:T(8,128)(2,1)}, bf16[256,384]{1,0:T(8,128)(2,1)S(1)}, u32[]{:S(2)}, u32[]{:S(2)}) collective-permute-start(bf16[256,384]{1,0:T(8,128)(2,1)} %param.4), channel_id=1, source_target_pairs={{0,1},{1,2},{2,3},{3,4},{4,5},{5,6},{6,7},{7,0},{8,9},{9,10},{10,1... | collective-permute-start | bytes 589832 | tf_op jit(solution)/shard_map/ppermute | solution.py:29
  33.6 1.9 %collective-permute-start.7 = (bf16[384,1536]{1,0:T(8,128)(2,1)}, bf16[384,1536]{1,0:T(8,128)(2,1)S(1)}, u32[]{:S(2)}, u32[]{:S(2)}) collective-permute-start(bf16[384,1536]{1,0:T(8,128)(2,1)} %param.5), channel_id=1, source_target_pairs={{0,8},{8,0},{1,9},{9,1},{2,10},{10,2},{3,11},{11,3},{4,12},{12,4},... | collective-permute-start | bytes 3538952 | tf_op jit(solution)/shard_map/ppermute | solution.py:46
  35.6 1.6 %bitcast_dynamic-update-slice_fusion.7 = bf16[8,256,384]{2,1,0:T(8,128)(2,1)} fusion(bf16[256,384]{1,0:T(8,128)(2,1)} %param.4), kind=kLoop, calls=%fused_computation.45 | loop fusion | bytes 393216
  37.2 5.1 %collective-permute-start.1 = (bf16[256,384]{1,0:T(8,128)(2,1)S(1)}, bf16[256,384]{1,0:T(8,128)(2,1)S(1)}, u32[]{:S(2)}, u32[]{:S(2)}) collective-permute-start(bf16[256,384]{1,0:T(8,128)(2,1)S(1)} %collective-permute-done), channel_id=1, source_target_pairs={{0,7},{1,0},{2,1},{3,2},{4,3},{5,4},{6,5},{7,6},{8,15},{9,8},{10,9... | collective-permute-start | bytes 589832 | tf_op jit(solution)/shard_map/ppermute | solution.py:32
  42.3 1.9 %collective-permute-start.4 = (bf16[256,384]{1,0:T(8,128)(2,1)S(1)}, bf16[256,384]{1,0:T(8,128)(2,1)S(1)}, u32[]{:S(2)}, u32[]{:S(2)}) collective-permute-start(bf16[256,384]{1,0:T(8,128)(2,1)S(1)} %collective-permute-done.3), channel_id=1, source_target_pairs={{0,1},{1,2},{2,3},{3,4},{4,5},{5,6},{6,7},{7,0},{8,9},{9,10},{10,1... | collective-permute-start | bytes 589832 | tf_op jit(solution)/shard_map/ppermute | solution.py:29
  45.0 2.2 %collective-permute-done.1 = bf16[256,384]{1,0:T(8,128)(2,1)S(1)} collective-permute-done((bf16[256,384]{1,0:T(8,128)(2,1)S(1)}, bf16[256,384]{1,0:T(8,128)(2,1)S(1)}, u32[]{:S(2)}, u32[]{:S(2)}) %collective-permute-start.1) | collective-permute-done | bytes 196640 | tf_op jit(solution)/shard_map/ppermute | solution.py:32
  47.1 5.6 %collective-permute-start.2 = (bf16[256,384]{1,0:T(8,128)(2,1)S(1)}, bf16[256,384]{1,0:T(8,128)(2,1)S(1)}, u32[]{:S(2)}, u32[]{:S(2)}) collective-permute-start(bf16[256,384]{1,0:T(8,128)(2,1)S(1)} %collective-permute-done.1), channel_id=1, source_target_pairs={{0,7},{1,0},{2,1},{3,2},{4,3},{5,4},{6,5},{7,6},{8,15},{9,8},{10,9... | collective-permute-start | bytes 589832 | tf_op jit(solution)/shard_map/ppermute | solution.py:32
  52.7 1.9 %collective-permute-start.5 = (bf16[256,384]{1,0:T(8,128)(2,1)S(1)}, bf16[256,384]{1,0:T(8,128)(2,1)S(1)}, u32[]{:S(2)}, u32[]{:S(2)}) collective-permute-start(bf16[256,384]{1,0:T(8,128)(2,1)S(1)} %collective-permute-done.4), channel_id=1, source_target_pairs={{0,1},{1,2},{2,3},{3,4},{4,5},{5,6},{6,7},{7,0},{8,9},{9,10},{10,1... | collective-permute-start | bytes 589832 | tf_op jit(solution)/shard_map/ppermute | solution.py:29
  55.4 6.7 %collective-permute-done.5 = bf16[256,384]{1,0:T(8,128)(2,1)S(1)} collective-permute-done((bf16[256,384]{1,0:T(8,128)(2,1)S(1)}, bf16[256,384]{1,0:T(8,128)(2,1)S(1)}, u32[]{:S(2)}, u32[]{:S(2)}) %collective-permute-start.5) | collective-permute-done | bytes 196640 | tf_op jit(solution)/shard_map/ppermute | solution.py:29
  62.1 1.9 %collective-permute-start.6 = (bf16[256,384]{1,0:T(8,128)(2,1)S(1)}, bf16[256,384]{1,0:T(8,128)(2,1)S(1)}, u32[]{:S(2)}, u32[]{:S(2)}) collective-permute-start(bf16[256,384]{1,0:T(8,128)(2,1)S(1)} %collective-permute-done.5), channel_id=1, source_target_pairs={{0,1},{1,2},{2,3},{3,4},{4,5},{5,6},{6,7},{7,0},{8,9},{9,10},{10,1... | collective-permute-start | bytes 589832 | tf_op jit(solution)/shard_map/ppermute | solution.py:29
  64.8 6.1 %collective-permute-done.6 = bf16[256,384]{1,0:T(8,128)(2,1)S(1)} collective-permute-done((bf16[256,384]{1,0:T(8,128)(2,1)S(1)}, bf16[256,384]{1,0:T(8,128)(2,1)S(1)}, u32[]{:S(2)}, u32[]{:S(2)}) %collective-permute-start.6) | collective-permute-done | bytes 196640 | tf_op jit(solution)/shard_map/ppermute | solution.py:29
  73.7 2.2 %copy.11 = bf16[4,8,32,1536]{3,2,1,0:T(8,128)(2,1)S(1)} copy(bf16[4,8,32,1536]{3,2,0,1:T(8,128)(2,1)} %bitcast.10) | data formatting | bytes 6291456 | tf_op jit(solution)/shard_map/transpose | solution.py:67
  75.9 1.8 %convolution_convert_fusion = bf16[1024,384]{1,0:T(8,128)(2,1)S(1)} fusion(bf16[1024,1536]{1,0:T(8,128)(2,1)S(1)} %bitcast.47, bf16[384,1536]{1,0:T(8,128)(2,1)S(1)} %collective-permute-done.7), kind=kOutput, calls=%fused_computation.16 | convolution fusion | flops 1208352768 | bytes 5111808 | tf_op jit(solution)/shard_map/dot_general | solution.py:70
  77.7 1.9 %collective-permute-start.8 = (bf16[1024,384]{1,0:T(8,128)(2,1)S(1)}, bf16[1024,384]{1,0:T(8,128)(2,1)S(1)}, u32[]{:S(2)}, u32[]{:S(2)}) collective-permute-start(bf16[1024,384]{1,0:T(8,128)(2,1)S(1)} %convolution_convert_fusion), channel_id=1, source_target_pairs={{0,8},{8,0},{1,9},{9,1},{2,10},{10,2},{3,11},{11,3},{4,12},{12,4},... | collective-permute-start | bytes 2359304 | tf_op jit(solution)/shard_map/ppermute | solution.py:71
  79.7 2.4 %collective-permute-start.9 = (bf16[8,4,32,1536]{3,2,1,0:T(8,128)(2,1)}, bf16[8,4,32,1536]{3,2,1,0:T(8,128)(2,1)S(1)}, u32[]{:S(2)}, u32[]{:S(2)}) collective-permute-start(bf16[8,4,32,1536]{3,2,1,0:T(8,128)(2,1)} %bitcast.1), channel_id=1, source_target_pairs={{0,8},{8,0},{1,9},{9,1},{2,10},{10,2},{3,11},{11,3},{4,12},{12,4},... | collective-permute-start | bytes 9437192 | tf_op jit(solution)/shard_map/ppermute | solution.py:51
  82.1 1.8 %fusion.7 = bf16[1,1024,384]{2,1,0:T(8,128)(2,1)S(1)} fusion(bf16[1024,1536]{1,0:T(8,128)(2,1)S(1)} %bitcast.48, bf16[384,1536]{1,0:T(8,128)(2,1)S(1)} %copy-done.1), kind=kOutput, calls=%fused_computation.18 | convolution fusion | flops 1208352768 | bytes 5111808 | tf_op jit(solution)/shard_map/dot_general | solution.py:69
  83.9 1.3 pad_maximum_fusion
  85.3 2.9 %fusion.1 = bf16[8,256,384]{2,1,0:T(8,128)(2,1)S(1)} fusion(s32[]{:T(128)S(6)} %select_n.59, bf16[8,256,384]{2,1,0:T(8,128)(2,1)} %bitcast_dynamic-update-slice_fusion), kind=kLoop, calls=%fused_computation.6 | loop fusion | flops 8650752 | bytes 3145732 | tf_op jit(solution)/shard_map/convert_element_type | solution.py:55
  88.7 3.3 %fusion.17 = f32[384,1536]{1,0:T(8,128)S(1)} fusion(bf16[1024,384]{1,0:T(8,128)(2,1)S(1)} %bitcast.50, bf16[1024,1536]{1,0:T(8,128)(2,1)} %bitcast.20), kind=kOutput, calls=%fused_computation.48 | convolution fusion | flops 1207959552 | bytes 6291456 | tf_op jit(solution)/shard_map/dot_general | solution.py:64
  92.0 2.5 %fusion.5 = bf16[384,1536]{1,0:T(8,128)(2,1)} fusion(f32[384,1536]{1,0:T(8,128)S(1)} %fusion.17, bf16[1024,384]{1,0:T(8,128)(2,1)S(1)} %bitcast.46, bf16[1024,1536]{1,0:T(8,128)(2,1)S(1)} %bitcast.45), kind=kOutput, calls=%fused_computation.13 | convolution fusion | flops 1209139200 | bytes 7471104 | tf_op jit(solution)/shard_map/dot_general | solution.py:65
  94.5 33.1 %reduce-scatter.2.cloned.1.call-done = bf16[2,128,384]{2,1,0:T(8,128)(2,1)} async-done(((bf16[2,1024,384]{2,1,0:T(8,128)(2,1)}), bf16[2,128,384]{2,1,0:T(8,128)(2,1)}) %reduce-scatter.2.cloned.1.call-update) | async-done | bytes 196624 | tf_op jit(solution)/shard_map/reduce_scatter | solution.py:73
  127.5 1.0 convert_element_type.26
  (30 shorter events, 6.5 us)
Async XLA Ops:
  7.2 66.5 %all-gather.4.cloned.1.call-start = ((), (), s32[]{:S(2)}) async-start(), calls=%async_computation.2 | async-start | bytes 3538944 | tf_op jit(solution)/shard_map/all_gather | solution.py:48
  25.2 102.3 %reduce-scatter.2.cloned.1.call-start = ((), (), s32[]{:S(2)}) async-start(), calls=%async_computation.1 | async-start | bytes 1769472 | tf_op jit(solution)/shard_map/reduce_scatter | solution.py:73
  25.2 12.0 %collective-permute-start = (bf16[256,384]{1,0:T(8,128)(2,1)}, bf16[256,384]{1,0:T(8,128)(2,1)S(1)}, u32[]{:S(2)}, u32[]{:S(2)}) collective-permute-start(bf16[256,384]{1,0:T(8,128)(2,1)} %param.4), channel_id=1, source_target_pairs={{0,7},{1,0},{2,1},{3,2},{4,3},{5,4},{6,5},{7,6},{8,15},{9,8},{10,9... | collective-permute-start | bytes 589832 | tf_op jit(solution)/shard_map/ppermute | solution.py:32
  31.7 10.6 %collective-permute-start.3 = (bf16[256,384]{1,0:T(8,128)(2,1)}, bf16[256,384]{1,0:T(8,128)(2,1)S(1)}, u32[]{:S(2)}, u32[]{:S(2)}) collective-permute-start(bf16[256,384]{1,0:T(8,128)(2,1)} %param.4), channel_id=1, source_target_pairs={{0,1},{1,2},{2,3},{3,4},{4,5},{5,6},{6,7},{7,0},{8,9},{9,10},{10,1... | collective-permute-start | bytes 589832 | tf_op jit(solution)/shard_map/ppermute | solution.py:29
  33.6 42.3 %collective-permute-start.7 = (bf16[384,1536]{1,0:T(8,128)(2,1)}, bf16[384,1536]{1,0:T(8,128)(2,1)S(1)}, u32[]{:S(2)}, u32[]{:S(2)}) collective-permute-start(bf16[384,1536]{1,0:T(8,128)(2,1)} %param.5), channel_id=1, source_target_pairs={{0,8},{8,0},{1,9},{9,1},{2,10},{10,2},{3,11},{11,3},{4,12},{12,4},... | collective-permute-start | bytes 3538952 | tf_op jit(solution)/shard_map/ppermute | solution.py:46
  37.2 9.9 %collective-permute-start.1 = (bf16[256,384]{1,0:T(8,128)(2,1)S(1)}, bf16[256,384]{1,0:T(8,128)(2,1)S(1)}, u32[]{:S(2)}, u32[]{:S(2)}) collective-permute-start(bf16[256,384]{1,0:T(8,128)(2,1)S(1)} %collective-permute-done), channel_id=1, source_target_pairs={{0,7},{1,0},{2,1},{3,2},{4,3},{5,4},{6,5},{7,6},{8,15},{9,8},{10,9... | collective-permute-start | bytes 589832 | tf_op jit(solution)/shard_map/ppermute | solution.py:32
  42.3 10.4 %collective-permute-start.4 = (bf16[256,384]{1,0:T(8,128)(2,1)S(1)}, bf16[256,384]{1,0:T(8,128)(2,1)S(1)}, u32[]{:S(2)}, u32[]{:S(2)}) collective-permute-start(bf16[256,384]{1,0:T(8,128)(2,1)S(1)} %collective-permute-done.3), channel_id=1, source_target_pairs={{0,1},{1,2},{2,3},{3,4},{4,5},{5,6},{6,7},{7,0},{8,9},{9,10},{10,1... | collective-permute-start | bytes 589832 | tf_op jit(solution)/shard_map/ppermute | solution.py:29
  47.1 16.9 %collective-permute-start.2 = (bf16[256,384]{1,0:T(8,128)(2,1)S(1)}, bf16[256,384]{1,0:T(8,128)(2,1)S(1)}, u32[]{:S(2)}, u32[]{:S(2)}) collective-permute-start(bf16[256,384]{1,0:T(8,128)(2,1)S(1)} %collective-permute-done.1), channel_id=1, source_target_pairs={{0,7},{1,0},{2,1},{3,2},{4,3},{5,4},{6,5},{7,6},{8,15},{9,8},{10,9... | collective-permute-start | bytes 589832 | tf_op jit(solution)/shard_map/ppermute | solution.py:32
  52.7 9.4 %collective-permute-start.5 = (bf16[256,384]{1,0:T(8,128)(2,1)S(1)}, bf16[256,384]{1,0:T(8,128)(2,1)S(1)}, u32[]{:S(2)}, u32[]{:S(2)}) collective-permute-start(bf16[256,384]{1,0:T(8,128)(2,1)S(1)} %collective-permute-done.4), channel_id=1, source_target_pairs={{0,1},{1,2},{2,3},{3,4},{4,5},{5,6},{6,7},{7,0},{8,9},{9,10},{10,1... | collective-permute-start | bytes 589832 | tf_op jit(solution)/shard_map/ppermute | solution.py:29
  62.1 8.8 %collective-permute-start.6 = (bf16[256,384]{1,0:T(8,128)(2,1)S(1)}, bf16[256,384]{1,0:T(8,128)(2,1)S(1)}, u32[]{:S(2)}, u32[]{:S(2)}) collective-permute-start(bf16[256,384]{1,0:T(8,128)(2,1)S(1)} %collective-permute-done.5), channel_id=1, source_target_pairs={{0,1},{1,2},{2,3},{3,4},{4,5},{5,6},{6,7},{7,0},{8,9},{9,10},{10,1... | collective-permute-start | bytes 589832 | tf_op jit(solution)/shard_map/ppermute | solution.py:29
  75.9 6.2 %copy-start.1 = (bf16[384,1536]{1,0:T(8,128)(2,1)S(1)}, bf16[384,1536]{1,0:T(8,128)(2,1)}, u32[]{:S(2)}) copy-start(bf16[384,1536]{1,0:T(8,128)(2,1)} %param.5) | copy-start | bytes 3538948
  77.7 6.2 %collective-permute-start.8 = (bf16[1024,384]{1,0:T(8,128)(2,1)S(1)}, bf16[1024,384]{1,0:T(8,128)(2,1)S(1)}, u32[]{:S(2)}, u32[]{:S(2)}) collective-permute-start(bf16[1024,384]{1,0:T(8,128)(2,1)S(1)} %convolution_convert_fusion), channel_id=1, source_target_pairs={{0,8},{8,0},{1,9},{9,1},{2,10},{10,2},{3,11},{11,3},{4,12},{12,4},... | collective-permute-start | bytes 2359304 | tf_op jit(solution)/shard_map/ppermute | solution.py:71
  79.7 12.3 %collective-permute-start.9 = (bf16[8,4,32,1536]{3,2,1,0:T(8,128)(2,1)}, bf16[8,4,32,1536]{3,2,1,0:T(8,128)(2,1)S(1)}, u32[]{:S(2)}, u32[]{:S(2)}) collective-permute-start(bf16[8,4,32,1536]{3,2,1,0:T(8,128)(2,1)} %bitcast.1), channel_id=1, source_target_pairs={{0,8},{8,0},{1,9},{9,1},{2,10},{10,2},{3,11},{11,3},{4,12},{12,4},... | collective-permute-start | bytes 9437192 | tf_op jit(solution)/shard_map/ppermute | solution.py:51
  94.5 34.1 %copy-start = (bf16[256,384]{1,0:T(8,128)(2,1)S(1)}, bf16[256,384]{1,0:T(8,128)(2,1)}, u32[]{:S(2)}) copy-start(bf16[256,384]{1,0:T(8,128)(2,1)} %param.4) | copy-start | bytes 589828
Sparse Core Ops, SparseCore 0:
  25.3 47.3 all-gather.3
  85.4 42.0 reduce-scatter.1

commit v5 on v4

--- a/solution.py
+++ b/solution.py
@@ -45,37 +45,38 @@
         tok_blk, width = grad_out.shape
         w_partner = lax.ppermute(down_weight, "rc", shift_pairs(n_core, 1))
         abs_x = lax.all_gather(grad_out, "rx", axis=0, tiled=False)
-        g_own = lax.all_gather(abs_x, "ry", axis=0, tiled=False)
+        g_own = lax.all_gather(abs_x, "ry", axis=1, tiled=False)
         rel = ring_gather(pre_act, "col", n_col)
         g_own, rel = lax.optimization_barrier((g_own, rel))
-        g_other = lax.ppermute(g_own, "rc", shift_pairs(n_core, 1))
-        n_y = g_own.shape[0]
+        n_y = g_own.shape[1]
         both = jnp.concatenate([rel, rel], axis=0)
         pre_abs = lax.dynamic_slice_in_dim(both, (n_col - c) % n_col, n_col, 0)
         hidden = gelu_fwd(pre_abs.astype(jnp.float32)).astype(jnp.bfloat16)
         hid = hidden.shape[-1]
         h5 = hidden.reshape(n_x, n_y, n_core, tok_blk, hid)
-        h5 = jnp.transpose(h5, (2, 1, 0, 3, 4))
+        h5 = jnp.transpose(h5, (2, 0, 1, 3, 4))
         h_own = lax.dynamic_index_in_dim(h5, rc, 0, keepdims=False).reshape(-1, hid)
         h_other = lax.dynamic_index_in_dim(h5, (rc + 1) % n_core, 0, keepdims=False).reshape(-1, hid)
         go = g_own.reshape(-1, width)
+        dn2 = (((1,), (1,)), ((), ()))
+        p_mine = lax.dot_general(go, down_weight, dn2, preferred_element_type=jnp.float32)
+        p_part = lax.dot_general(go, w_partner, dn2, preferred_element_type=jnp.float32)
+        p_recv = lax.ppermute(p_part.astype(jnp.bfloat16), "rc", shift_pairs(n_core, 1))
+        stacked = jnp.stack([p_mine.astype(jnp.bfloat16), p_recv])
+        g_late, stacked = lax.optimization_barrier((g_own, stacked))
+        g_other = lax.ppermute(g_late, "rc", shift_pairs(n_core, 1))
+        red = lax.psum_scatter(stacked, "col", scatter_dimension=1, tiled=True)
         gt = g_other.reshape(-1, width)
         dn = (((0,), (0,)), ((), ()))
         gw = lax.dot_general(h_own, go, dn, preferred_element_type=jnp.float32)
         gw = gw + lax.dot_general(h_other, gt, dn, preferred_element_type=jnp.float32)
         grad_weight = gw.astype(jnp.bfloat16)
-        go_t = jnp.transpose(g_own, (1, 0, 2, 3)).reshape(-1, width)
-        dn2 = (((1,), (1,)), ((), ()))
-        p_mine = lax.dot_general(go_t, down_weight, dn2, preferred_element_type=jnp.float32)
-        p_part = lax.dot_general(go_t, w_partner, dn2, preferred_element_type=jnp.float32)
-        p_recv = lax.ppermute(p_part.astype(jnp.bfloat16), "rc", shift_pairs(n_core, 1))
-        stacked = jnp.stack([p_mine.astype(jnp.bfloat16), p_recv])
-        red = lax.psum_scatter(stacked, "col", scatter_dimension=1, tiled=True)
         sub = pre_act.shape[0] // (tok_blk * n_core)
-        red = red.astype(jnp.float32).reshape(n_core, sub, tok_blk, hid)
-        first = jnp.where(rc == 0, red[0], red[1])
-        second = jnp.where(rc == 0, red[1], red[0])
-        grad_hidden = jnp.stack([first, second], axis=1).reshape(pre_act.shape)
+        red = red.reshape(n_core, sub, tok_blk, hid)
+        grad_weight, red = lax.optimization_barrier((grad_weight, red))
+        first = lax.dynamic_index_in_dim(red, rc, 0, keepdims=False)
+        second = lax.dynamic_index_in_dim(red, (rc + 1) % n_core, 0, keepdims=False)
+        grad_hidden = jnp.stack([first, second], axis=1).reshape(pre_act.shape).astype(jnp.float32)
         grad_pre = (grad_hidden * gelu_grad(pre_act.astype(jnp.float32))).astype(jnp.bfloat16)
         return (grad_pre, grad_weight)
 

time: 137 us -> 137 us (level)
    transpose x1 -> x0, local copies, waits for them, and re-layouts: 2.21 us -> none  [body(): go_t = jnp.transpose(g_own, (1, 0, 2, 3)).reshape(-1, width)]
    dot_general x2, matrix products: 3.61 us -> 5.64 us  [the longest x1 3.84 us: body(): lax.dot_general(go, w_partner, dn2, preferred_element_type=jnp.float32)]
    dot_general x1, matrix products: 3.31 us -> 1.42 us  [body(): gw = lax.dot_general(h_own, go, dn, preferred_element_type=jnp.float32)]
    unnamed x11 -> x15, local copies, waits for them, and re-layouts: 5.83 us -> 7.5 us
  transfers between devices with their start and end apart: 12 -> 12, of which waited for: 4 -> 5; matrix products, arithmetic and copies ran while one was open for 15% -> 11% of each run, Pallas kernels for 0% -> 0%
where the time goes in v5:
time: 137 us; the launch traced here: 136 us
  waiting for transfers between devices  49 us (36%)
  starting transfers between devices  30.8 us (22%)
  blocking collectives  17.9 us (13%)
  between operations  14.3 us (10%)
  matrix products  9.52 us (7%)
  local copies, waits for them, and re-layouts  9.39 us (7%)
  other arithmetic  5.26 us (4%)
    reduce_scatter x1, waiting for transfers between devices, body(): red = lax.psum_scatter(stacked, 'col', scatter_dimension=1, tiled=True)  33.5 us
    all_gather x1, blocking collectives, body(): abs_x = lax.all_gather(grad_out, 'rx', axis=0, tiled=False)  17.9 us
    ppermute x3, starting transfers between devices, ring_gather(): bwd = lax.ppermute(bwd, axis, [(i, (i - 1) % n) for i in range(n)])  17.2 us
    ppermute x4, waiting for transfers between devices, ring_gather(): fwd = lax.ppermute(fwd, axis, [(i, (i + 1) % n) for i in range(n)])  12.9 us
    ppermute x4, starting transfers between devices, ring_gather(): fwd = lax.ppermute(fwd, axis, [(i, (i + 1) % n) for i in range(n)])  7.67 us
    unnamed x15, local copies, waits for them, and re-layouts  7.5 us
    dot_general x1, matrix products, body(): lax.dot_general(go, w_partner, dn2, preferred_element_type=jnp.float32)  3.84 us
    convert_element_type x1, other arithmetic, body(): hidden = gelu_fwd(pre_abs.astype(jnp.float32)).astype(jnp.bfloat16)  2.91 us
  transfers between devices with their start and end apart: 12, of which 5 were waited for; matrix products, arithmetic and copies ran while one was open for 11% of the time, Pallas kernels for 0%

profile of v5, /device:TPU:6, one launch (start us, length us, event | category | flops | bytes accessed | tf_op | source)
XLA Modules:
  0.0 136.2 jit_solution(12693800515319046594)
XLA Ops:
  7.2 17.9 %all-gather = bf16[128,1536]{1,0:T(8,128)(2,1)} all-gather(bf16[32,1536]{1,0:T(8,128)(2,1)} %param.3), channel_id=2, replica_groups=mesh['rx'=4,'ry'=8,'rc'=2,'col'=8] {'rx'}, dimensions={0}, use_global_device_ids=true | all-gather | bytes 491520 | tf_op jit(solution)/shard_map/all_gather | solution.py:47
  25.2 6.5 %collective-permute-start = (bf16[256,384]{1,0:T(8,128)(2,1)}, bf16[256,384]{1,0:T(8,128)(2,1)S(1)}, u32[]{:S(2)}, u32[]{:S(2)}) collective-permute-start(bf16[256,384]{1,0:T(8,128)(2,1)} %param.4), channel_id=1, source_target_pairs={{0,7},{1,0},{2,1},{3,2},{4,3},{5,4},{6,5},{7,6},{8,15},{9,8},{10,9... | collective-permute-start | bytes 589832 | tf_op jit(solution)/shard_map/ppermute | solution.py:32
  31.7 1.9 %collective-permute-start.3 = (bf16[256,384]{1,0:T(8,128)(2,1)}, bf16[256,384]{1,0:T(8,128)(2,1)S(1)}, u32[]{:S(2)}, u32[]{:S(2)}) collective-permute-start(bf16[256,384]{1,0:T(8,128)(2,1)} %param.4), channel_id=1, source_target_pairs={{0,1},{1,2},{2,3},{3,4},{4,5},{5,6},{6,7},{7,0},{8,9},{9,10},{10,1... | collective-permute-start | bytes 589832 | tf_op jit(solution)/shard_map/ppermute | solution.py:29
  33.6 1.9 %collective-permute-start.7 = (bf16[384,1536]{1,0:T(8,128)(2,1)}, bf16[384,1536]{1,0:T(8,128)(2,1)S(1)}, u32[]{:S(2)}, u32[]{:S(2)}) collective-permute-start(bf16[384,1536]{1,0:T(8,128)(2,1)} %param.5), channel_id=1, source_target_pairs={{0,8},{8,0},{1,9},{9,1},{2,10},{10,2},{3,11},{11,3},{4,12},{12,4},... | collective-permute-start | bytes 3538952 | tf_op jit(solution)/shard_map/ppermute | solution.py:46
  35.6 1.6 %bitcast_dynamic-update-slice_fusion.7 = bf16[8,256,384]{2,1,0:T(8,128)(2,1)} fusion(bf16[256,384]{1,0:T(8,128)(2,1)} %param.4), kind=kLoop, calls=%fused_computation.43 | loop fusion | bytes 393216
  37.2 5.1 %collective-permute-start.1 = (bf16[256,384]{1,0:T(8,128)(2,1)S(1)}, bf16[256,384]{1,0:T(8,128)(2,1)S(1)}, u32[]{:S(2)}, u32[]{:S(2)}) collective-permute-start(bf16[256,384]{1,0:T(8,128)(2,1)S(1)} %collective-permute-done), channel_id=1, source_target_pairs={{0,7},{1,0},{2,1},{3,2},{4,3},{5,4},{6,5},{7,6},{8,15},{9,8},{10,9... | collective-permute-start | bytes 589832 | tf_op jit(solution)/shard_map/ppermute | solution.py:32
  42.3 1.9 %collective-permute-start.4 = (bf16[256,384]{1,0:T(8,128)(2,1)S(1)}, bf16[256,384]{1,0:T(8,128)(2,1)S(1)}, u32[]{:S(2)}, u32[]{:S(2)}) collective-permute-start(bf16[256,384]{1,0:T(8,128)(2,1)S(1)} %collective-permute-done.3), channel_id=1, source_target_pairs={{0,1},{1,2},{2,3},{3,4},{4,5},{5,6},{6,7},{7,0},{8,9},{9,10},{10,1... | collective-permute-start | bytes 589832 | tf_op jit(solution)/shard_map/ppermute | solution.py:29
  45.0 2.2 %collective-permute-done.1 = bf16[256,384]{1,0:T(8,128)(2,1)S(1)} collective-permute-done((bf16[256,384]{1,0:T(8,128)(2,1)S(1)}, bf16[256,384]{1,0:T(8,128)(2,1)S(1)}, u32[]{:S(2)}, u32[]{:S(2)}) %collective-permute-start.1) | collective-permute-done | bytes 196640 | tf_op jit(solution)/shard_map/ppermute | solution.py:32
  47.1 5.6 %collective-permute-start.2 = (bf16[256,384]{1,0:T(8,128)(2,1)S(1)}, bf16[256,384]{1,0:T(8,128)(2,1)S(1)}, u32[]{:S(2)}, u32[]{:S(2)}) collective-permute-start(bf16[256,384]{1,0:T(8,128)(2,1)S(1)} %collective-permute-done.1), channel_id=1, source_target_pairs={{0,7},{1,0},{2,1},{3,2},{4,3},{5,4},{6,5},{7,6},{8,15},{9,8},{10,9... | collective-permute-start | bytes 589832 | tf_op jit(solution)/shard_map/ppermute | solution.py:32
  52.7 1.9 %collective-permute-start.5 = (bf16[256,384]{1,0:T(8,128)(2,1)S(1)}, bf16[256,384]{1,0:T(8,128)(2,1)S(1)}, u32[]{:S(2)}, u32[]{:S(2)}) collective-permute-start(bf16[256,384]{1,0:T(8,128)(2,1)S(1)} %collective-permute-done.4), channel_id=1, source_target_pairs={{0,1},{1,2},{2,3},{3,4},{4,5},{5,6},{6,7},{7,0},{8,9},{9,10},{10,1... | collective-permute-start | bytes 589832 | tf_op jit(solution)/shard_map/ppermute | solution.py:29
  55.4 6.7 %collective-permute-done.5 = bf16[256,384]{1,0:T(8,128)(2,1)S(1)} collective-permute-done((bf16[256,384]{1,0:T(8,128)(2,1)S(1)}, bf16[256,384]{1,0:T(8,128)(2,1)S(1)}, u32[]{:S(2)}, u32[]{:S(2)}) %collective-permute-start.5) | collective-permute-done | bytes 196640 | tf_op jit(solution)/shard_map/ppermute | solution.py:29
  62.1 1.9 %collective-permute-start.6 = (bf16[256,384]{1,0:T(8,128)(2,1)S(1)}, bf16[256,384]{1,0:T(8,128)(2,1)S(1)}, u32[]{:S(2)}, u32[]{:S(2)}) collective-permute-start(bf16[256,384]{1,0:T(8,128)(2,1)S(1)} %collective-permute-done.5), channel_id=1, source_target_pairs={{0,1},{1,2},{2,3},{3,4},{4,5},{5,6},{6,7},{7,0},{8,9},{9,10},{10,1... | collective-permute-start | bytes 589832 | tf_op jit(solution)/shard_map/ppermute | solution.py:29
  64.8 6.1 %collective-permute-done.6 = bf16[256,384]{1,0:T(8,128)(2,1)S(1)} collective-permute-done((bf16[256,384]{1,0:T(8,128)(2,1)S(1)}, bf16[256,384]{1,0:T(8,128)(2,1)S(1)}, u32[]{:S(2)}, u32[]{:S(2)}) %collective-permute-start.6) | collective-permute-done | bytes 196640 | tf_op jit(solution)/shard_map/ppermute | solution.py:29
  73.7 3.8 %convolution_convert_fusion = bf16[1024,384]{1,0:T(8,128)(2,1)S(1)} fusion(bf16[1024,1536]{1,0:T(8,128)(2,1)} %bitcast.49, bf16[384,1536]{1,0:T(8,128)(2,1)S(1)} %collective-permute-done.7), kind=kOutput, calls=%fused_computation.16 | convolution fusion | flops 1208352768 | bytes 5111808 | tf_op jit(solution)/shard_map/dot_general | solution.py:63
  77.5 1.9 %collective-permute-start.8 = (bf16[1024,384]{1,0:T(8,128)(2,1)S(1)}, bf16[1024,384]{1,0:T(8,128)(2,1)S(1)}, u32[]{:S(2)}, u32[]{:S(2)}) collective-permute-start(bf16[1024,384]{1,0:T(8,128)(2,1)S(1)} %convolution_convert_fusion), channel_id=1, source_target_pairs={{0,8},{8,0},{1,9},{9,1},{2,10},{10,2},{3,11},{11,3},{4,12},{12,4},... | collective-permute-start | bytes 2359304 | tf_op jit(solution)/shard_map/ppermute | solution.py:64
  79.5 1.8 %fusion.7 = bf16[1,1024,384]{2,1,0:T(8,128)(2,1)S(1)} fusion(bf16[1024,1536]{1,0:T(8,128)(2,1)S(1)} %bitcast.51, bf16[384,1536]{1,0:T(8,128)(2,1)S(1)} %copy-done.3), kind=kOutput, calls=%fused_computation.18 | convolution fusion | flops 1208352768 | bytes 5111808 | tf_op jit(solution)/shard_map/dot_general | solution.py:62
  81.7 1.3 pad_maximum_fusion
  83.1 2.0 %collective-permute-start.9 = (bf16[4,8,32,1536]{3,2,1,0:T(8,128)(2,1)}, bf16[4,8,32,1536]{3,2,1,0:T(8,128)(2,1)S(1)}, u32[]{:S(2)}, u32[]{:S(2)}) collective-permute-start(bf16[4,8,32,1536]{3,2,1,0:T(8,128)(2,1)} %bitcast.50), channel_id=1, source_target_pairs={{0,8},{8,0},{1,9},{9,1},{2,10},{10,2},{3,11},{11,3},{4,12},{12,4},... | collective-permute-start | bytes 9437192 | tf_op jit(solution)/shard_map/ppermute | solution.py:67
  85.2 2.9 %fusion.1 = bf16[8,256,384]{2,1,0:T(8,128)(2,1)S(1)} fusion(s32[]{:T(128)S(6)} %select_n.27, bf16[8,256,384]{2,1,0:T(8,128)(2,1)} %bitcast_dynamic-update-slice_fusion), kind=kLoop, calls=%fused_computation.6 | loop fusion | flops 8650752 | bytes 3145732 | tf_op jit(solution)/shard_map/convert_element_type | solution.py:54
  88.3 1.6 %copy-done.2 = bf16[4,256,1536]{2,1,0:T(8,128)(2,1)S(1)} copy-done((bf16[4,256,1536]{2,1,0:T(8,128)(2,1)S(1)}, bf16[4,256,1536]{2,1,0:T(8,128)(2,1)}, u32[]{:S(2)}) %copy-start.2) | copy-done | bytes 3145752
  90.0 1.4 %fusion.17 = f32[384,1536]{1,0:T(8,128)S(1)} fusion(bf16[1024,384]{1,0:T(8,128)(2,1)S(1)} %bitcast.47, bf16[1024,1536]{1,0:T(8,128)(2,1)S(1)} %bitcast.52), kind=kOutput, calls=%fused_computation.48 | convolution fusion | flops 1207959552 | bytes 6291456 | tf_op jit(solution)/shard_map/dot_general | solution.py:71
  91.4 2.5 %fusion.5 = bf16[384,1536]{1,0:T(8,128)(2,1)} fusion(f32[384,1536]{1,0:T(8,128)S(1)} %fusion.17, bf16[1024,384]{1,0:T(8,128)(2,1)S(1)} %bitcast.44, bf16[1024,1536]{1,0:T(8,128)(2,1)S(1)} %bitcast.43), kind=kOutput, calls=%fused_computation.13 | convolution fusion | flops 1209139200 | bytes 7471104 | tf_op jit(solution)/shard_map/dot_general | solution.py:72
  93.9 33.5 %reduce-scatter.2.cloned.1.call-done = bf16[2,128,384]{2,1,0:T(8,128)(2,1)} async-done(((bf16[2,1024,384]{2,1,0:T(8,128)(2,1)}), bf16[2,128,384]{2,1,0:T(8,128)(2,1)}) %reduce-scatter.2.cloned.1.call-update) | async-done | bytes 196624 | tf_op jit(solution)/shard_map/reduce_scatter | solution.py:68
  128.4 1.0 fusion.15
  (29 shorter events, 6.7 us)
Async XLA Ops:
  7.2 66.5 %all-gather.4.cloned.1.call-start = ((), (), s32[]{:S(2)}) async-start(), calls=%async_computation.2 | async-start | bytes 3538944 | tf_op jit(solution)/shard_map/all_gather | solution.py:48
  25.1 102.2 %reduce-scatter.2.cloned.1.call-start = ((), (), s32[]{:S(2)}) async-start(), calls=%async_computation.1 | async-start | bytes 1769472 | tf_op jit(solution)/shard_map/reduce_scatter | solution.py:68
  25.2 12.0 %collective-permute-start = (bf16[256,384]{1,0:T(8,128)(2,1)}, bf16[256,384]{1,0:T(8,128)(2,1)S(1)}, u32[]{:S(2)}, u32[]{:S(2)}) collective-permute-start(bf16[256,384]{1,0:T(8,128)(2,1)} %param.4), channel_id=1, source_target_pairs={{0,7},{1,0},{2,1},{3,2},{4,3},{5,4},{6,5},{7,6},{8,15},{9,8},{10,9... | collective-permute-start | bytes 589832 | tf_op jit(solution)/shard_map/ppermute | solution.py:32
  31.7 10.6 %collective-permute-start.3 = (bf16[256,384]{1,0:T(8,128)(2,1)}, bf16[256,384]{1,0:T(8,128)(2,1)S(1)}, u32[]{:S(2)}, u32[]{:S(2)}) collective-permute-start(bf16[256,384]{1,0:T(8,128)(2,1)} %param.4), channel_id=1, source_target_pairs={{0,1},{1,2},{2,3},{3,4},{4,5},{5,6},{6,7},{7,0},{8,9},{9,10},{10,1... | collective-permute-start | bytes 589832 | tf_op jit(solution)/shard_map/ppermute | solution.py:29
  33.6 40.1 %collective-permute-start.7 = (bf16[384,1536]{1,0:T(8,128)(2,1)}, bf16[384,1536]{1,0:T(8,128)(2,1)S(1)}, u32[]{:S(2)}, u32[]{:S(2)}) collective-permute-start(bf16[384,1536]{1,0:T(8,128)(2,1)} %param.5), channel_id=1, source_target_pairs={{0,8},{8,0},{1,9},{9,1},{2,10},{10,2},{3,11},{11,3},{4,12},{12,4},... | collective-permute-start | bytes 3538952 | tf_op jit(solution)/shard_map/ppermute | solution.py:46
  37.2 9.9 %collective-permute-start.1 = (bf16[256,384]{1,0:T(8,128)(2,1)S(1)}, bf16[256,384]{1,0:T(8,128)(2,1)S(1)}, u32[]{:S(2)}, u32[]{:S(2)}) collective-permute-start(bf16[256,384]{1,0:T(8,128)(2,1)S(1)} %collective-permute-done), channel_id=1, source_target_pairs={{0,7},{1,0},{2,1},{3,2},{4,3},{5,4},{6,5},{7,6},{8,15},{9,8},{10,9... | collective-permute-start | bytes 589832 | tf_op jit(solution)/shard_map/ppermute | solution.py:32
  42.3 10.4 %collective-permute-start.4 = (bf16[256,384]{1,0:T(8,128)(2,1)S(1)}, bf16[256,384]{1,0:T(8,128)(2,1)S(1)}, u32[]{:S(2)}, u32[]{:S(2)}) collective-permute-start(bf16[256,384]{1,0:T(8,128)(2,1)S(1)} %collective-permute-done.3), channel_id=1, source_target_pairs={{0,1},{1,2},{2,3},{3,4},{4,5},{5,6},{6,7},{7,0},{8,9},{9,10},{10,1... | collective-permute-start | bytes 589832 | tf_op jit(solution)/shard_map/ppermute | solution.py:29
  47.1 16.9 %collective-permute-start.2 = (bf16[256,384]{1,0:T(8,128)(2,1)S(1)}, bf16[256,384]{1,0:T(8,128)(2,1)S(1)}, u32[]{:S(2)}, u32[]{:S(2)}) collective-permute-start(bf16[256,384]{1,0:T(8,128)(2,1)S(1)} %collective-permute-done.1), channel_id=1, source_target_pairs={{0,7},{1,0},{2,1},{3,2},{4,3},{5,4},{6,5},{7,6},{8,15},{9,8},{10,9... | collective-permute-start | bytes 589832 | tf_op jit(solution)/shard_map/ppermute | solution.py:32
  52.7 9.4 %collective-permute-start.5 = (bf16[256,384]{1,0:T(8,128)(2,1)S(1)}, bf16[256,384]{1,0:T(8,128)(2,1)S(1)}, u32[]{:S(2)}, u32[]{:S(2)}) collective-permute-start(bf16[256,384]{1,0:T(8,128)(2,1)S(1)} %collective-permute-done.4), channel_id=1, source_target_pairs={{0,1},{1,2},{2,3},{3,4},{4,5},{5,6},{6,7},{7,0},{8,9},{9,10},{10,1... | collective-permute-start | bytes 589832 | tf_op jit(solution)/shard_map/ppermute | solution.py:29
  62.1 8.8 %collective-permute-start.6 = (bf16[256,384]{1,0:T(8,128)(2,1)S(1)}, bf16[256,384]{1,0:T(8,128)(2,1)S(1)}, u32[]{:S(2)}, u32[]{:S(2)}) collective-permute-start(bf16[256,384]{1,0:T(8,128)(2,1)S(1)} %collective-permute-done.5), channel_id=1, source_target_pairs={{0,1},{1,2},{2,3},{3,4},{4,5},{5,6},{6,7},{7,0},{8,9},{9,10},{10,1... | collective-permute-start | bytes 589832 | tf_op jit(solution)/shard_map/ppermute | solution.py:29
  73.7 5.8 %copy-start.1 = (bf16[4,256,1536]{2,1,0:T(8,128)(2,1)S(1)}, bf16[4,256,1536]{2,1,0:T(8,128)(2,1)}, u32[]{:S(2)}) copy-start(bf16[4,256,1536]{2,1,0:T(8,128)(2,1)} %all-gather.4.cloned.1.call-done) | copy-start | bytes 9437188
  73.7 5.8 %copy-start.3 = (bf16[384,1536]{1,0:T(8,128)(2,1)S(1)}, bf16[384,1536]{1,0:T(8,128)(2,1)}, u32[]{:S(2)}) copy-start(bf16[384,1536]{1,0:T(8,128)(2,1)} %param.5) | copy-start | bytes 3538948
  77.5 4.2 %collective-permute-start.8 = (bf16[1024,384]{1,0:T(8,128)(2,1)S(1)}, bf16[1024,384]{1,0:T(8,128)(2,1)S(1)}, u32[]{:S(2)}, u32[]{:S(2)}) collective-permute-start(bf16[1024,384]{1,0:T(8,128)(2,1)S(1)} %convolution_convert_fusion), channel_id=1, source_target_pairs={{0,8},{8,0},{1,9},{9,1},{2,10},{10,2},{3,11},{11,3},{4,12},{12,4},... | collective-permute-start | bytes 2359304 | tf_op jit(solution)/shard_map/ppermute | solution.py:64
  83.1 8.3 %collective-permute-start.9 = (bf16[4,8,32,1536]{3,2,1,0:T(8,128)(2,1)}, bf16[4,8,32,1536]{3,2,1,0:T(8,128)(2,1)S(1)}, u32[]{:S(2)}, u32[]{:S(2)}) collective-permute-start(bf16[4,8,32,1536]{3,2,1,0:T(8,128)(2,1)} %bitcast.50), channel_id=1, source_target_pairs={{0,8},{8,0},{1,9},{9,1},{2,10},{10,2},{3,11},{11,3},{4,12},{12,4},... | collective-permute-start | bytes 9437192 | tf_op jit(solution)/shard_map/ppermute | solution.py:67
  88.1 1.9 %copy-start.2 = (bf16[4,256,1536]{2,1,0:T(8,128)(2,1)S(1)}, bf16[4,256,1536]{2,1,0:T(8,128)(2,1)}, u32[]{:S(2)}) copy-start(bf16[4,256,1536]{2,1,0:T(8,128)(2,1)} %all-gather.4.cloned.1.call-done) | copy-start | bytes 9437188
  91.4 37.0 %copy-start = (bf16[256,384]{1,0:T(8,128)(2,1)S(1)}, bf16[256,384]{1,0:T(8,128)(2,1)}, u32[]{:S(2)}) copy-start(bf16[256,384]{1,0:T(8,128)(2,1)} %param.4) | copy-start | bytes 589828
Sparse Core Ops, SparseCore 0:
  25.3 47.3 all-gather.3
  85.3 42.0 reduce-scatter.1

commit v6 on v5

--- a/solution.py
+++ b/solution.py
@@ -44,6 +44,7 @@
         c = lax.axis_index("col")
         tok_blk, width = grad_out.shape
         w_partner = lax.ppermute(down_weight, "rc", shift_pairs(n_core, 1))
+        w_both = jnp.concatenate([down_weight, w_partner], axis=0)
         abs_x = lax.all_gather(grad_out, "rx", axis=0, tiled=False)
         g_own = lax.all_gather(abs_x, "ry", axis=1, tiled=False)
         rel = ring_gather(pre_act, "col", n_col)
@@ -59,23 +60,23 @@
         h_other = lax.dynamic_index_in_dim(h5, (rc + 1) % n_core, 0, keepdims=False).reshape(-1, hid)
         go = g_own.reshape(-1, width)
         dn2 = (((1,), (1,)), ((), ()))
-        p_mine = lax.dot_general(go, down_weight, dn2, preferred_element_type=jnp.float32)
-        p_part = lax.dot_general(go, w_partner, dn2, preferred_element_type=jnp.float32)
-        p_recv = lax.ppermute(p_part.astype(jnp.bfloat16), "rc", shift_pairs(n_core, 1))
-        stacked = jnp.stack([p_mine.astype(jnp.bfloat16), p_recv])
-        g_late, stacked = lax.optimization_barrier((g_own, stacked))
+        p_both = lax.dot_general(go, w_both, dn2, preferred_element_type=jnp.float32)
+        p_both = p_both.astype(jnp.bfloat16)
+        g_late, p_both = lax.optimization_barrier((g_own, p_both))
+        red = lax.psum_scatter(p_both, "col", scatter_dimension=0, tiled=True)
         g_other = lax.ppermute(g_late, "rc", shift_pairs(n_core, 1))
-        red = lax.psum_scatter(stacked, "col", scatter_dimension=1, tiled=True)
         gt = g_other.reshape(-1, width)
         dn = (((0,), (0,)), ((), ()))
         gw = lax.dot_general(h_own, go, dn, preferred_element_type=jnp.float32)
         gw = gw + lax.dot_general(h_other, gt, dn, preferred_element_type=jnp.float32)
         grad_weight = gw.astype(jnp.bfloat16)
         sub = pre_act.shape[0] // (tok_blk * n_core)
-        red = red.reshape(n_core, sub, tok_blk, hid)
         grad_weight, red = lax.optimization_barrier((grad_weight, red))
-        first = lax.dynamic_index_in_dim(red, rc, 0, keepdims=False)
-        second = lax.dynamic_index_in_dim(red, (rc + 1) % n_core, 0, keepdims=False)
+        mine = red[:, :hid].reshape(sub, tok_blk, hid)
+        theirs = lax.ppermute(red[:, hid:], "rc", shift_pairs(n_core, 1)).reshape(sub, tok_blk, hid)
+        halves = jnp.stack([mine, theirs])
+        first = lax.dynamic_index_in_dim(halves, rc, 0, keepdims=False)
+        second = lax.dynamic_index_in_dim(halves, (rc + 1) % n_core, 0, keepdims=False)
         grad_hidden = jnp.stack([first, second], axis=1).reshape(pre_act.shape).astype(jnp.float32)
         grad_pre = (grad_hidden * gelu_grad(pre_act.astype(jnp.float32))).astype(jnp.bfloat16)
         return (grad_pre, grad_weight)

time: 137 us -> 138 us (level); the launches traced: 136 us -> 136 us
    dot_general x2 -> x1, matrix products: 5.64 us -> 5.68 us  [body(): lax.dot_general(go, w_both, dn2, preferred_element_type=jnp.float32)]
    unnamed x15 -> x13, local copies, waits for them, and re-layouts: 7.5 us -> 7.5 us
  transfers between devices with their start and end apart: 12 -> 12, of which waited for: 5 -> 5; matrix products, arithmetic and copies ran while one was open for 11% -> 10% of each run, Pallas kernels for 0% -> 0%
where the time goes in v6:
time: 138 us; the launch traced here: 136 us
  waiting for transfers between devices  49.8 us (36%)
  starting transfers between devices  30.9 us (22%)
  blocking collectives  17.9 us (13%)
  between operations  14.2 us (10%)
  matrix products  9.56 us (7%)
  local copies, waits for them, and re-layouts  9.39 us (7%)
  other arithmetic  4.01 us (3%)
    reduce_scatter x1, waiting for transfers between devices, body(): red = lax.psum_scatter(p_both, 'col', scatter_dimension=0, tiled=True)  33.4 us
    all_gather x1, blocking collectives, body(): abs_x = lax.all_gather(grad_out, 'rx', axis=0, tiled=False)  17.9 us
    ppermute x3, starting transfers between devices, ring_gather(): bwd = lax.ppermute(bwd, axis, [(i, (i - 1) % n) for i in range(n)])  17.3 us
    ppermute x4, waiting for transfers between devices, ring_gather(): fwd = lax.ppermute(fwd, axis, [(i, (i + 1) % n) for i in range(n)])  12.9 us
    ppermute x4, starting transfers between devices, ring_gather(): fwd = lax.ppermute(fwd, axis, [(i, (i + 1) % n) for i in range(n)])  7.67 us
    unnamed x13, local copies, waits for them, and re-layouts  7.5 us
    dot_general x1, matrix products, body(): lax.dot_general(go, w_both, dn2, preferred_element_type=jnp.float32)  5.68 us
    convert_element_type x1, other arithmetic, body(): hidden = gelu_fwd(pre_abs.astype(jnp.float32)).astype(jnp.bfloat16)  2.91 us
  transfers between devices with their start and end apart: 12, of which 5 were waited for; matrix products, arithmetic and copies ran while one was open for 10% of the time, Pallas kernels for 0%

profile of v6, /device:TPU:6, one launch (start us, length us, event | category | flops | bytes accessed | tf_op | source)
XLA Modules:
  0.0 135.8 jit_solution(3866268638849148183)
XLA Ops:
  7.2 17.9 %all-gather = bf16[128,1536]{1,0:T(8,128)(2,1)} all-gather(bf16[32,1536]{1,0:T(8,128)(2,1)} %param.3), channel_id=2, replica_groups=mesh['rx'=4,'ry'=8,'rc'=2,'col'=8] {'rx'}, dimensions={0}, use_global_device_ids=true | all-gather | bytes 491520 | tf_op jit(solution)/shard_map/all_gather | solution.py:48
  25.2 6.6 %collective-permute-start = (bf16[256,384]{1,0:T(8,128)(2,1)}, bf16[256,384]{1,0:T(8,128)(2,1)S(1)}, u32[]{:S(2)}, u32[]{:S(2)}) collective-permute-start(bf16[256,384]{1,0:T(8,128)(2,1)} %param.4), channel_id=1, source_target_pairs={{0,7},{1,0},{2,1},{3,2},{4,3},{5,4},{6,5},{7,6},{8,15},{9,8},{10,9... | collective-permute-start | bytes 589832 | tf_op jit(solution)/shard_map/ppermute | solution.py:32
  31.9 1.9 %collective-permute-start.3 = (bf16[256,384]{1,0:T(8,128)(2,1)}, bf16[256,384]{1,0:T(8,128)(2,1)S(1)}, u32[]{:S(2)}, u32[]{:S(2)}) collective-permute-start(bf16[256,384]{1,0:T(8,128)(2,1)} %param.4), channel_id=1, source_target_pairs={{0,1},{1,2},{2,3},{3,4},{4,5},{5,6},{6,7},{7,0},{8,9},{9,10},{10,1... | collective-permute-start | bytes 589832 | tf_op jit(solution)/shard_map/ppermute | solution.py:29
  33.8 1.9 %collective-permute-start.7 = (bf16[384,1536]{1,0:T(8,128)(2,1)}, bf16[384,1536]{1,0:T(8,128)(2,1)S(1)}, u32[]{:S(2)}, u32[]{:S(2)}) collective-permute-start(bf16[384,1536]{1,0:T(8,128)(2,1)} %param.5), channel_id=1, source_target_pairs={{0,8},{8,0},{1,9},{9,1},{2,10},{10,2},{3,11},{11,3},{4,12},{12,4},... | collective-permute-start | bytes 3538952 | tf_op jit(solution)/shard_map/ppermute | solution.py:46
  35.7 1.6 %bitcast_dynamic-update-slice_fusion.7 = bf16[8,256,384]{2,1,0:T(8,128)(2,1)} fusion(bf16[256,384]{1,0:T(8,128)(2,1)} %param.4), kind=kLoop, calls=%fused_computation.48 | loop fusion | bytes 393216
  37.4 5.1 %collective-permute-start.1 = (bf16[256,384]{1,0:T(8,128)(2,1)S(1)}, bf16[256,384]{1,0:T(8,128)(2,1)S(1)}, u32[]{:S(2)}, u32[]{:S(2)}) collective-permute-start(bf16[256,384]{1,0:T(8,128)(2,1)S(1)} %collective-permute-done), channel_id=1, source_target_pairs={{0,7},{1,0},{2,1},{3,2},{4,3},{5,4},{6,5},{7,6},{8,15},{9,8},{10,9... | collective-permute-start | bytes 589832 | tf_op jit(solution)/shard_map/ppermute | solution.py:32
  42.5 1.9 %collective-permute-start.4 = (bf16[256,384]{1,0:T(8,128)(2,1)S(1)}, bf16[256,384]{1,0:T(8,128)(2,1)S(1)}, u32[]{:S(2)}, u32[]{:S(2)}) collective-permute-start(bf16[256,384]{1,0:T(8,128)(2,1)S(1)} %collective-permute-done.3), channel_id=1, source_target_pairs={{0,1},{1,2},{2,3},{3,4},{4,5},{5,6},{6,7},{7,0},{8,9},{9,10},{10,1... | collective-permute-start | bytes 589832 | tf_op jit(solution)/shard_map/ppermute | solution.py:29
  45.1 2.2 %collective-permute-done.1 = bf16[256,384]{1,0:T(8,128)(2,1)S(1)} collective-permute-done((bf16[256,384]{1,0:T(8,128)(2,1)S(1)}, bf16[256,384]{1,0:T(8,128)(2,1)S(1)}, u32[]{:S(2)}, u32[]{:S(2)}) %collective-permute-start.1) | collective-permute-done | bytes 196640 | tf_op jit(solution)/shard_map/ppermute | solution.py:32
  47.3 5.6 %collective-permute-start.2 = (bf16[256,384]{1,0:T(8,128)(2,1)S(1)}, bf16[256,384]{1,0:T(8,128)(2,1)S(1)}, u32[]{:S(2)}, u32[]{:S(2)}) collective-permute-start(bf16[256,384]{1,0:T(8,128)(2,1)S(1)} %collective-permute-done.1), channel_id=1, source_target_pairs={{0,7},{1,0},{2,1},{3,2},{4,3},{5,4},{6,5},{7,6},{8,15},{9,8},{10,9... | collective-permute-start | bytes 589832 | tf_op jit(solution)/shard_map/ppermute | solution.py:32
  52.9 1.9 %collective-permute-start.5 = (bf16[256,384]{1,0:T(8,128)(2,1)S(1)}, bf16[256,384]{1,0:T(8,128)(2,1)S(1)}, u32[]{:S(2)}, u32[]{:S(2)}) collective-permute-start(bf16[256,384]{1,0:T(8,128)(2,1)S(1)} %collective-permute-done.4), channel_id=1, source_target_pairs={{0,1},{1,2},{2,3},{3,4},{4,5},{5,6},{6,7},{7,0},{8,9},{9,10},{10,1... | collective-permute-start | bytes 589832 | tf_op jit(solution)/shard_map/ppermute | solution.py:29
  55.5 6.7 %collective-permute-done.5 = bf16[256,384]{1,0:T(8,128)(2,1)S(1)} collective-permute-done((bf16[256,384]{1,0:T(8,128)(2,1)S(1)}, bf16[256,384]{1,0:T(8,128)(2,1)S(1)}, u32[]{:S(2)}, u32[]{:S(2)}) %collective-permute-start.5) | collective-permute-done | bytes 196640 | tf_op jit(solution)/shard_map/ppermute | solution.py:29
  62.3 1.9 %collective-permute-start.6 = (bf16[256,384]{1,0:T(8,128)(2,1)S(1)}, bf16[256,384]{1,0:T(8,128)(2,1)S(1)}, u32[]{:S(2)}, u32[]{:S(2)}) collective-permute-start(bf16[256,384]{1,0:T(8,128)(2,1)S(1)} %collective-permute-done.5), channel_id=1, source_target_pairs={{0,1},{1,2},{2,3},{3,4},{4,5},{5,6},{6,7},{7,0},{8,9},{9,10},{10,1... | collective-permute-start | bytes 589832 | tf_op jit(solution)/shard_map/ppermute | solution.py:29
  64.9 6.1 %collective-permute-done.6 = bf16[256,384]{1,0:T(8,128)(2,1)S(1)} collective-permute-done((bf16[256,384]{1,0:T(8,128)(2,1)S(1)}, bf16[256,384]{1,0:T(8,128)(2,1)S(1)}, u32[]{:S(2)}, u32[]{:S(2)}) %collective-permute-start.6) | collective-permute-done | bytes 196640 | tf_op jit(solution)/shard_map/ppermute | solution.py:29
  73.8 5.7 %fusion.10 = bf16[1024,768]{1,0:T(8,128)(2,1)} fusion(bf16[1024,1536]{1,0:T(8,128)(2,1)} %bitcast.44, bf16[384,1536]{1,0:T(8,128)(2,1)S(1)} %collective-permute-done.7, bf16[384,1536]{1,0:T(8,128)(2,1)S(1)} %copy-done.2), kind=kOutput, calls=%fused_computation.18 | convolution fusion | flops 2421424128 | bytes 7077888 | tf_op jit(solution)/shard_map/dot_general | solution.py:63
  79.5 1.9 %collective-permute-start.8 = (bf16[4,8,32,1536]{3,2,1,0:T(8,128)(2,1)}, bf16[4,8,32,1536]{3,2,1,0:T(8,128)(2,1)S(1)}, u32[]{:S(2)}, u32[]{:S(2)}) collective-permute-start(bf16[4,8,32,1536]{3,2,1,0:T(8,128)(2,1)} %bitcast.45), channel_id=1, source_target_pairs={{0,8},{8,0},{1,9},{9,1},{2,10},{10,2},{3,11},{11,3},{4,12},{12,4},... | collective-permute-start | bytes 9437192 | tf_op jit(solution)/shard_map/ppermute | solution.py:67
  81.5 2.9 %fusion.1 = bf16[8,256,384]{2,1,0:T(8,128)(2,1)S(1)} fusion(s32[]{:T(128)S(6)} %select_n.27, bf16[8,256,384]{2,1,0:T(8,128)(2,1)} %bitcast_dynamic-update-slice_fusion), kind=kLoop, calls=%fused_computation.6 | loop fusion | flops 8650752 | bytes 3145732 | tf_op jit(solution)/shard_map/convert_element_type | solution.py:55
  84.7 1.6 %copy-done.1 = bf16[4,256,1536]{2,1,0:T(8,128)(2,1)S(1)} copy-done((bf16[4,256,1536]{2,1,0:T(8,128)(2,1)S(1)}, bf16[4,256,1536]{2,1,0:T(8,128)(2,1)}, u32[]{:S(2)}) %copy-start.1) | copy-done | bytes 3145752
  86.3 1.4 %fusion.29 = f32[384,1536]{1,0:T(8,128)S(1)} fusion(bf16[1024,384]{1,0:T(8,128)(2,1)S(1)} %bitcast.41, bf16[1024,1536]{1,0:T(8,128)(2,1)S(1)} %bitcast.46), kind=kOutput, calls=%fused_computation.57 | convolution fusion | flops 1207959552 | bytes 6291456 | tf_op jit(solution)/shard_map/dot_general | solution.py:70
  87.7 2.5 %fusion.5 = bf16[384,1536]{1,0:T(8,128)(2,1)} fusion(f32[384,1536]{1,0:T(8,128)S(1)} %fusion.29, bf16[1024,384]{1,0:T(8,128)(2,1)S(1)} %bitcast.39, bf16[1024,1536]{1,0:T(8,128)(2,1)S(1)} %bitcast.38), kind=kOutput, calls=%fused_computation.13 | convolution fusion | flops 1209139200 | bytes 7471104 | tf_op jit(solution)/shard_map/dot_general | solution.py:71
  90.2 33.4 %reduce-scatter.2.cloned.1.call-done = bf16[128,768]{1,0:T(8,128)(2,1)} async-done(((bf16[1024,768]{1,0:T(8,128)(2,1)}), bf16[128,768]{1,0:T(8,128)(2,1)}) %reduce-scatter.2.cloned.1.call-update) | async-done | bytes 196624 | tf_op jit(solution)/shard_map/reduce_scatter | solution.py:66
  123.6 1.0 fusion.28
  124.6 1.9 %collective-permute-start.9 = (bf16[128,384]{1,0:T(8,128)(2,1)S(1)}, bf16[128,384]{1,0:T(8,128)(2,1)S(1)}, u32[]{:S(2)}, u32[]{:S(2)}) collective-permute-start(bf16[128,384]{1,0:T(8,128)(2,1)S(1)} %get-tuple-element.18), channel_id=1, source_target_pairs={{0,8},{8,0},{1,9},{9,1},{2,10},{10,2},{3,11},{11,3},{4,12},{12,4},... | collective-permute-start | bytes 294920 | tf_op jit(solution)/shard_map/ppermute | solution.py:76
  126.5 1.3 collective-permute-done.9
  127.9 1.0 fusion.21
  (26 shorter events, 5.4 us)
Async XLA Ops:
  7.2 66.7 %all-gather.4.cloned.1.call-start = ((), (), s32[]{:S(2)}) async-start(), calls=%async_computation.2 | async-start | bytes 3538944 | tf_op jit(solution)/shard_map/all_gather | solution.py:49
  25.1 48.7 %copy-start.2 = (bf16[384,1536]{1,0:T(8,128)(2,1)S(1)}, bf16[384,1536]{1,0:T(8,128)(2,1)}, u32[]{:S(2)}) copy-start(bf16[384,1536]{1,0:T(8,128)(2,1)} %param.5) | copy-start | bytes 3538948
  25.2 98.5 %reduce-scatter.2.cloned.1.call-start = ((), (), s32[]{:S(2)}) async-start(), calls=%async_computation.1 | async-start | bytes 1769472 | tf_op jit(solution)/shard_map/reduce_scatter | solution.py:66
  25.2 12.1 %collective-permute-start = (bf16[256,384]{1,0:T(8,128)(2,1)}, bf16[256,384]{1,0:T(8,128)(2,1)S(1)}, u32[]{:S(2)}, u32[]{:S(2)}) collective-permute-start(bf16[256,384]{1,0:T(8,128)(2,1)} %param.4), channel_id=1, source_target_pairs={{0,7},{1,0},{2,1},{3,2},{4,3},{5,4},{6,5},{7,6},{8,15},{9,8},{10,9... | collective-permute-start | bytes 589832 | tf_op jit(solution)/shard_map/ppermute | solution.py:32
  31.9 10.6 %collective-permute-start.3 = (bf16[256,384]{1,0:T(8,128)(2,1)}, bf16[256,384]{1,0:T(8,128)(2,1)S(1)}, u32[]{:S(2)}, u32[]{:S(2)}) collective-permute-start(bf16[256,384]{1,0:T(8,128)(2,1)} %param.4), channel_id=1, source_target_pairs={{0,1},{1,2},{2,3},{3,4},{4,5},{5,6},{6,7},{7,0},{8,9},{9,10},{10,1... | collective-permute-start | bytes 589832 | tf_op jit(solution)/shard_map/ppermute | solution.py:29
  33.8 40.1 %collective-permute-start.7 = (bf16[384,1536]{1,0:T(8,128)(2,1)}, bf16[384,1536]{1,0:T(8,128)(2,1)S(1)}, u32[]{:S(2)}, u32[]{:S(2)}) collective-permute-start(bf16[384,1536]{1,0:T(8,128)(2,1)} %param.5), channel_id=1, source_target_pairs={{0,8},{8,0},{1,9},{9,1},{2,10},{10,2},{3,11},{11,3},{4,12},{12,4},... | collective-permute-start | bytes 3538952 | tf_op jit(solution)/shard_map/ppermute | solution.py:46
  37.4 9.9 %collective-permute-start.1 = (bf16[256,384]{1,0:T(8,128)(2,1)S(1)}, bf16[256,384]{1,0:T(8,128)(2,1)S(1)}, u32[]{:S(2)}, u32[]{:S(2)}) collective-permute-start(bf16[256,384]{1,0:T(8,128)(2,1)S(1)} %collective-permute-done), channel_id=1, source_target_pairs={{0,7},{1,0},{2,1},{3,2},{4,3},{5,4},{6,5},{7,6},{8,15},{9,8},{10,9... | collective-permute-start | bytes 589832 | tf_op jit(solution)/shard_map/ppermute | solution.py:32
  42.5 10.4 %collective-permute-start.4 = (bf16[256,384]{1,0:T(8,128)(2,1)S(1)}, bf16[256,384]{1,0:T(8,128)(2,1)S(1)}, u32[]{:S(2)}, u32[]{:S(2)}) collective-permute-start(bf16[256,384]{1,0:T(8,128)(2,1)S(1)} %collective-permute-done.3), channel_id=1, source_target_pairs={{0,1},{1,2},{2,3},{3,4},{4,5},{5,6},{6,7},{7,0},{8,9},{9,10},{10,1... | collective-permute-start | bytes 589832 | tf_op jit(solution)/shard_map/ppermute | solution.py:29
  47.3 16.9 %collective-permute-start.2 = (bf16[256,384]{1,0:T(8,128)(2,1)S(1)}, bf16[256,384]{1,0:T(8,128)(2,1)S(1)}, u32[]{:S(2)}, u32[]{:S(2)}) collective-permute-start(bf16[256,384]{1,0:T(8,128)(2,1)S(1)} %collective-permute-done.1), channel_id=1, source_target_pairs={{0,7},{1,0},{2,1},{3,2},{4,3},{5,4},{6,5},{7,6},{8,15},{9,8},{10,9... | collective-permute-start | bytes 589832 | tf_op jit(solution)/shard_map/ppermute | solution.py:32
  52.9 9.4 %collective-permute-start.5 = (bf16[256,384]{1,0:T(8,128)(2,1)S(1)}, bf16[256,384]{1,0:T(8,128)(2,1)S(1)}, u32[]{:S(2)}, u32[]{:S(2)}) collective-permute-start(bf16[256,384]{1,0:T(8,128)(2,1)S(1)} %collective-permute-done.4), channel_id=1, source_target_pairs={{0,1},{1,2},{2,3},{3,4},{4,5},{5,6},{6,7},{7,0},{8,9},{9,10},{10,1... | collective-permute-start | bytes 589832 | tf_op jit(solution)/shard_map/ppermute | solution.py:29
  62.3 8.8 %collective-permute-start.6 = (bf16[256,384]{1,0:T(8,128)(2,1)S(1)}, bf16[256,384]{1,0:T(8,128)(2,1)S(1)}, u32[]{:S(2)}, u32[]{:S(2)}) collective-permute-start(bf16[256,384]{1,0:T(8,128)(2,1)S(1)} %collective-permute-done.5), channel_id=1, source_target_pairs={{0,1},{1,2},{2,3},{3,4},{4,5},{5,6},{6,7},{7,0},{8,9},{9,10},{10,1... | collective-permute-start | bytes 589832 | tf_op jit(solution)/shard_map/ppermute | solution.py:29
  79.5 8.2 %collective-permute-start.8 = (bf16[4,8,32,1536]{3,2,1,0:T(8,128)(2,1)}, bf16[4,8,32,1536]{3,2,1,0:T(8,128)(2,1)S(1)}, u32[]{:S(2)}, u32[]{:S(2)}) collective-permute-start(bf16[4,8,32,1536]{3,2,1,0:T(8,128)(2,1)} %bitcast.45), channel_id=1, source_target_pairs={{0,8},{8,0},{1,9},{9,1},{2,10},{10,2},{3,11},{11,3},{4,12},{12,4},... | collective-permute-start | bytes 9437192 | tf_op jit(solution)/shard_map/ppermute | solution.py:67
  84.4 1.9 %copy-start.1 = (bf16[4,256,1536]{2,1,0:T(8,128)(2,1)S(1)}, bf16[4,256,1536]{2,1,0:T(8,128)(2,1)}, u32[]{:S(2)}) copy-start(bf16[4,256,1536]{2,1,0:T(8,128)(2,1)} %all-gather.4.cloned.1.call-done) | copy-start | bytes 9437188
  87.7 40.2 %copy-start = (bf16[256,384]{1,0:T(8,128)(2,1)S(1)}, bf16[256,384]{1,0:T(8,128)(2,1)}, u32[]{:S(2)}) copy-start(bf16[256,384]{1,0:T(8,128)(2,1)} %param.4) | copy-start | bytes 589828
  124.6 3.2 %collective-permute-start.9 = (bf16[128,384]{1,0:T(8,128)(2,1)S(1)}, bf16[128,384]{1,0:T(8,128)(2,1)S(1)}, u32[]{:S(2)}, u32[]{:S(2)}) collective-permute-start(bf16[128,384]{1,0:T(8,128)(2,1)S(1)} %get-tuple-element.18), channel_id=1, source_target_pairs={{0,8},{8,0},{1,9},{9,1},{2,10},{10,2},{3,11},{11,3},{4,12},{12,4},... | collective-permute-start | bytes 294920 | tf_op jit(solution)/shard_map/ppermute | solution.py:76
Sparse Core Ops, SparseCore 0:
  25.3 47.3 all-gather.3
  81.6 42.0 reduce-scatter.1

commit v7 on v5

--- a/solution.py
+++ b/solution.py
@@ -31,7 +31,7 @@
         if k < n - k:
             bwd = lax.ppermute(bwd, axis, [(i, (i - 1) % n) for i in range(n)])
             got[k] = bwd
-    return jnp.stack([got[k] for k in range(n)])
+    return [got[k] for k in range(n)]
 
 
 def shift_pairs(n, s):
@@ -47,8 +47,16 @@
         abs_x = lax.all_gather(grad_out, "rx", axis=0, tiled=False)
         g_own = lax.all_gather(abs_x, "ry", axis=1, tiled=False)
         rel = ring_gather(pre_act, "col", n_col)
-        g_own, rel = lax.optimization_barrier((g_own, rel))
         n_y = g_own.shape[1]
+        go = g_own.reshape(-1, width)
+        dn2 = (((1,), (1,)), ((), ()))
+        p_mine = lax.dot_general(go, down_weight, dn2, preferred_element_type=jnp.float32)
+        p_part = lax.dot_general(go, w_partner, dn2, preferred_element_type=jnp.float32)
+        p_both = jnp.stack([p_mine, p_part]).astype(jnp.bfloat16)
+        g_late, rel, p_both = lax.optimization_barrier((g_own, rel, p_both))
+        red = lax.psum_scatter(p_both, "col", scatter_dimension=1, tiled=True)
+        g_other = lax.ppermute(g_late, "rc", shift_pairs(n_core, 1))
+        rel = jnp.stack(rel)
         both = jnp.concatenate([rel, rel], axis=0)
         pre_abs = lax.dynamic_slice_in_dim(both, (n_col - c) % n_col, n_col, 0)
         hidden = gelu_fwd(pre_abs.astype(jnp.float32)).astype(jnp.bfloat16)
@@ -57,27 +65,20 @@
         h5 = jnp.transpose(h5, (2, 0, 1, 3, 4))
         h_own = lax.dynamic_index_in_dim(h5, rc, 0, keepdims=False).reshape(-1, hid)
         h_other = lax.dynamic_index_in_dim(h5, (rc + 1) % n_core, 0, keepdims=False).reshape(-1, hid)
-        go = g_own.reshape(-1, width)
-        dn2 = (((1,), (1,)), ((), ()))
-        p_mine = lax.dot_general(go, down_weight, dn2, preferred_element_type=jnp.float32)
-        p_part = lax.dot_general(go, w_partner, dn2, preferred_element_type=jnp.float32)
-        p_recv = lax.ppermute(p_part.astype(jnp.bfloat16), "rc", shift_pairs(n_core, 1))
-        stacked = jnp.stack([p_mine.astype(jnp.bfloat16), p_recv])
-        g_late, stacked = lax.optimization_barrier((g_own, stacked))
-        g_other = lax.ppermute(g_late, "rc", shift_pairs(n_core, 1))
-        red = lax.psum_scatter(stacked, "col", scatter_dimension=1, tiled=True)
         gt = g_other.reshape(-1, width)
         dn = (((0,), (0,)), ((), ()))
         gw = lax.dot_general(h_own, go, dn, preferred_element_type=jnp.float32)
         gw = gw + lax.dot_general(h_other, gt, dn, preferred_element_type=jnp.float32)
         grad_weight = gw.astype(jnp.bfloat16)
         sub = pre_act.shape[0] // (tok_blk * n_core)
-        red = red.reshape(n_core, sub, tok_blk, hid)
-        grad_weight, red = lax.optimization_barrier((grad_weight, red))
-        first = lax.dynamic_index_in_dim(red, rc, 0, keepdims=False)
-        second = lax.dynamic_index_in_dim(red, (rc + 1) % n_core, 0, keepdims=False)
-        grad_hidden = jnp.stack([first, second], axis=1).reshape(pre_act.shape).astype(jnp.float32)
-        grad_pre = (grad_hidden * gelu_grad(pre_act.astype(jnp.float32))).astype(jnp.bfloat16)
+        mine = red[0].reshape(sub, tok_blk, hid)
+        theirs = lax.ppermute(red[1], "rc", shift_pairs(n_core, 1)).reshape(sub, tok_blk, hid)
+        first = jnp.where(rc == 0, mine, theirs)
+        second = jnp.where(rc == 0, theirs, mine)
+        gg = gelu_grad(pre_act.astype(jnp.float32)).reshape(sub, n_core, tok_blk, hid)
+        out0 = first.astype(jnp.float32) * gg[:, 0]
+        out1 = second.astype(jnp.float32) * gg[:, 1]
+        grad_pre = jnp.stack([out0, out1], axis=1).reshape(pre_act.shape).astype(jnp.bfloat16)
         return (grad_pre, grad_weight)
 
     return body

time: 137 us -> 142 us (1.036); the launches traced: 136 us -> 139 us
  matrix products: 9.52 us -> 14.5 us
  waiting for transfers between devices: 49 us -> 46.3 us
  local copies, waits for them, and re-layouts: 9.39 us -> 11.5 us
    all_gather x1, waiting for transfers between devices: 0.01 us -> 12.5 us  [body(): g_own = lax.all_gather(abs_x, 'ry', axis=1, tiled=False)]
    reduce_scatter x1, waiting for transfers between devices: 33.5 us -> 27.2 us  [body(): red = lax.psum_scatter(p_both, 'col', scatter_dimension=1, tiled=True)]
    ppermute x4, waiting for transfers between devices: 12.9 us -> 6.59 us  [ring_gather(): fwd = lax.ppermute(fwd, axis, [(i, (i + 1) % n) for i in range(n)])]
    dot_general x1, matrix products: 1.8 us -> 4.17 us  [body(): lax.dot_general(go, down_weight, dn2, preferred_element_type=jnp.float32)]
    ppermute x3, waiting for transfers between devices: 2.17 us -> 0.01 us  [ring_gather(): bwd = lax.ppermute(bwd, axis, [(i, (i - 1) % n) for i in range(n)])]
    add x0 -> x1, other arithmetic: none -> 1.96 us  [gelu_grad(): 0.5 * (1.0 + tangent)]
    dot_general x1, matrix products: 2.45 us -> 4.38 us  [body(): lax.dot_general(h_other, gt, dn, preferred_element_type=jnp.float32)]
    convert_element_type x1, other arithmetic: 2.91 us -> 1.11 us  [body(): hidden = gelu_fwd(pre_abs.astype(jnp.float32)).astype(jnp.bfloat16)]
  transfers between devices with their start and end apart: 12 -> 12, of which waited for: 5 -> 5; matrix products, arithmetic and copies ran while one was open for 11% -> 21% of each run, Pallas kernels for 0% -> 0%
where the time goes in v7:
time: 142 us; the launch traced here: 139 us
  waiting for transfers between devices  46.3 us (33%)
  starting transfers between devices  30.4 us (21%)
  blocking collectives  17.9 us (13%)
  matrix products  14.5 us (10%)
  between operations  14.4 us (10%)
  local copies, waits for them, and re-layouts  11.5 us (8%)
  other arithmetic  4.5 us (3%)
    reduce_scatter x1, waiting for transfers between devices, body(): red = lax.psum_scatter(p_both, 'col', scatter_dimension=1, tiled=True)  27.2 us
    all_gather x1, blocking collectives, body(): abs_x = lax.all_gather(grad_out, 'rx', axis=0, tiled=False)  17.9 us
    ppermute x3, starting transfers between devices, ring_gather(): bwd = lax.ppermute(bwd, axis, [(i, (i - 1) % n) for i in range(n)])  16.8 us
    all_gather x1, waiting for transfers between devices, body(): g_own = lax.all_gather(abs_x, 'ry', axis=1, tiled=False)  12.5 us
    unnamed x43, local copies, waits for them, and re-layouts  8.68 us
    ppermute x4, starting transfers between devices, ring_gather(): fwd = lax.ppermute(fwd, axis, [(i, (i + 1) % n) for i in range(n)])  7.65 us
    ppermute x4, waiting for transfers between devices, ring_gather(): fwd = lax.ppermute(fwd, axis, [(i, (i + 1) % n) for i in range(n)])  6.59 us
    dot_general x1, matrix products, body(): lax.dot_general(h_other, gt, dn, preferred_element_type=jnp.float32)  4.38 us
  transfers between devices with their start and end apart: 12, of which 5 were waited for; matrix products, arithmetic and copies ran while one was open for 21% of the time, Pallas kernels for 0%

profile of v7, /device:TPU:6, one launch (start us, length us, event | category | flops | bytes accessed | tf_op | source)
XLA Modules:
  0.0 139.5 jit_solution(9870550237841051686)
XLA Ops:
  7.2 17.9 %all-gather = bf16[128,1536]{1,0:T(8,128)(2,1)} all-gather(bf16[32,1536]{1,0:T(8,128)(2,1)} %param.3), channel_id=2, replica_groups=mesh['rx'=4,'ry'=8,'rc'=2,'col'=8] {'rx'}, dimensions={0}, use_global_device_ids=true | all-gather | bytes 491520 | tf_op jit(solution)/shard_map/all_gather | solution.py:47
  25.2 1.9 %collective-permute-start.7 = (bf16[384,1536]{1,0:T(8,128)(2,1)}, bf16[384,1536]{1,0:T(8,128)(2,1)}, u32[]{:S(2)}, u32[]{:S(2)}) collective-permute-start(bf16[384,1536]{1,0:T(8,128)(2,1)} %param.5), channel_id=1, source_target_pairs={{0,8},{8,0},{1,9},{9,1},{2,10},{10,2},{3,11},{11,3},{4,12},{12,4},... | collective-permute-start | bytes 3538952 | tf_op jit(solution)/shard_map/ppermute | solution.py:46
  27.1 1.9 %collective-permute-start.3 = (bf16[256,384]{1,0:T(8,128)(2,1)}, bf16[256,384]{1,0:T(8,128)(2,1)S(1)}, u32[]{:S(2)}, u32[]{:S(2)}) collective-permute-start(bf16[256,384]{1,0:T(8,128)(2,1)} %param.4), channel_id=1, source_target_pairs={{0,1},{1,2},{2,3},{3,4},{4,5},{5,6},{6,7},{7,0},{8,9},{9,10},{10,1... | collective-permute-start | bytes 589832 | tf_op jit(solution)/shard_map/ppermute | solution.py:29
  29.0 6.5 %collective-permute-start = (bf16[256,384]{1,0:T(8,128)(2,1)}, bf16[256,384]{1,0:T(8,128)(2,1)S(1)}, u32[]{:S(2)}, u32[]{:S(2)}) collective-permute-start(bf16[256,384]{1,0:T(8,128)(2,1)} %param.4), channel_id=1, source_target_pairs={{0,7},{1,0},{2,1},{3,2},{4,3},{5,4},{6,5},{7,6},{8,15},{9,8},{10,9... | collective-permute-start | bytes 589832 | tf_op jit(solution)/shard_map/ppermute | solution.py:32
  35.6 3.8 %collective-permute-done.3 = bf16[256,384]{1,0:T(8,128)(2,1)S(1)} collective-permute-done((bf16[256,384]{1,0:T(8,128)(2,1)}, bf16[256,384]{1,0:T(8,128)(2,1)S(1)}, u32[]{:S(2)}, u32[]{:S(2)}) %collective-permute-start.3) | collective-permute-done | bytes 196640 | tf_op jit(solution)/shard_map/ppermute | solution.py:29
  39.4 1.9 %collective-permute-start.4 = (bf16[256,384]{1,0:T(8,128)(2,1)S(1)}, bf16[256,384]{1,0:T(8,128)(2,1)S(1)}, u32[]{:S(2)}, u32[]{:S(2)}) collective-permute-start(bf16[256,384]{1,0:T(8,128)(2,1)S(1)} %collective-permute-done.3), channel_id=1, source_target_pairs={{0,1},{1,2},{2,3},{3,4},{4,5},{5,6},{6,7},{7,0},{8,9},{9,10},{10,1... | collective-permute-start | bytes 589832 | tf_op jit(solution)/shard_map/ppermute | solution.py:29
  41.4 5.1 %collective-permute-start.1 = (bf16[256,384]{1,0:T(8,128)(2,1)S(1)}, bf16[256,384]{1,0:T(8,128)(2,1)S(1)}, u32[]{:S(2)}, u32[]{:S(2)}) collective-permute-start(bf16[256,384]{1,0:T(8,128)(2,1)S(1)} %collective-permute-done), channel_id=1, source_target_pairs={{0,7},{1,0},{2,1},{3,2},{4,3},{5,4},{6,5},{7,6},{8,15},{9,8},{10,9... | collective-permute-start | bytes 589832 | tf_op jit(solution)/shard_map/ppermute | solution.py:32
  46.5 2.7 %collective-permute-done.4 = bf16[256,384]{1,0:T(8,128)(2,1)S(1)} collective-permute-done((bf16[256,384]{1,0:T(8,128)(2,1)S(1)}, bf16[256,384]{1,0:T(8,128)(2,1)S(1)}, u32[]{:S(2)}, u32[]{:S(2)}) %collective-permute-start.4) | collective-permute-done | bytes 196640 | tf_op jit(solution)/shard_map/ppermute | solution.py:29
  49.2 1.9 %collective-permute-start.5 = (bf16[256,384]{1,0:T(8,128)(2,1)S(1)}, bf16[256,384]{1,0:T(8,128)(2,1)S(1)}, u32[]{:S(2)}, u32[]{:S(2)}) collective-permute-start(bf16[256,384]{1,0:T(8,128)(2,1)S(1)} %collective-permute-done.4), channel_id=1, source_target_pairs={{0,1},{1,2},{2,3},{3,4},{4,5},{5,6},{6,7},{7,0},{8,9},{9,10},{10,1... | collective-permute-start | bytes 589832 | tf_op jit(solution)/shard_map/ppermute | solution.py:29
  51.1 2.0 %fusion.13 = f32[256,384]{1,0:T(8,128)} fusion(bf16[256,384]{1,0:T(8,128)(2,1)} %param.4), kind=kLoop, calls=%fused_computation.29 | loop fusion | flops 1769472 | bytes 589824 | tf_op jit(solution)/shard_map/add | solution.py:19
  53.1 5.1 %collective-permute-start.2 = (bf16[256,384]{1,0:T(8,128)(2,1)S(1)}, bf16[256,384]{1,0:T(8,128)(2,1)S(1)}, u32[]{:S(2)}, u32[]{:S(2)}) collective-permute-start(bf16[256,384]{1,0:T(8,128)(2,1)S(1)} %collective-permute-done.1), channel_id=1, source_target_pairs={{0,7},{1,0},{2,1},{3,2},{4,3},{5,4},{6,5},{7,6},{8,15},{9,8},{10,9... | collective-permute-start | bytes 589832 | tf_op jit(solution)/shard_map/ppermute | solution.py:32
  58.3 1.9 %collective-permute-start.6 = (bf16[256,384]{1,0:T(8,128)(2,1)S(1)}, bf16[256,384]{1,0:T(8,128)(2,1)S(1)}, u32[]{:S(2)}, u32[]{:S(2)}) collective-permute-start(bf16[256,384]{1,0:T(8,128)(2,1)S(1)} %collective-permute-done.5), channel_id=1, source_target_pairs={{0,1},{1,2},{2,3},{3,4},{4,5},{5,6},{6,7},{7,0},{8,9},{9,10},{10,1... | collective-permute-start | bytes 589832 | tf_op jit(solution)/shard_map/ppermute | solution.py:29
  60.2 12.5 %all-gather.4.cloned.1.call-done = bf16[4,256,1536]{2,1,0:T(8,128)(2,1)} async-done(((bf16[4,32,1536]{2,1,0:T(8,128)(2,1)}), bf16[4,256,1536]{2,1,0:T(8,128)(2,1)}) %all-gather.4.cloned.1.call-update) | async-done | bytes 3145744 | tf_op jit(solution)/shard_map/all_gather | solution.py:48
  72.7 4.2 %fusion.6 = bf16[1,1024,384]{2,1,0:T(8,128)(2,1)S(1)} fusion(bf16[1024,1536]{1,0:T(8,128)(2,1)} %bitcast.70, bf16[384,1536]{1,0:T(8,128)(2,1)} %param.5), kind=kOutput, calls=%fused_computation.15 | convolution fusion | flops 1208352768 | bytes 5111808 | tf_op jit(solution)/shard_map/dot_general | solution.py:53
  76.9 3.1 %fusion.7 = bf16[1,1024,384]{2,1,0:T(8,128)(2,1)S(1)} fusion(bf16[1024,1536]{1,0:T(8,128)(2,1)S(1)} %bitcast.72, bf16[384,1536]{1,0:T(8,128)(2,1)} %collective-permute-done.7), kind=kOutput, calls=%fused_computation.16 | convolution fusion | flops 1208352768 | bytes 5111808 | tf_op jit(solution)/shard_map/dot_general | solution.py:54
  80.0 1.4 pad_maximum_fusion
  82.2 2.1 %collective-permute-start.9 = (bf16[4,8,32,1536]{3,2,1,0:T(8,128)(2,1)}, bf16[4,8,32,1536]{3,2,1,0:T(8,128)(2,1)S(1)}, u32[]{:S(2)}, u32[]{:S(2)}) collective-permute-start(bf16[4,8,32,1536]{3,2,1,0:T(8,128)(2,1)} %bitcast.71), channel_id=1, source_target_pairs={{0,8},{8,0},{1,9},{9,1},{2,10},{10,2},{3,11},{11,3},{4,12},{12,4},... | collective-permute-start | bytes 9437192 | tf_op jit(solution)/shard_map/ppermute | solution.py:58
  84.3 1.0 bitcast_dynamic-update-slice_fusion.12
  92.3 1.1 fusion.1
  93.4 1.1 constant_dynamic-slice_fusion
  94.5 2.8 %fusion.20 = f32[384,1536]{1,0:T(8,128)} fusion(bf16[1024,384]{1,0:T(8,128)(2,1)S(1)} %bitcast.66, bf16[1024,1536]{1,0:T(8,128)(2,1)S(1)} %bitcast.73), kind=kOutput, calls=%fused_computation.58 | convolution fusion | flops 1207959552 | bytes 6291456 | tf_op jit(solution)/shard_map/dot_general | solution.py:70
  97.4 27.2 %reduce-scatter.2.cloned.1.call-done = bf16[2,128,384]{2,1,0:T(8,128)(2,1)} async-done(((bf16[2,1024,384]{2,1,0:T(8,128)(2,1)}), bf16[2,128,384]{2,1,0:T(8,128)(2,1)}) %reduce-scatter.2.cloned.1.call-update) | async-done | bytes 196624 | tf_op jit(solution)/shard_map/reduce_scatter | solution.py:57
  125.5 1.9 %collective-permute-start.8 = (bf16[128,384]{1,0:T(8,128)(2,1)S(1)}, bf16[128,384]{1,0:T(8,128)(2,1)S(1)}, u32[]{:S(2)}, u32[]{:S(2)}) collective-permute-start(bf16[128,384]{1,0:T(8,128)(2,1)S(1)} %get-tuple-element.27), channel_id=1, source_target_pairs={{0,8},{8,0},{1,9},{9,1},{2,10},{10,2},{3,11},{11,3},{4,12},{12,4},... | collective-permute-start | bytes 294920 | tf_op jit(solution)/shard_map/ppermute | solution.py:75
  127.5 4.4 %fusion.5 = bf16[384,1536]{1,0:T(8,128)(2,1)} fusion(f32[384,1536]{1,0:T(8,128)} %fusion.20, bf16[1024,384]{1,0:T(8,128)(2,1)} %bitcast.63, bf16[1024,1536]{1,0:T(8,128)(2,1)S(1)} %bitcast.62), kind=kOutput, calls=%fused_computation.11 | convolution fusion | flops 1209139200 | bytes 7471104 | tf_op jit(solution)/shard_map/dot_general | solution.py:71
  (59 shorter events, 9.7 us)
Async XLA Ops:
  7.2 65.5 %all-gather.4.cloned.1.call-start = ((), (), s32[]{:S(2)}) async-start(), calls=%async_computation.2 | async-start | bytes 3538944 | tf_op jit(solution)/shard_map/all_gather | solution.py:48
  25.1 99.4 %reduce-scatter.2.cloned.1.call-start = ((), (), s32[]{:S(2)}) async-start(), calls=%async_computation.1 | async-start | bytes 1769472 | tf_op jit(solution)/shard_map/reduce_scatter | solution.py:57
  25.2 51.7 %collective-permute-start.7 = (bf16[384,1536]{1,0:T(8,128)(2,1)}, bf16[384,1536]{1,0:T(8,128)(2,1)}, u32[]{:S(2)}, u32[]{:S(2)}) collective-permute-start(bf16[384,1536]{1,0:T(8,128)(2,1)} %param.5), channel_id=1, source_target_pairs={{0,8},{8,0},{1,9},{9,1},{2,10},{10,2},{3,11},{11,3},{4,12},{12,4},... | collective-permute-start | bytes 3538952 | tf_op jit(solution)/shard_map/ppermute | solution.py:46
  27.1 12.3 %collective-permute-start.3 = (bf16[256,384]{1,0:T(8,128)(2,1)}, bf16[256,384]{1,0:T(8,128)(2,1)S(1)}, u32[]{:S(2)}, u32[]{:S(2)}) collective-permute-start(bf16[256,384]{1,0:T(8,128)(2,1)} %param.4), channel_id=1, source_target_pairs={{0,1},{1,2},{2,3},{3,4},{4,5},{5,6},{6,7},{7,0},{8,9},{9,10},{10,1... | collective-permute-start | bytes 589832 | tf_op jit(solution)/shard_map/ppermute | solution.py:29
  29.0 12.3 %collective-permute-start = (bf16[256,384]{1,0:T(8,128)(2,1)}, bf16[256,384]{1,0:T(8,128)(2,1)S(1)}, u32[]{:S(2)}, u32[]{:S(2)}) collective-permute-start(bf16[256,384]{1,0:T(8,128)(2,1)} %param.4), channel_id=1, source_target_pairs={{0,7},{1,0},{2,1},{3,2},{4,3},{5,4},{6,5},{7,6},{8,15},{9,8},{10,9... | collective-permute-start | bytes 589832 | tf_op jit(solution)/shard_map/ppermute | solution.py:32
  39.4 9.8 %collective-permute-start.4 = (bf16[256,384]{1,0:T(8,128)(2,1)S(1)}, bf16[256,384]{1,0:T(8,128)(2,1)S(1)}, u32[]{:S(2)}, u32[]{:S(2)}) collective-permute-start(bf16[256,384]{1,0:T(8,128)(2,1)S(1)} %collective-permute-done.3), channel_id=1, source_target_pairs={{0,1},{1,2},{2,3},{3,4},{4,5},{5,6},{6,7},{7,0},{8,9},{9,10},{10,1... | collective-permute-start | bytes 589832 | tf_op jit(solution)/shard_map/ppermute | solution.py:29
  41.4 35.5 %copy-start.4 = (bf16[256,384]{1,0:T(8,128)(2,1)}, bf16[256,384]{1,0:T(8,128)(2,1)S(1)}, u32[]{:S(2)}) copy-start(bf16[256,384]{1,0:T(8,128)(2,1)S(1)} %collective-permute-done) | copy-start | bytes 589828
  41.4 11.7 %collective-permute-start.1 = (bf16[256,384]{1,0:T(8,128)(2,1)S(1)}, bf16[256,384]{1,0:T(8,128)(2,1)S(1)}, u32[]{:S(2)}, u32[]{:S(2)}) collective-permute-start(bf16[256,384]{1,0:T(8,128)(2,1)S(1)} %collective-permute-done), channel_id=1, source_target_pairs={{0,7},{1,0},{2,1},{3,2},{4,3},{5,4},{6,5},{7,6},{8,15},{9,8},{10,9... | collective-permute-start | bytes 589832 | tf_op jit(solution)/shard_map/ppermute | solution.py:32
  49.2 27.7 %copy-start.2 = (bf16[256,384]{1,0:T(8,128)(2,1)}, bf16[256,384]{1,0:T(8,128)(2,1)S(1)}, u32[]{:S(2)}) copy-start(bf16[256,384]{1,0:T(8,128)(2,1)S(1)} %collective-permute-done.4) | copy-start | bytes 589828
  49.2 9.1 %collective-permute-start.5 = (bf16[256,384]{1,0:T(8,128)(2,1)S(1)}, bf16[256,384]{1,0:T(8,128)(2,1)S(1)}, u32[]{:S(2)}, u32[]{:S(2)}) collective-permute-start(bf16[256,384]{1,0:T(8,128)(2,1)S(1)} %collective-permute-done.4), channel_id=1, source_target_pairs={{0,1},{1,2},{2,3},{3,4},{4,5},{5,6},{6,7},{7,0},{8,9},{9,10},{10,1... | collective-permute-start | bytes 589832 | tf_op jit(solution)/shard_map/ppermute | solution.py:29
  53.1 23.8 %copy-start.7 = (bf16[256,384]{1,0:T(8,128)(2,1)}, bf16[256,384]{1,0:T(8,128)(2,1)S(1)}, u32[]{:S(2)}) copy-start(bf16[256,384]{1,0:T(8,128)(2,1)S(1)} %collective-permute-done.1) | copy-start | bytes 589828
  53.1 28.3 %collective-permute-start.2 = (bf16[256,384]{1,0:T(8,128)(2,1)S(1)}, bf16[256,384]{1,0:T(8,128)(2,1)S(1)}, u32[]{:S(2)}, u32[]{:S(2)}) collective-permute-start(bf16[256,384]{1,0:T(8,128)(2,1)S(1)} %collective-permute-done.1), channel_id=1, source_target_pairs={{0,7},{1,0},{2,1},{3,2},{4,3},{5,4},{6,5},{7,6},{8,15},{9,8},{10,9... | collective-permute-start | bytes 589832 | tf_op jit(solution)/shard_map/ppermute | solution.py:32
  58.3 18.6 %copy-start.5 = (bf16[256,384]{1,0:T(8,128)(2,1)}, bf16[256,384]{1,0:T(8,128)(2,1)S(1)}, u32[]{:S(2)}) copy-start(bf16[256,384]{1,0:T(8,128)(2,1)S(1)} %collective-permute-done.5) | copy-start | bytes 589828
  58.3 23.1 %collective-permute-start.6 = (bf16[256,384]{1,0:T(8,128)(2,1)S(1)}, bf16[256,384]{1,0:T(8,128)(2,1)S(1)}, u32[]{:S(2)}, u32[]{:S(2)}) collective-permute-start(bf16[256,384]{1,0:T(8,128)(2,1)S(1)} %collective-permute-done.5), channel_id=1, source_target_pairs={{0,1},{1,2},{2,3},{3,4},{4,5},{5,6},{6,7},{7,0},{8,9},{9,10},{10,1... | collective-permute-start | bytes 589832 | tf_op jit(solution)/shard_map/ppermute | solution.py:29
  72.7 4.2 %copy-start.12 = (bf16[4,256,1536]{2,1,0:T(8,128)(2,1)S(1)}, bf16[4,256,1536]{2,1,0:T(8,128)(2,1)}, u32[]{:S(2)}) copy-start(bf16[4,256,1536]{2,1,0:T(8,128)(2,1)} %all-gather.4.cloned.1.call-done) | copy-start | bytes 9437188
  80.0 2.1 %copy-start = (bf16[256,384]{1,0:T(8,128)(2,1)S(1)}, bf16[256,384]{1,0:T(8,128)(2,1)}, u32[]{:S(2)}) copy-start(bf16[256,384]{1,0:T(8,128)(2,1)} %param.4) | copy-start | bytes 589828
  82.1 10.0 %copy-start.6 = (bf16[256,384]{1,0:T(8,128)(2,1)S(1)}, bf16[256,384]{1,0:T(8,128)(2,1)}, u32[]{:S(2)}) copy-start(bf16[256,384]{1,0:T(8,128)(2,1)} %copy-done.5) | copy-start | bytes 589828
  82.1 10.1 %copy-start.3 = (bf16[256,384]{1,0:T(8,128)(2,1)S(1)}, bf16[256,384]{1,0:T(8,128)(2,1)}, u32[]{:S(2)}) copy-start(bf16[256,384]{1,0:T(8,128)(2,1)} %copy-done.2) | copy-start | bytes 589828
  82.2 9.9 %copy-start.9 = (bf16[256,384]{1,0:T(8,128)(2,1)S(1)}, bf16[256,384]{1,0:T(8,128)(2,1)}, u32[]{:S(2)}) copy-start(bf16[256,384]{1,0:T(8,128)(2,1)} %copy-done.8) | copy-start | bytes 589828
  82.2 9.9 %copy-start.11 = (bf16[256,384]{1,0:T(8,128)(2,1)S(1)}, bf16[256,384]{1,0:T(8,128)(2,1)}, u32[]{:S(2)}) copy-start(bf16[256,384]{1,0:T(8,128)(2,1)} %copy-done.10) | copy-start | bytes 589828
  82.2 45.3 %collective-permute-start.9 = (bf16[4,8,32,1536]{3,2,1,0:T(8,128)(2,1)}, bf16[4,8,32,1536]{3,2,1,0:T(8,128)(2,1)S(1)}, u32[]{:S(2)}, u32[]{:S(2)}) collective-permute-start(bf16[4,8,32,1536]{3,2,1,0:T(8,128)(2,1)} %bitcast.71), channel_id=1, source_target_pairs={{0,8},{8,0},{1,9},{9,1},{2,10},{10,2},{3,11},{11,3},{4,12},{12,4},... | collective-permute-start | bytes 9437192 | tf_op jit(solution)/shard_map/ppermute | solution.py:58
  92.3 2.3 %copy-start.13 = (bf16[4,256,1536]{2,1,0:T(8,128)(2,1)S(1)}, bf16[4,256,1536]{2,1,0:T(8,128)(2,1)}, u32[]{:S(2)}) copy-start(bf16[4,256,1536]{2,1,0:T(8,128)(2,1)} %all-gather.4.cloned.1.call-done) | copy-start | bytes 9437188
  125.5 6.3 %collective-permute-start.8 = (bf16[128,384]{1,0:T(8,128)(2,1)S(1)}, bf16[128,384]{1,0:T(8,128)(2,1)S(1)}, u32[]{:S(2)}, u32[]{:S(2)}) collective-permute-start(bf16[128,384]{1,0:T(8,128)(2,1)S(1)} %get-tuple-element.27), channel_id=1, source_target_pairs={{0,8},{8,0},{1,9},{9,1},{2,10},{10,2},{3,11},{11,3},{4,12},{12,4},... | collective-permute-start | bytes 294920 | tf_op jit(solution)/shard_map/ppermute | solution.py:75
  127.5 4.4 %copy-start.1 = (f32[256,384]{1,0:T(8,128)S(1)}, f32[256,384]{1,0:T(8,128)}, u32[]{:S(2)}) copy-start(f32[256,384]{1,0:T(8,128)} %fusion.13) | copy-start | bytes 1179652
  (2 other events, 1.4 us)
Sparse Core Ops, SparseCore 0:
  25.3 47.3 all-gather.3
  81.5 42.9 reduce-scatter.1

commit v8 on v7

--- a/solution.py
+++ b/solution.py
@@ -71,6 +71,7 @@
         gw = gw + lax.dot_general(h_other, gt, dn, preferred_element_type=jnp.float32)
         grad_weight = gw.astype(jnp.bfloat16)
         sub = pre_act.shape[0] // (tok_blk * n_core)
+        grad_weight, red = lax.optimization_barrier((grad_weight, red))
         mine = red[0].reshape(sub, tok_blk, hid)
         theirs = lax.ppermute(red[1], "rc", shift_pairs(n_core, 1)).reshape(sub, tok_blk, hid)
         first = jnp.where(rc == 0, mine, theirs)

time: 142 us -> 137 us (0.965)
  waiting for transfers between devices: 46.3 us -> 57 us
  local copies, waits for them, and re-layouts: 11.5 us -> 2.96 us
  matrix products: 14.5 us -> 9.84 us
  other arithmetic: 4.5 us -> 2.76 us
    unnamed x43 -> x21, local copies, waits for them, and re-layouts: 8.68 us -> 1.03 us
    reduce_scatter x1, waiting for transfers between devices: 27.2 us -> 33 us  [body(): red = lax.psum_scatter(p_both, 'col', scatter_dimension=1, tiled=True)]
    ppermute x4, waiting for transfers between devices: 6.59 us -> 8.55 us  [ring_gather(): fwd = lax.ppermute(fwd, axis, [(i, (i + 1) % n) for i in range(n)])]
    dot_general x1, matrix products: 4.38 us -> 2.45 us  [body(): lax.dot_general(h_other, gt, dn, preferred_element_type=jnp.float32)]
    ppermute x1, waiting for transfers between devices: 0.01 us -> 1.9 us  [body(): g_other = lax.ppermute(g_late, 'rc', shift_pairs(n_core, 1))]
    add x1, other arithmetic: 1.96 us -> 0.25 us  [gelu_grad(): 0.5 * (1.0 + tangent)]
  transfers between devices with their start and end apart: 12 -> 12, of which waited for: 5 -> 7; matrix products, arithmetic and copies ran while one was open for 21% -> 10% of each run, Pallas kernels for 0% -> 0%
where the time goes in v8:
time: 137 us; the launch traced here: 135 us
  waiting for transfers between devices  57 us (42%)
  starting transfers between devices  30.3 us (22%)
  blocking collectives  17.9 us (13%)
  between operations  14.4 us (11%)
  matrix products  9.84 us (7%)
  local copies, waits for them, and re-layouts  2.96 us (2%)
  other arithmetic  2.76 us (2%)
    reduce_scatter x1, waiting for transfers between devices, body(): red = lax.psum_scatter(p_both, 'col', scatter_dimension=1, tiled=True)  33 us
    all_gather x1, blocking collectives, body(): abs_x = lax.all_gather(grad_out, 'rx', axis=0, tiled=False)  17.9 us
    ppermute x3, starting transfers between devices, ring_gather(): bwd = lax.ppermute(bwd, axis, [(i, (i - 1) % n) for i in range(n)])  16.8 us
    all_gather x1, waiting for transfers between devices, body(): g_own = lax.all_gather(abs_x, 'ry', axis=1, tiled=False)  12.5 us
    ppermute x4, waiting for transfers between devices, ring_gather(): fwd = lax.ppermute(fwd, axis, [(i, (i + 1) % n) for i in range(n)])  8.55 us
    ppermute x4, starting transfers between devices, ring_gather(): fwd = lax.ppermute(fwd, axis, [(i, (i + 1) % n) for i in range(n)])  7.65 us
    dot_general x1, matrix products, body(): lax.dot_general(go, down_weight, dn2, preferred_element_type=jnp.float32)  4.16 us
  transfers between devices with their start and end apart: 12, of which 7 were waited for; matrix products, arithmetic and copies ran while one was open for 10% of the time, Pallas kernels for 0%

profile of v8, /device:TPU:6, one launch (start us, length us, event | category | flops | bytes accessed | tf_op | source)
XLA Modules:
  0.0 135.1 jit_solution(3761284599460089181)
XLA Ops:
  7.2 17.9 %all-gather = bf16[128,1536]{1,0:T(8,128)(2,1)} all-gather(bf16[32,1536]{1,0:T(8,128)(2,1)} %param.3), channel_id=2, replica_groups=mesh['rx'=4,'ry'=8,'rc'=2,'col'=8] {'rx'}, dimensions={0}, use_global_device_ids=true | all-gather | bytes 491520 | tf_op jit(solution)/shard_map/all_gather | solution.py:47
  25.2 1.9 %collective-permute-start.7 = (bf16[384,1536]{1,0:T(8,128)(2,1)}, bf16[384,1536]{1,0:T(8,128)(2,1)S(1)}, u32[]{:S(2)}, u32[]{:S(2)}) collective-permute-start(bf16[384,1536]{1,0:T(8,128)(2,1)} %param.5), channel_id=1, source_target_pairs={{0,8},{8,0},{1,9},{9,1},{2,10},{10,2},{3,11},{11,3},{4,12},{12,4},... | collective-permute-start | bytes 3538952 | tf_op jit(solution)/shard_map/ppermute | solution.py:46
  27.1 1.9 %collective-permute-start.3 = (bf16[256,384]{1,0:T(8,128)(2,1)}, bf16[256,384]{1,0:T(8,128)(2,1)S(1)}, u32[]{:S(2)}, u32[]{:S(2)}) collective-permute-start(bf16[256,384]{1,0:T(8,128)(2,1)} %param.4), channel_id=1, source_target_pairs={{0,1},{1,2},{2,3},{3,4},{4,5},{5,6},{6,7},{7,0},{8,9},{9,10},{10,1... | collective-permute-start | bytes 589832 | tf_op jit(solution)/shard_map/ppermute | solution.py:29
  29.1 6.5 %collective-permute-start = (bf16[256,384]{1,0:T(8,128)(2,1)}, bf16[256,384]{1,0:T(8,128)(2,1)S(1)}, u32[]{:S(2)}, u32[]{:S(2)}) collective-permute-start(bf16[256,384]{1,0:T(8,128)(2,1)} %param.4), channel_id=1, source_target_pairs={{0,7},{1,0},{2,1},{3,2},{4,3},{5,4},{6,5},{7,6},{8,15},{9,8},{10,9... | collective-permute-start | bytes 589832 | tf_op jit(solution)/shard_map/ppermute | solution.py:32
  35.6 3.8 %collective-permute-done.3 = bf16[256,384]{1,0:T(8,128)(2,1)S(1)} collective-permute-done((bf16[256,384]{1,0:T(8,128)(2,1)}, bf16[256,384]{1,0:T(8,128)(2,1)S(1)}, u32[]{:S(2)}, u32[]{:S(2)}) %collective-permute-start.3) | collective-permute-done | bytes 196640 | tf_op jit(solution)/shard_map/ppermute | solution.py:29
  39.4 1.9 %collective-permute-start.4 = (bf16[256,384]{1,0:T(8,128)(2,1)S(1)}, bf16[256,384]{1,0:T(8,128)(2,1)S(1)}, u32[]{:S(2)}, u32[]{:S(2)}) collective-permute-start(bf16[256,384]{1,0:T(8,128)(2,1)S(1)} %collective-permute-done.3), channel_id=1, source_target_pairs={{0,1},{1,2},{2,3},{3,4},{4,5},{5,6},{6,7},{7,0},{8,9},{9,10},{10,1... | collective-permute-start | bytes 589832 | tf_op jit(solution)/shard_map/ppermute | solution.py:29
  41.3 5.1 %collective-permute-start.1 = (bf16[256,384]{1,0:T(8,128)(2,1)S(1)}, bf16[256,384]{1,0:T(8,128)(2,1)S(1)}, u32[]{:S(2)}, u32[]{:S(2)}) collective-permute-start(bf16[256,384]{1,0:T(8,128)(2,1)S(1)} %collective-permute-done), channel_id=1, source_target_pairs={{0,7},{1,0},{2,1},{3,2},{4,3},{5,4},{6,5},{7,6},{8,15},{9,8},{10,9... | collective-permute-start | bytes 589832 | tf_op jit(solution)/shard_map/ppermute | solution.py:32
  46.5 2.7 %collective-permute-done.4 = bf16[256,384]{1,0:T(8,128)(2,1)S(1)} collective-permute-done((bf16[256,384]{1,0:T(8,128)(2,1)S(1)}, bf16[256,384]{1,0:T(8,128)(2,1)S(1)}, u32[]{:S(2)}, u32[]{:S(2)}) %collective-permute-start.4) | collective-permute-done | bytes 196640 | tf_op jit(solution)/shard_map/ppermute | solution.py:29
  49.2 1.9 %collective-permute-start.5 = (bf16[256,384]{1,0:T(8,128)(2,1)S(1)}, bf16[256,384]{1,0:T(8,128)(2,1)S(1)}, u32[]{:S(2)}, u32[]{:S(2)}) collective-permute-start(bf16[256,384]{1,0:T(8,128)(2,1)S(1)} %collective-permute-done.4), channel_id=1, source_target_pairs={{0,1},{1,2},{2,3},{3,4},{4,5},{5,6},{6,7},{7,0},{8,9},{9,10},{10,1... | collective-permute-start | bytes 589832 | tf_op jit(solution)/shard_map/ppermute | solution.py:29
  51.2 5.1 %collective-permute-start.2 = (bf16[256,384]{1,0:T(8,128)(2,1)S(1)}, bf16[256,384]{1,0:T(8,128)(2,1)S(1)}, u32[]{:S(2)}, u32[]{:S(2)}) collective-permute-start(bf16[256,384]{1,0:T(8,128)(2,1)S(1)} %collective-permute-done.1), channel_id=1, source_target_pairs={{0,7},{1,0},{2,1},{3,2},{4,3},{5,4},{6,5},{7,6},{8,15},{9,8},{10,9... | collective-permute-start | bytes 589832 | tf_op jit(solution)/shard_map/ppermute | solution.py:32
  56.3 2.0 %collective-permute-done.5 = bf16[256,384]{1,0:T(8,128)(2,1)S(1)} collective-permute-done((bf16[256,384]{1,0:T(8,128)(2,1)S(1)}, bf16[256,384]{1,0:T(8,128)(2,1)S(1)}, u32[]{:S(2)}, u32[]{:S(2)}) %collective-permute-start.5) | collective-permute-done | bytes 196640 | tf_op jit(solution)/shard_map/ppermute | solution.py:29
  58.3 1.9 %collective-permute-start.6 = (bf16[256,384]{1,0:T(8,128)(2,1)S(1)}, bf16[256,384]{1,0:T(8,128)(2,1)S(1)}, u32[]{:S(2)}, u32[]{:S(2)}) collective-permute-start(bf16[256,384]{1,0:T(8,128)(2,1)S(1)} %collective-permute-done.5), channel_id=1, source_target_pairs={{0,1},{1,2},{2,3},{3,4},{4,5},{5,6},{6,7},{7,0},{8,9},{9,10},{10,1... | collective-permute-start | bytes 589832 | tf_op jit(solution)/shard_map/ppermute | solution.py:29
  60.2 12.5 %all-gather.4.cloned.1.call-done = bf16[4,256,1536]{2,1,0:T(8,128)(2,1)} async-done(((bf16[4,32,1536]{2,1,0:T(8,128)(2,1)}), bf16[4,256,1536]{2,1,0:T(8,128)(2,1)}) %all-gather.4.cloned.1.call-update) | async-done | bytes 3145744 | tf_op jit(solution)/shard_map/all_gather | solution.py:48
  72.7 4.2 %fusion.6 = bf16[1,1024,384]{2,1,0:T(8,128)(2,1)S(1)} fusion(bf16[1024,1536]{1,0:T(8,128)(2,1)} %bitcast.70, bf16[384,1536]{1,0:T(8,128)(2,1)} %param.5), kind=kOutput, calls=%fused_computation.15 | convolution fusion | flops 1208352768 | bytes 5111808 | tf_op jit(solution)/shard_map/dot_general | solution.py:53
  76.9 1.8 %fusion.7 = bf16[1,1024,384]{2,1,0:T(8,128)(2,1)S(1)} fusion(bf16[1024,1536]{1,0:T(8,128)(2,1)S(1)} %bitcast.72, bf16[384,1536]{1,0:T(8,128)(2,1)S(1)} %collective-permute-done.7), kind=kOutput, calls=%fused_computation.16 | convolution fusion | flops 1208352768 | bytes 5111808 | tf_op jit(solution)/shard_map/dot_general | solution.py:54
  78.7 1.3 pad_maximum_fusion
  80.1 1.9 %collective-permute-start.8 = (bf16[4,8,32,1536]{3,2,1,0:T(8,128)(2,1)}, bf16[4,8,32,1536]{3,2,1,0:T(8,128)(2,1)S(1)}, u32[]{:S(2)}, u32[]{:S(2)}) collective-permute-start(bf16[4,8,32,1536]{3,2,1,0:T(8,128)(2,1)} %bitcast.71), channel_id=1, source_target_pairs={{0,8},{8,0},{1,9},{9,1},{2,10},{10,2},{3,11},{11,3},{4,12},{12,4},... | collective-permute-start | bytes 9437192 | tf_op jit(solution)/shard_map/ppermute | solution.py:58
  82.7 1.1 fusion.1
  84.5 1.4 %fusion.20 = f32[384,1536]{1,0:T(8,128)S(1)} fusion(bf16[1024,384]{1,0:T(8,128)(2,1)S(1)} %bitcast.66, bf16[1024,1536]{1,0:T(8,128)(2,1)S(1)} %bitcast.73), kind=kOutput, calls=%fused_computation.58 | convolution fusion | flops 1207959552 | bytes 6291456 | tf_op jit(solution)/shard_map/dot_general | solution.py:70
  86.0 1.9 %collective-permute-done.8 = bf16[4,8,32,1536]{3,2,1,0:T(8,128)(2,1)S(1)} collective-permute-done((bf16[4,8,32,1536]{3,2,1,0:T(8,128)(2,1)}, bf16[4,8,32,1536]{3,2,1,0:T(8,128)(2,1)S(1)}, u32[]{:S(2)}, u32[]{:S(2)}) %collective-permute-start.8) | collective-permute-done | bytes 3145760 | tf_op jit(solution)/shard_map/ppermute | solution.py:58
  87.9 2.5 %fusion.5 = bf16[384,1536]{1,0:T(8,128)(2,1)} fusion(f32[384,1536]{1,0:T(8,128)S(1)} %fusion.20, bf16[1024,384]{1,0:T(8,128)(2,1)S(1)} %bitcast.63, bf16[1024,1536]{1,0:T(8,128)(2,1)S(1)} %bitcast.62), kind=kOutput, calls=%fused_computation.11 | convolution fusion | flops 1209139200 | bytes 7471104 | tf_op jit(solution)/shard_map/dot_general | solution.py:71
  90.3 33.0 %reduce-scatter.2.cloned.1.call-done = bf16[2,128,384]{2,1,0:T(8,128)(2,1)} async-done(((bf16[2,1024,384]{2,1,0:T(8,128)(2,1)}), bf16[2,128,384]{2,1,0:T(8,128)(2,1)}) %reduce-scatter.2.cloned.1.call-update) | async-done | bytes 196624 | tf_op jit(solution)/shard_map/reduce_scatter | solution.py:57
  124.3 1.9 %collective-permute-start.9 = (bf16[128,384]{1,0:T(8,128)(2,1)S(1)}, bf16[128,384]{1,0:T(8,128)(2,1)S(1)}, u32[]{:S(2)}, u32[]{:S(2)}) collective-permute-start(bf16[128,384]{1,0:T(8,128)(2,1)S(1)} %get-tuple-element.31), channel_id=1, source_target_pairs={{0,8},{8,0},{1,9},{9,1},{2,10},{10,2},{3,11},{11,3},{4,12},{12,4},... | collective-permute-start | bytes 294920 | tf_op jit(solution)/shard_map/ppermute | solution.py:76
  126.5 1.0 collective-permute-done.9
  (37 shorter events, 3.4 us)
Async XLA Ops:
  7.2 65.5 %all-gather.4.cloned.1.call-start = ((), (), s32[]{:S(2)}) async-start(), calls=%async_computation.2 | async-start | bytes 3538944 | tf_op jit(solution)/shard_map/all_gather | solution.py:48
  25.1 98.2 %reduce-scatter.2.cloned.1.call-start = ((), (), s32[]{:S(2)}) async-start(), calls=%async_computation.1 | async-start | bytes 1769472 | tf_op jit(solution)/shard_map/reduce_scatter | solution.py:57
  25.2 51.7 %collective-permute-start.7 = (bf16[384,1536]{1,0:T(8,128)(2,1)}, bf16[384,1536]{1,0:T(8,128)(2,1)S(1)}, u32[]{:S(2)}, u32[]{:S(2)}) collective-permute-start(bf16[384,1536]{1,0:T(8,128)(2,1)} %param.5), channel_id=1, source_target_pairs={{0,8},{8,0},{1,9},{9,1},{2,10},{10,2},{3,11},{11,3},{4,12},{12,4},... | collective-permute-start | bytes 3538952 | tf_op jit(solution)/shard_map/ppermute | solution.py:46
  27.1 12.3 %collective-permute-start.3 = (bf16[256,384]{1,0:T(8,128)(2,1)}, bf16[256,384]{1,0:T(8,128)(2,1)S(1)}, u32[]{:S(2)}, u32[]{:S(2)}) collective-permute-start(bf16[256,384]{1,0:T(8,128)(2,1)} %param.4), channel_id=1, source_target_pairs={{0,1},{1,2},{2,3},{3,4},{4,5},{5,6},{6,7},{7,0},{8,9},{9,10},{10,1... | collective-permute-start | bytes 589832 | tf_op jit(solution)/shard_map/ppermute | solution.py:29
  29.1 12.3 %collective-permute-start = (bf16[256,384]{1,0:T(8,128)(2,1)}, bf16[256,384]{1,0:T(8,128)(2,1)S(1)}, u32[]{:S(2)}, u32[]{:S(2)}) collective-permute-start(bf16[256,384]{1,0:T(8,128)(2,1)} %param.4), channel_id=1, source_target_pairs={{0,7},{1,0},{2,1},{3,2},{4,3},{5,4},{6,5},{7,6},{8,15},{9,8},{10,9... | collective-permute-start | bytes 589832 | tf_op jit(solution)/shard_map/ppermute | solution.py:32
  39.4 9.8 %collective-permute-start.4 = (bf16[256,384]{1,0:T(8,128)(2,1)S(1)}, bf16[256,384]{1,0:T(8,128)(2,1)S(1)}, u32[]{:S(2)}, u32[]{:S(2)}) collective-permute-start(bf16[256,384]{1,0:T(8,128)(2,1)S(1)} %collective-permute-done.3), channel_id=1, source_target_pairs={{0,1},{1,2},{2,3},{3,4},{4,5},{5,6},{6,7},{7,0},{8,9},{9,10},{10,1... | collective-permute-start | bytes 589832 | tf_op jit(solution)/shard_map/ppermute | solution.py:29
  41.3 9.8 %collective-permute-start.1 = (bf16[256,384]{1,0:T(8,128)(2,1)S(1)}, bf16[256,384]{1,0:T(8,128)(2,1)S(1)}, u32[]{:S(2)}, u32[]{:S(2)}) collective-permute-start(bf16[256,384]{1,0:T(8,128)(2,1)S(1)} %collective-permute-done), channel_id=1, source_target_pairs={{0,7},{1,0},{2,1},{3,2},{4,3},{5,4},{6,5},{7,6},{8,15},{9,8},{10,9... | collective-permute-start | bytes 589832 | tf_op jit(solution)/shard_map/ppermute | solution.py:32
  49.2 9.1 %collective-permute-start.5 = (bf16[256,384]{1,0:T(8,128)(2,1)S(1)}, bf16[256,384]{1,0:T(8,128)(2,1)S(1)}, u32[]{:S(2)}, u32[]{:S(2)}) collective-permute-start(bf16[256,384]{1,0:T(8,128)(2,1)S(1)} %collective-permute-done.4), channel_id=1, source_target_pairs={{0,1},{1,2},{2,3},{3,4},{4,5},{5,6},{6,7},{7,0},{8,9},{9,10},{10,1... | collective-permute-start | bytes 589832 | tf_op jit(solution)/shard_map/ppermute | solution.py:29
  51.2 28.9 %collective-permute-start.2 = (bf16[256,384]{1,0:T(8,128)(2,1)S(1)}, bf16[256,384]{1,0:T(8,128)(2,1)S(1)}, u32[]{:S(2)}, u32[]{:S(2)}) collective-permute-start(bf16[256,384]{1,0:T(8,128)(2,1)S(1)} %collective-permute-done.1), channel_id=1, source_target_pairs={{0,7},{1,0},{2,1},{3,2},{4,3},{5,4},{6,5},{7,6},{8,15},{9,8},{10,9... | collective-permute-start | bytes 589832 | tf_op jit(solution)/shard_map/ppermute | solution.py:32
  58.3 21.8 %collective-permute-start.6 = (bf16[256,384]{1,0:T(8,128)(2,1)S(1)}, bf16[256,384]{1,0:T(8,128)(2,1)S(1)}, u32[]{:S(2)}, u32[]{:S(2)}) collective-permute-start(bf16[256,384]{1,0:T(8,128)(2,1)S(1)} %collective-permute-done.5), channel_id=1, source_target_pairs={{0,1},{1,2},{2,3},{3,4},{4,5},{5,6},{6,7},{7,0},{8,9},{9,10},{10,1... | collective-permute-start | bytes 589832 | tf_op jit(solution)/shard_map/ppermute | solution.py:29
  72.7 4.2 %copy-start.1 = (bf16[4,256,1536]{2,1,0:T(8,128)(2,1)S(1)}, bf16[4,256,1536]{2,1,0:T(8,128)(2,1)}, u32[]{:S(2)}) copy-start(bf16[4,256,1536]{2,1,0:T(8,128)(2,1)} %all-gather.4.cloned.1.call-done) | copy-start | bytes 9437188
  78.7 1.4 %copy-start = (bf16[256,384]{1,0:T(8,128)(2,1)S(1)}, bf16[256,384]{1,0:T(8,128)(2,1)}, u32[]{:S(2)}) copy-start(bf16[256,384]{1,0:T(8,128)(2,1)} %param.4) | copy-start | bytes 589828
  80.1 7.8 %collective-permute-start.8 = (bf16[4,8,32,1536]{3,2,1,0:T(8,128)(2,1)}, bf16[4,8,32,1536]{3,2,1,0:T(8,128)(2,1)S(1)}, u32[]{:S(2)}, u32[]{:S(2)}) collective-permute-start(bf16[4,8,32,1536]{3,2,1,0:T(8,128)(2,1)} %bitcast.71), channel_id=1, source_target_pairs={{0,8},{8,0},{1,9},{9,1},{2,10},{10,2},{3,11},{11,3},{4,12},{12,4},... | collective-permute-start | bytes 9437192 | tf_op jit(solution)/shard_map/ppermute | solution.py:58
  82.7 1.9 %copy-start.2 = (bf16[4,256,1536]{2,1,0:T(8,128)(2,1)S(1)}, bf16[4,256,1536]{2,1,0:T(8,128)(2,1)}, u32[]{:S(2)}) copy-start(bf16[4,256,1536]{2,1,0:T(8,128)(2,1)} %all-gather.4.cloned.1.call-done) | copy-start | bytes 9437188
  124.3 3.2 %collective-permute-start.9 = (bf16[128,384]{1,0:T(8,128)(2,1)S(1)}, bf16[128,384]{1,0:T(8,128)(2,1)S(1)}, u32[]{:S(2)}, u32[]{:S(2)}) collective-permute-start(bf16[128,384]{1,0:T(8,128)(2,1)S(1)} %get-tuple-element.31), channel_id=1, source_target_pairs={{0,8},{8,0},{1,9},{9,1},{2,10},{10,2},{3,11},{11,3},{4,12},{12,4},... | collective-permute-start | bytes 294920 | tf_op jit(solution)/shard_map/ppermute | solution.py:76
Sparse Core Ops, SparseCore 0:
  25.3 47.3 all-gather.3
  80.2 43.0 reduce-scatter.1

commit v9 on v8

--- a/solution.py
+++ b/solution.py
@@ -38,23 +38,32 @@
     return [(i, (i + s) % n) for i in range(n)]
 
 
-def make_body(n_x, n_col, n_core):
+def make_body(n_x, n_y, n_col, n_core):
     def body(grad_out, pre_act, down_weight):
         rc = lax.axis_index("rc")
         c = lax.axis_index("col")
         tok_blk, width = grad_out.shape
         w_partner = lax.ppermute(down_weight, "rc", shift_pairs(n_core, 1))
         abs_x = lax.all_gather(grad_out, "rx", axis=0, tiled=False)
-        g_own = lax.all_gather(abs_x, "ry", axis=1, tiled=False)
+        rel_y = ring_gather(abs_x, "ry", n_y)
+        iy = lax.axis_index("ry")
+        stack_y = jnp.stack(rel_y, axis=1)
+        twice_y = jnp.concatenate([stack_y, stack_y], axis=1)
+        g_own = lax.dynamic_slice_in_dim(twice_y, (n_y - iy) % n_y, n_y, 1)
         rel = ring_gather(pre_act, "col", n_col)
-        n_y = g_own.shape[1]
         go = g_own.reshape(-1, width)
         dn2 = (((1,), (1,)), ((), ()))
         p_mine = lax.dot_general(go, down_weight, dn2, preferred_element_type=jnp.float32)
         p_part = lax.dot_general(go, w_partner, dn2, preferred_element_type=jnp.float32)
         p_both = jnp.stack([p_mine, p_part]).astype(jnp.bfloat16)
         g_late, rel, p_both = lax.optimization_barrier((g_own, rel, p_both))
-        red = lax.psum_scatter(p_both, "col", scatter_dimension=1, tiled=True)
+        blocks = p_both.reshape(n_core, n_col, -1, down_weight.shape[0])
+        twice_b = jnp.concatenate([blocks, blocks], axis=1)
+        rel_b = lax.dynamic_slice_in_dim(twice_b, c, n_col, 1)
+        acc = rel_b[:, 0].astype(jnp.float32)
+        for k in range(1, n_col):
+            acc = acc + lax.ppermute(rel_b[:, k], "col", shift_pairs(n_col, k)).astype(jnp.float32)
+        red = acc.astype(jnp.bfloat16)
         g_other = lax.ppermute(g_late, "rc", shift_pairs(n_core, 1))
         rel = jnp.stack(rel)
         both = jnp.concatenate([rel, rel], axis=0)
@@ -98,5 +107,5 @@
     in_specs = (P(row, "col"), P("col", row), P(row, "col"))
     out_specs = (P("col", row), P(row, "col"))
     return jax.shard_map(
-        make_body(n_x, n_col, n_core), mesh=split, in_specs=in_specs, out_specs=out_specs, check_vma=False
+        make_body(n_x, n_row // (n_x * n_core), n_col, n_core), mesh=split, in_specs=in_specs, out_specs=out_specs, check_vma=False
     )

time: 137 us -> 157 us (1.15)
  starting transfers between devices: 30.3 us -> 87.1 us
  waiting for transfers between devices: 57 us -> 39.5 us
  between operations: 14.4 us -> 1.33 us
  blocking collectives: 17.9 us -> 13.5 us
  matrix products: 9.84 us -> 7.47 us
    reduce_scatter x1 -> x0, waiting for transfers between devices: 33 us -> none  [body(): red = lax.psum_scatter(p_both, 'col', scatter_dimension=1, tiled=True)]
    ppermute x0 -> x7, starting transfers between devices: none -> 29.8 us  [body(): lax.ppermute(rel_b[:, k], 'col', shift_pairs(n_col, k)).astype(jnp.float32)]
    ppermute x3 -> x6, starting transfers between devices: 16.8 us -> 33.8 us  [ring_gather(): bwd = lax.ppermute(bwd, axis, [(i, (i - 1) % n) for i in range(n)])]
    ppermute x0 -> x7, waiting for transfers between devices: none -> 16 us  [body(): lax.ppermute(rel_b[:, k], 'col', shift_pairs(n_col, k)).astype(jnp.float32)]
    ppermute x4 -> x8, waiting for transfers between devices: 8.55 us -> 22.4 us  [ring_gather(): fwd = lax.ppermute(fwd, axis, [(i, (i + 1) % n) for i in range(n)])]
    all_gather x1 -> x0, waiting for transfers between devices: 12.5 us -> none  [body(): g_own = lax.all_gather(abs_x, 'ry', axis=1, tiled=False)]
    ppermute x4 -> x8, starting transfers between devices: 7.65 us -> 17.7 us  [ring_gather(): fwd = lax.ppermute(fwd, axis, [(i, (i + 1) % n) for i in range(n)])]
    all_gather x1, blocking collectives: 17.9 us -> 13.5 us  [body(): abs_x = lax.all_gather(grad_out, 'rx', axis=0, tiled=False)]
  transfers between devices with their start and end apart: 12 -> 24, of which waited for: 7 -> 10; matrix products, arithmetic and copies ran while one was open for 10% -> 4% of each run, Pallas kernels for 0% -> 0%
where the time goes in v9:
time: 157 us; the launch traced here: 155 us
  starting transfers between devices  87.1 us (55%)
  waiting for transfers between devices  39.5 us (25%)
  blocking collectives  13.5 us (9%)
  matrix products  7.47 us (5%)
  other arithmetic  3.15 us (2%)
  local copies, waits for them, and re-layouts  2.66 us (2%)
    ppermute x6, starting transfers between devices, ring_gather(): bwd = lax.ppermute(bwd, axis, [(i, (i - 1) % n) for i in range(n)])  33.8 us
    ppermute x7, starting transfers between devices, body(): lax.ppermute(rel_b[:, k], 'col', shift_pairs(n_col, k)).astype(jnp.float32)  29.8 us
    ppermute x8, waiting for transfers between devices, ring_gather(): fwd = lax.ppermute(fwd, axis, [(i, (i + 1) % n) for i in range(n)])  22.4 us
    ppermute x8, starting transfers between devices, ring_gather(): fwd = lax.ppermute(fwd, axis, [(i, (i + 1) % n) for i in range(n)])  17.7 us
    ppermute x7, waiting for transfers between devices, body(): lax.ppermute(rel_b[:, k], 'col', shift_pairs(n_col, k)).astype(jnp.float32)  16 us
    all_gather x1, blocking collectives, body(): abs_x = lax.all_gather(grad_out, 'rx', axis=0, tiled=False)  13.5 us
  transfers between devices with their start and end apart: 24, of which 10 were waited for; matrix products, arithmetic and copies ran while one was open for 4% of the time, Pallas kernels for 0%

profile of v9, /device:TPU:6, one launch (start us, length us, event | category | flops | bytes accessed | tf_op | source)
XLA Modules:
  0.0 154.7 jit_solution(16957675072038191653)
XLA Ops:
  0.6 4.3 %collective-permute-start.10 = (bf16[256,384]{1,0:T(8,128)(2,1)}, bf16[256,384]{1,0:T(8,128)(2,1)S(1)}, u32[]{:S(2)}, u32[]{:S(2)}) collective-permute-start(bf16[256,384]{1,0:T(8,128)(2,1)} %param.4), channel_id=1, source_target_pairs={{0,1},{1,2},{2,3},{3,4},{4,5},{5,6},{6,7},{7,0},{8,9},{9,10},{10,1... | collective-permute-start | bytes 589832 | tf_op jit(solution)/shard_map/ppermute | solution.py:29
  4.9 13.5 %all-gather = bf16[128,1536]{1,0:T(8,128)(2,1)S(1)} all-gather(bf16[32,1536]{1,0:T(8,128)(2,1)} %param.3), channel_id=2, replica_groups=mesh['rx'=4,'ry'=8,'rc'=2,'col'=8] {'rx'}, dimensions={0}, use_global_device_ids=true | all-gather | bytes 491520 | tf_op jit(solution)/shard_map/all_gather | solution.py:47
  18.4 5.0 %collective-permute-start = (bf16[4,32,1536]{2,1,0:T(8,128)(2,1)S(1)}, bf16[4,32,1536]{2,1,0:T(8,128)(2,1)S(1)}, u32[]{:S(2)}, u32[]{:S(2)}) collective-permute-start(bf16[4,32,1536]{2,1,0:T(8,128)(2,1)S(1)} %bitcast.133), channel_id=1, source_target_pairs={{0,112},{16,0},{32,16},{48,32},{64,48},{80,64},{96,80},{112,96},{1... | collective-permute-start | bytes 1179656 | tf_op jit(solution)/shard_map/ppermute | solution.py:32
  25.3 8.6 %collective-permute-start.7 = (bf16[256,384]{1,0:T(8,128)(2,1)}, bf16[256,384]{1,0:T(8,128)(2,1)S(1)}, u32[]{:S(2)}, u32[]{:S(2)}) collective-permute-start(bf16[256,384]{1,0:T(8,128)(2,1)} %param.4), channel_id=1, source_target_pairs={{0,7},{1,0},{2,1},{3,2},{4,3},{5,4},{6,5},{7,6},{8,15},{9,8},{10,9... | collective-permute-start | bytes 589832 | tf_op jit(solution)/shard_map/ppermute | solution.py:32
  33.9 1.9 %collective-permute-start.14 = (bf16[384,1536]{1,0:T(8,128)(2,1)}, bf16[384,1536]{1,0:T(8,128)(2,1)S(1)}, u32[]{:S(2)}, u32[]{:S(2)}) collective-permute-start(bf16[384,1536]{1,0:T(8,128)(2,1)} %param.5), channel_id=1, source_target_pairs={{0,8},{8,0},{1,9},{9,1},{2,10},{10,2},{3,11},{11,3},{4,12},{12,4},... | collective-permute-start | bytes 3538952 | tf_op jit(solution)/shard_map/ppermute | solution.py:46
  35.9 1.9 %collective-permute-start.11 = (bf16[256,384]{1,0:T(8,128)(2,1)S(1)}, bf16[256,384]{1,0:T(8,128)(2,1)S(1)}, u32[]{:S(2)}, u32[]{:S(2)}) collective-permute-start(bf16[256,384]{1,0:T(8,128)(2,1)S(1)} %collective-permute-done.10), channel_id=1, source_target_pairs={{0,1},{1,2},{2,3},{3,4},{4,5},{5,6},{6,7},{7,0},{8,9},{9,10},{10,1... | collective-permute-start | bytes 589832 | tf_op jit(solution)/shard_map/ppermute | solution.py:29
  37.9 5.1 %collective-permute-start.8 = (bf16[256,384]{1,0:T(8,128)(2,1)S(1)}, bf16[256,384]{1,0:T(8,128)(2,1)S(1)}, u32[]{:S(2)}, u32[]{:S(2)}) collective-permute-start(bf16[256,384]{1,0:T(8,128)(2,1)S(1)} %collective-permute-done.7), channel_id=1, source_target_pairs={{0,7},{1,0},{2,1},{3,2},{4,3},{5,4},{6,5},{7,6},{8,15},{9,8},{10,9... | collective-permute-start | bytes 589832 | tf_op jit(solution)/shard_map/ppermute | solution.py:32
  43.0 5.1 %collective-permute-start.1 = (bf16[4,32,1536]{2,1,0:T(8,128)(2,1)S(1)}, bf16[4,32,1536]{2,1,0:T(8,128)(2,1)S(1)}, u32[]{:S(2)}, u32[]{:S(2)}) collective-permute-start(bf16[4,32,1536]{2,1,0:T(8,128)(2,1)S(1)} %collective-permute-done), channel_id=1, source_target_pairs={{0,112},{16,0},{32,16},{48,32},{64,48},{80,64},{96,80},{112,96},{1... | collective-permute-start | bytes 1179656 | tf_op jit(solution)/shard_map/ppermute | solution.py:32
  52.1 5.1 %collective-permute-start.9 = (bf16[256,384]{1,0:T(8,128)(2,1)S(1)}, bf16[256,384]{1,0:T(8,128)(2,1)S(1)}, u32[]{:S(2)}, u32[]{:S(2)}) collective-permute-start(bf16[256,384]{1,0:T(8,128)(2,1)S(1)} %collective-permute-done.8), channel_id=1, source_target_pairs={{0,7},{1,0},{2,1},{3,2},{4,3},{5,4},{6,5},{7,6},{8,15},{9,8},{10,9... | collective-permute-start | bytes 589832 | tf_op jit(solution)/shard_map/ppermute | solution.py:32
  57.2 2.5 %collective-permute-done.12 = bf16[256,384]{1,0:T(8,128)(2,1)S(1)} collective-permute-done((bf16[256,384]{1,0:T(8,128)(2,1)S(1)}, bf16[256,384]{1,0:T(8,128)(2,1)S(1)}, u32[]{:S(2)}, u32[]{:S(2)}) %collective-permute-start.12) | collective-permute-done | bytes 196640 | tf_op jit(solution)/shard_map/ppermute | solution.py:29
  61.6 4.9 %collective-permute-start.2 = (bf16[4,32,1536]{2,1,0:T(8,128)(2,1)S(1)}, bf16[4,32,1536]{2,1,0:T(8,128)(2,1)S(1)}, u32[]{:S(2)}, u32[]{:S(2)}) collective-permute-start(bf16[4,32,1536]{2,1,0:T(8,128)(2,1)S(1)} %collective-permute-done.1), channel_id=1, source_target_pairs={{0,112},{16,0},{32,16},{48,32},{64,48},{80,64},{96,80},{112,96},{1... | collective-permute-start | bytes 1179656 | tf_op jit(solution)/shard_map/ppermute | solution.py:32
  68.5 10.4 %collective-permute-done.5 = bf16[4,32,1536]{2,1,0:T(8,128)(2,1)S(1)} collective-permute-done((bf16[4,32,1536]{2,1,0:T(8,128)(2,1)S(1)}, bf16[4,32,1536]{2,1,0:T(8,128)(2,1)S(1)}, u32[]{:S(2)}, u32[]{:S(2)}) %collective-permute-start.5) | collective-permute-done | bytes 393248 | tf_op jit(solution)/shard_map/ppermute | solution.py:29
  80.8 9.5 %collective-permute-done.6 = bf16[4,32,1536]{2,1,0:T(8,128)(2,1)S(1)} collective-permute-done((bf16[4,32,1536]{2,1,0:T(8,128)(2,1)S(1)}, bf16[4,32,1536]{2,1,0:T(8,128)(2,1)S(1)}, u32[]{:S(2)}, u32[]{:S(2)}) %collective-permute-start.6) | collective-permute-done | bytes 393248 | tf_op jit(solution)/shard_map/ppermute | solution.py:29
  98.7 5.7 %collective-permute-start.17 = (bf16[2,128,384]{2,1,0:T(8,128)(2,1)S(1)}, bf16[2,128,384]{2,1,0:T(8,128)(2,1)S(1)}, u32[]{:S(2)}, u32[]{:S(2)}) collective-permute-start(bf16[2,128,384]{2,1,0:T(8,128)(2,1)S(1)} %get-tuple-element.29), channel_id=1, source_target_pairs={{0,2},{1,3},{2,4},{3,5},{4,6},{5,7},{6,0},{7,1},{8,10},{9,11},{10,... | collective-permute-start | bytes 589832 | tf_op jit(solution)/shard_map/ppermute | solution.py:65
  104.4 1.9 %collective-permute-start.18 = (bf16[2,128,384]{2,1,0:T(8,128)(2,1)S(1)}, bf16[2,128,384]{2,1,0:T(8,128)(2,1)S(1)}, u32[]{:S(2)}, u32[]{:S(2)}) collective-permute-start(bf16[2,128,384]{2,1,0:T(8,128)(2,1)S(1)} %get-tuple-element.28), channel_id=1, source_target_pairs={{0,3},{1,4},{2,5},{3,6},{4,7},{5,0},{6,1},{7,2},{8,11},{9,12},{10,... | collective-permute-start | bytes 589832 | tf_op jit(solution)/shard_map/ppermute | solution.py:65
  106.3 4.7 %collective-permute-start.19 = (bf16[2,128,384]{2,1,0:T(8,128)(2,1)S(1)}, bf16[2,128,384]{2,1,0:T(8,128)(2,1)S(1)}, u32[]{:S(2)}, u32[]{:S(2)}) collective-permute-start(bf16[2,128,384]{2,1,0:T(8,128)(2,1)S(1)} %get-tuple-element.27), channel_id=1, source_target_pairs={{0,4},{1,5},{2,6},{3,7},{4,0},{5,1},{6,2},{7,3},{8,12},{9,13},{10,... | collective-permute-start | bytes 589832 | tf_op jit(solution)/shard_map/ppermute | solution.py:65
  113.6 6.9 %collective-permute-start.20 = (bf16[2,128,384]{2,1,0:T(8,128)(2,1)S(1)}, bf16[2,128,384]{2,1,0:T(8,128)(2,1)S(1)}, u32[]{:S(2)}, u32[]{:S(2)}) collective-permute-start(bf16[2,128,384]{2,1,0:T(8,128)(2,1)S(1)} %get-tuple-element.32), channel_id=1, source_target_pairs={{0,5},{1,6},{2,7},{3,0},{4,1},{5,2},{6,3},{7,4},{8,13},{9,14},{10,... | collective-permute-start | bytes 589832 | tf_op jit(solution)/shard_map/ppermute | solution.py:65
  120.6 2.6 %collective-permute-start.21 = (bf16[2,128,384]{2,1,0:T(8,128)(2,1)S(1)}, bf16[2,128,384]{2,1,0:T(8,128)(2,1)S(1)}, u32[]{:S(2)}, u32[]{:S(2)}) collective-permute-start(bf16[2,128,384]{2,1,0:T(8,128)(2,1)S(1)} %get-tuple-element.31), channel_id=1, source_target_pairs={{0,6},{1,7},{2,0},{3,1},{4,2},{5,3},{6,4},{7,5},{8,14},{9,15},{10,... | collective-permute-start | bytes 589832 | tf_op jit(solution)/shard_map/ppermute | solution.py:65
  123.2 3.7 %collective-permute-done.18 = bf16[2,128,384]{2,1,0:T(8,128)(2,1)S(1)} collective-permute-done((bf16[2,128,384]{2,1,0:T(8,128)(2,1)S(1)}, bf16[2,128,384]{2,1,0:T(8,128)(2,1)S(1)}, u32[]{:S(2)}, u32[]{:S(2)}) %collective-permute-start.18) | collective-permute-done | bytes 196640 | tf_op jit(solution)/shard_map/ppermute | solution.py:65
  126.9 6.1 %collective-permute-start.22 = (bf16[2,128,384]{2,1,0:T(8,128)(2,1)S(1)}, bf16[2,128,384]{2,1,0:T(8,128)(2,1)S(1)}, u32[]{:S(2)}, u32[]{:S(2)}) collective-permute-start(bf16[2,128,384]{2,1,0:T(8,128)(2,1)S(1)} %get-tuple-element.30), channel_id=1, source_target_pairs={{0,7},{1,0},{2,1},{3,2},{4,3},{5,4},{6,5},{7,6},{8,15},{9,8},{10,9... | collective-permute-start | bytes 589832 | tf_op jit(solution)/shard_map/ppermute | solution.py:65
  135.0 2.8 %collective-permute-done.20 = bf16[2,128,384]{2,1,0:T(8,128)(2,1)S(1)} collective-permute-done((bf16[2,128,384]{2,1,0:T(8,128)(2,1)S(1)}, bf16[2,128,384]{2,1,0:T(8,128)(2,1)S(1)}, u32[]{:S(2)}, u32[]{:S(2)}) %collective-permute-start.20) | collective-permute-done | bytes 196640 | tf_op jit(solution)/shard_map/ppermute | solution.py:65
  137.8 4.7 %collective-permute-done.21 = bf16[2,128,384]{2,1,0:T(8,128)(2,1)S(1)} collective-permute-done((bf16[2,128,384]{2,1,0:T(8,128)(2,1)S(1)}, bf16[2,128,384]{2,1,0:T(8,128)(2,1)S(1)}, u32[]{:S(2)}, u32[]{:S(2)}) %collective-permute-start.21) | collective-permute-done | bytes 196640 | tf_op jit(solution)/shard_map/ppermute | solution.py:65
  142.5 4.1 %collective-permute-done.22 = bf16[2,128,384]{2,1,0:T(8,128)(2,1)S(1)} collective-permute-done((bf16[2,128,384]{2,1,0:T(8,128)(2,1)S(1)}, bf16[2,128,384]{2,1,0:T(8,128)(2,1)S(1)}, u32[]{:S(2)}, u32[]{:S(2)}) %collective-permute-start.22) | collective-permute-done | bytes 196640 | tf_op jit(solution)/shard_map/ppermute | solution.py:65
  148.2 2.5 %fusion.5 = bf16[384,1536]{1,0:T(8,128)(2,1)} fusion(f32[384,1536]{1,0:T(8,128)S(1)} %fusion.26, bf16[1024,384]{1,0:T(8,128)(2,1)S(1)} %bitcast.137, bf16[1024,1536]{1,0:T(8,128)(2,1)S(1)} %bitcast.130), kind=kOutput, calls=%fused_computation.13 | convolution fusion | flops 1209139200 | bytes 7471104 | tf_op jit(solution)/shard_map/dot_general | solution.py:79
  (76 shorter events, 29.9 us)
Async XLA Ops:
  0.6 35.3 %collective-permute-start.10 = (bf16[256,384]{1,0:T(8,128)(2,1)}, bf16[256,384]{1,0:T(8,128)(2,1)S(1)}, u32[]{:S(2)}, u32[]{:S(2)}) collective-permute-start(bf16[256,384]{1,0:T(8,128)(2,1)} %param.4), channel_id=1, source_target_pairs={{0,1},{1,2},{2,3},{3,4},{4,5},{5,6},{6,7},{7,0},{8,9},{9,10},{10,1... | collective-permute-start | bytes 589832 | tf_op jit(solution)/shard_map/ppermute | solution.py:29
  18.4 24.6 %collective-permute-start = (bf16[4,32,1536]{2,1,0:T(8,128)(2,1)S(1)}, bf16[4,32,1536]{2,1,0:T(8,128)(2,1)S(1)}, u32[]{:S(2)}, u32[]{:S(2)}) collective-permute-start(bf16[4,32,1536]{2,1,0:T(8,128)(2,1)S(1)} %bitcast.133), channel_id=1, source_target_pairs={{0,112},{16,0},{32,16},{48,32},{64,48},{80,64},{96,80},{112,96},{1... | collective-permute-start | bytes 1179656 | tf_op jit(solution)/shard_map/ppermute | solution.py:32
  23.4 24.8 %collective-permute-start.3 = (bf16[4,32,1536]{2,1,0:T(8,128)(2,1)S(1)}, bf16[4,32,1536]{2,1,0:T(8,128)(2,1)S(1)}, u32[]{:S(2)}, u32[]{:S(2)}) collective-permute-start(bf16[4,32,1536]{2,1,0:T(8,128)(2,1)S(1)} %bitcast.134), channel_id=1, source_target_pairs={{0,16},{16,32},{32,48},{48,64},{64,80},{80,96},{96,112},{112,0},{1... | collective-permute-start | bytes 1179656 | tf_op jit(solution)/shard_map/ppermute | solution.py:29
  25.3 12.5 %collective-permute-start.7 = (bf16[256,384]{1,0:T(8,128)(2,1)}, bf16[256,384]{1,0:T(8,128)(2,1)S(1)}, u32[]{:S(2)}, u32[]{:S(2)}) collective-permute-start(bf16[256,384]{1,0:T(8,128)(2,1)} %param.4), channel_id=1, source_target_pairs={{0,7},{1,0},{2,1},{3,2},{4,3},{5,4},{6,5},{7,6},{8,15},{9,8},{10,9... | collective-permute-start | bytes 589832 | tf_op jit(solution)/shard_map/ppermute | solution.py:32
  33.9 59.9 %collective-permute-start.14 = (bf16[384,1536]{1,0:T(8,128)(2,1)}, bf16[384,1536]{1,0:T(8,128)(2,1)S(1)}, u32[]{:S(2)}, u32[]{:S(2)}) collective-permute-start(bf16[384,1536]{1,0:T(8,128)(2,1)} %param.5), channel_id=1, source_target_pairs={{0,8},{8,0},{1,9},{9,1},{2,10},{10,2},{3,11},{11,3},{4,12},{12,4},... | collective-permute-start | bytes 3538952 | tf_op jit(solution)/shard_map/ppermute | solution.py:46
  35.9 14.2 %collective-permute-start.11 = (bf16[256,384]{1,0:T(8,128)(2,1)S(1)}, bf16[256,384]{1,0:T(8,128)(2,1)S(1)}, u32[]{:S(2)}, u32[]{:S(2)}) collective-permute-start(bf16[256,384]{1,0:T(8,128)(2,1)S(1)} %collective-permute-done.10), channel_id=1, source_target_pairs={{0,1},{1,2},{2,3},{3,4},{4,5},{5,6},{6,7},{7,0},{8,9},{9,10},{10,1... | collective-permute-start | bytes 589832 | tf_op jit(solution)/shard_map/ppermute | solution.py:29
  37.9 14.2 %collective-permute-start.8 = (bf16[256,384]{1,0:T(8,128)(2,1)S(1)}, bf16[256,384]{1,0:T(8,128)(2,1)S(1)}, u32[]{:S(2)}, u32[]{:S(2)}) collective-permute-start(bf16[256,384]{1,0:T(8,128)(2,1)S(1)} %collective-permute-done.7), channel_id=1, source_target_pairs={{0,7},{1,0},{2,1},{3,2},{4,3},{5,4},{6,5},{7,6},{8,15},{9,8},{10,9... | collective-permute-start | bytes 589832 | tf_op jit(solution)/shard_map/ppermute | solution.py:32
  43.0 18.6 %collective-permute-start.1 = (bf16[4,32,1536]{2,1,0:T(8,128)(2,1)S(1)}, bf16[4,32,1536]{2,1,0:T(8,128)(2,1)S(1)}, u32[]{:S(2)}, u32[]{:S(2)}) collective-permute-start(bf16[4,32,1536]{2,1,0:T(8,128)(2,1)S(1)} %collective-permute-done), channel_id=1, source_target_pairs={{0,112},{16,0},{32,16},{48,32},{64,48},{80,64},{96,80},{112,96},{1... | collective-permute-start | bytes 1179656 | tf_op jit(solution)/shard_map/ppermute | solution.py:32
  48.2 18.3 %collective-permute-start.4 = (bf16[4,32,1536]{2,1,0:T(8,128)(2,1)S(1)}, bf16[4,32,1536]{2,1,0:T(8,128)(2,1)S(1)}, u32[]{:S(2)}, u32[]{:S(2)}) collective-permute-start(bf16[4,32,1536]{2,1,0:T(8,128)(2,1)S(1)} %collective-permute-done.3), channel_id=1, source_target_pairs={{0,16},{16,32},{32,48},{48,64},{64,80},{80,96},{96,112},{112,0},{1... | collective-permute-start | bytes 1179656 | tf_op jit(solution)/shard_map/ppermute | solution.py:29
  50.1 9.6 %collective-permute-start.12 = (bf16[256,384]{1,0:T(8,128)(2,1)S(1)}, bf16[256,384]{1,0:T(8,128)(2,1)S(1)}, u32[]{:S(2)}, u32[]{:S(2)}) collective-permute-start(bf16[256,384]{1,0:T(8,128)(2,1)S(1)} %collective-permute-done.11), channel_id=1, source_target_pairs={{0,1},{1,2},{2,3},{3,4},{4,5},{5,6},{6,7},{7,0},{8,9},{9,10},{10,1... | collective-permute-start | bytes 589832 | tf_op jit(solution)/shard_map/ppermute | solution.py:29
  52.1 43.8 %collective-permute-start.9 = (bf16[256,384]{1,0:T(8,128)(2,1)S(1)}, bf16[256,384]{1,0:T(8,128)(2,1)S(1)}, u32[]{:S(2)}, u32[]{:S(2)}) collective-permute-start(bf16[256,384]{1,0:T(8,128)(2,1)S(1)} %collective-permute-done.8), channel_id=1, source_target_pairs={{0,7},{1,0},{2,1},{3,2},{4,3},{5,4},{6,5},{7,6},{8,15},{9,8},{10,9... | collective-permute-start | bytes 589832 | tf_op jit(solution)/shard_map/ppermute | solution.py:32
  59.7 36.2 %collective-permute-start.13 = (bf16[256,384]{1,0:T(8,128)(2,1)S(1)}, bf16[256,384]{1,0:T(8,128)(2,1)S(1)}, u32[]{:S(2)}, u32[]{:S(2)}) collective-permute-start(bf16[256,384]{1,0:T(8,128)(2,1)S(1)} %collective-permute-done.12), channel_id=1, source_target_pairs={{0,1},{1,2},{2,3},{3,4},{4,5},{5,6},{6,7},{7,0},{8,9},{9,10},{10,1... | collective-permute-start | bytes 589832 | tf_op jit(solution)/shard_map/ppermute | solution.py:29
  61.6 19.2 %collective-permute-start.2 = (bf16[4,32,1536]{2,1,0:T(8,128)(2,1)S(1)}, bf16[4,32,1536]{2,1,0:T(8,128)(2,1)S(1)}, u32[]{:S(2)}, u32[]{:S(2)}) collective-permute-start(bf16[4,32,1536]{2,1,0:T(8,128)(2,1)S(1)} %collective-permute-done.1), channel_id=1, source_target_pairs={{0,112},{16,0},{32,16},{48,32},{64,48},{80,64},{96,80},{112,96},{1... | collective-permute-start | bytes 1179656 | tf_op jit(solution)/shard_map/ppermute | solution.py:32
  66.5 12.4 %collective-permute-start.5 = (bf16[4,32,1536]{2,1,0:T(8,128)(2,1)S(1)}, bf16[4,32,1536]{2,1,0:T(8,128)(2,1)S(1)}, u32[]{:S(2)}, u32[]{:S(2)}) collective-permute-start(bf16[4,32,1536]{2,1,0:T(8,128)(2,1)S(1)} %collective-permute-done.4), channel_id=1, source_target_pairs={{0,16},{16,32},{32,48},{48,64},{64,80},{80,96},{96,112},{112,0},{1... | collective-permute-start | bytes 1179656 | tf_op jit(solution)/shard_map/ppermute | solution.py:29
  78.9 11.5 %collective-permute-start.6 = (bf16[4,32,1536]{2,1,0:T(8,128)(2,1)S(1)}, bf16[4,32,1536]{2,1,0:T(8,128)(2,1)S(1)}, u32[]{:S(2)}, u32[]{:S(2)}) collective-permute-start(bf16[4,32,1536]{2,1,0:T(8,128)(2,1)S(1)} %collective-permute-done.5), channel_id=1, source_target_pairs={{0,16},{16,32},{32,48},{48,64},{64,80},{80,96},{96,112},{112,0},{1... | collective-permute-start | bytes 1179656 | tf_op jit(solution)/shard_map/ppermute | solution.py:29
  96.8 16.8 %collective-permute-start.16 = (bf16[2,128,384]{2,1,0:T(8,128)(2,1)S(1)}, bf16[2,128,384]{2,1,0:T(8,128)(2,1)S(1)}, u32[]{:S(2)}, u32[]{:S(2)}) collective-permute-start(bf16[2,128,384]{2,1,0:T(8,128)(2,1)S(1)} %get-tuple-element.26), channel_id=1, source_target_pairs={{0,1},{1,2},{2,3},{3,4},{4,5},{5,6},{6,7},{7,0},{8,9},{9,10},{10,1... | collective-permute-start | bytes 589832 | tf_op jit(solution)/shard_map/ppermute | solution.py:65
  98.7 21.9 %collective-permute-start.17 = (bf16[2,128,384]{2,1,0:T(8,128)(2,1)S(1)}, bf16[2,128,384]{2,1,0:T(8,128)(2,1)S(1)}, u32[]{:S(2)}, u32[]{:S(2)}) collective-permute-start(bf16[2,128,384]{2,1,0:T(8,128)(2,1)S(1)} %get-tuple-element.29), channel_id=1, source_target_pairs={{0,2},{1,3},{2,4},{3,5},{4,6},{5,7},{6,0},{7,1},{8,10},{9,11},{10,... | collective-permute-start | bytes 589832 | tf_op jit(solution)/shard_map/ppermute | solution.py:65
  104.4 22.6 %collective-permute-start.18 = (bf16[2,128,384]{2,1,0:T(8,128)(2,1)S(1)}, bf16[2,128,384]{2,1,0:T(8,128)(2,1)S(1)}, u32[]{:S(2)}, u32[]{:S(2)}) collective-permute-start(bf16[2,128,384]{2,1,0:T(8,128)(2,1)S(1)} %get-tuple-element.28), channel_id=1, source_target_pairs={{0,3},{1,4},{2,5},{3,6},{4,7},{5,0},{6,1},{7,2},{8,11},{9,12},{10,... | collective-permute-start | bytes 589832 | tf_op jit(solution)/shard_map/ppermute | solution.py:65
  106.3 28.7 %collective-permute-start.19 = (bf16[2,128,384]{2,1,0:T(8,128)(2,1)S(1)}, bf16[2,128,384]{2,1,0:T(8,128)(2,1)S(1)}, u32[]{:S(2)}, u32[]{:S(2)}) collective-permute-start(bf16[2,128,384]{2,1,0:T(8,128)(2,1)S(1)} %get-tuple-element.27), channel_id=1, source_target_pairs={{0,4},{1,5},{2,6},{3,7},{4,0},{5,1},{6,2},{7,3},{8,12},{9,13},{10,... | collective-permute-start | bytes 589832 | tf_op jit(solution)/shard_map/ppermute | solution.py:65
  111.0 35.8 %collective-permute-start.15 = (bf16[4,8,32,1536]{3,2,1,0:T(8,128)(2,1)S(1)}, bf16[4,8,32,1536]{3,2,1,0:T(8,128)(2,1)S(1)}, u32[]{:S(2)}, u32[]{:S(2)}) collective-permute-start(bf16[4,8,32,1536]{3,2,1,0:T(8,128)(2,1)S(1)} %constant_dynamic-slice_fusion.2), channel_id=1, source_target_pairs={{0,8},{8,0},{1,9},{9,1},{2,10},{10,2},{3,11},{11,3},{4,12},{12,4},... | collective-permute-start | bytes 9437192 | tf_op jit(solution)/shard_map/ppermute | solution.py:67
  113.6 24.2 %collective-permute-start.20 = (bf16[2,128,384]{2,1,0:T(8,128)(2,1)S(1)}, bf16[2,128,384]{2,1,0:T(8,128)(2,1)S(1)}, u32[]{:S(2)}, u32[]{:S(2)}) collective-permute-start(bf16[2,128,384]{2,1,0:T(8,128)(2,1)S(1)} %get-tuple-element.32), channel_id=1, source_target_pairs={{0,5},{1,6},{2,7},{3,0},{4,1},{5,2},{6,3},{7,4},{8,13},{9,14},{10,... | collective-permute-start | bytes 589832 | tf_op jit(solution)/shard_map/ppermute | solution.py:65
  120.6 21.9 %collective-permute-start.21 = (bf16[2,128,384]{2,1,0:T(8,128)(2,1)S(1)}, bf16[2,128,384]{2,1,0:T(8,128)(2,1)S(1)}, u32[]{:S(2)}, u32[]{:S(2)}) collective-permute-start(bf16[2,128,384]{2,1,0:T(8,128)(2,1)S(1)} %get-tuple-element.31), channel_id=1, source_target_pairs={{0,6},{1,7},{2,0},{3,1},{4,2},{5,3},{6,4},{7,5},{8,14},{9,15},{10,... | collective-permute-start | bytes 589832 | tf_op jit(solution)/shard_map/ppermute | solution.py:65
  126.9 19.7 %collective-permute-start.22 = (bf16[2,128,384]{2,1,0:T(8,128)(2,1)S(1)}, bf16[2,128,384]{2,1,0:T(8,128)(2,1)S(1)}, u32[]{:S(2)}, u32[]{:S(2)}) collective-permute-start(bf16[2,128,384]{2,1,0:T(8,128)(2,1)S(1)} %get-tuple-element.30), channel_id=1, source_target_pairs={{0,7},{1,0},{2,1},{3,2},{4,3},{5,4},{6,5},{7,6},{8,15},{9,8},{10,9... | collective-permute-start | bytes 589832 | tf_op jit(solution)/shard_map/ppermute | solution.py:65
  150.7 3.2 %collective-permute-start.23 = (bf16[128,384]{1,0:T(8,128)(2,1)S(1)}, bf16[128,384]{1,0:T(8,128)(2,1)S(1)}, u32[]{:S(2)}, u32[]{:S(2)}) collective-permute-start(bf16[128,384]{1,0:T(8,128)(2,1)S(1)} %get-tuple-element.38), channel_id=1, source_target_pairs={{0,8},{8,0},{1,9},{9,1},{2,10},{10,2},{3,11},{11,3},{4,12},{12,4},... | collective-permute-start | bytes 294920 | tf_op jit(solution)/shard_map/ppermute | solution.py:85
  (2 other events, 16.4 us)

commit v10 on v8

--- a/solution.py
+++ b/solution.py
@@ -72,14 +72,13 @@
         grad_weight = gw.astype(jnp.bfloat16)
         sub = pre_act.shape[0] // (tok_blk * n_core)
         grad_weight, red = lax.optimization_barrier((grad_weight, red))
-        mine = red[0].reshape(sub, tok_blk, hid)
-        theirs = lax.ppermute(red[1], "rc", shift_pairs(n_core, 1)).reshape(sub, tok_blk, hid)
-        first = jnp.where(rc == 0, mine, theirs)
-        second = jnp.where(rc == 0, theirs, mine)
+        got = lax.ppermute(red, "rc", shift_pairs(n_core, 1))
+        mine = red[0].reshape(sub, 1, tok_blk, hid)
+        theirs = got[1].reshape(sub, 1, tok_blk, hid)
+        slot = lax.broadcasted_iota(jnp.int32, (sub, n_core, tok_blk, hid), 1)
+        gh = jnp.where(slot == rc, mine, theirs).astype(jnp.float32)
         gg = gelu_grad(pre_act.astype(jnp.float32)).reshape(sub, n_core, tok_blk, hid)
-        out0 = first.astype(jnp.float32) * gg[:, 0]
-        out1 = second.astype(jnp.float32) * gg[:, 1]
-        grad_pre = jnp.stack([out0, out1], axis=1).reshape(pre_act.shape).astype(jnp.bfloat16)
+        grad_pre = (gh * gg).reshape(pre_act.shape).astype(jnp.bfloat16)
         return (grad_pre, grad_weight)
 
     return body

time: 137 us -> 136 us (level)
  no operation moved by 1% of the time
where the time goes in v10:
time: 136 us; the launch traced here: 135 us
  waiting for transfers between devices  56.5 us (42%)
  starting transfers between devices  30.2 us (22%)
  blocking collectives  17.9 us (13%)
  between operations  14.4 us (11%)
  matrix products  9.84 us (7%)
  other arithmetic  3.42 us (3%)
  local copies, waits for them, and re-layouts  2.38 us (2%)
    reduce_scatter x1, waiting for transfers between devices, body(): red = lax.psum_scatter(p_both, 'col', scatter_dimension=1, tiled=True)  33 us
    all_gather x1, blocking collectives, body(): abs_x = lax.all_gather(grad_out, 'rx', axis=0, tiled=False)  17.9 us
    ppermute x3, starting transfers between devices, ring_gather(): bwd = lax.ppermute(bwd, axis, [(i, (i - 1) % n) for i in range(n)])  16.7 us
    all_gather x1, waiting for transfers between devices, body(): g_own = lax.all_gather(abs_x, 'ry', axis=1, tiled=False)  12.5 us
    ppermute x4, waiting for transfers between devices, ring_gather(): fwd = lax.ppermute(fwd, axis, [(i, (i + 1) % n) for i in range(n)])  8.55 us
    ppermute x4, starting transfers between devices, ring_gather(): fwd = lax.ppermute(fwd, axis, [(i, (i + 1) % n) for i in range(n)])  7.65 us
    dot_general x1, matrix products, body(): lax.dot_general(go, down_weight, dn2, preferred_element_type=jnp.float32)  4.16 us
  transfers between devices with their start and end apart: 12, of which 7 were waited for; matrix products, arithmetic and copies ran while one was open for 10% of the time, Pallas kernels for 0%

profile of v10, /device:TPU:6, one launch (start us, length us, event | category | flops | bytes accessed | tf_op | source)
XLA Modules:
  0.0 134.7 jit_solution(9836162100826538734)
XLA Ops:
  7.2 17.9 %all-gather = bf16[128,1536]{1,0:T(8,128)(2,1)} all-gather(bf16[32,1536]{1,0:T(8,128)(2,1)} %param.3), channel_id=2, replica_groups=mesh['rx'=4,'ry'=8,'rc'=2,'col'=8] {'rx'}, dimensions={0}, use_global_device_ids=true | all-gather | bytes 491520 | tf_op jit(solution)/shard_map/all_gather | solution.py:47
  25.2 1.9 %collective-permute-start.7 = (bf16[384,1536]{1,0:T(8,128)(2,1)}, bf16[384,1536]{1,0:T(8,128)(2,1)S(1)}, u32[]{:S(2)}, u32[]{:S(2)}) collective-permute-start(bf16[384,1536]{1,0:T(8,128)(2,1)} %param.5), channel_id=1, source_target_pairs={{0,8},{8,0},{1,9},{9,1},{2,10},{10,2},{3,11},{11,3},{4,12},{12,4},... | collective-permute-start | bytes 3538952 | tf_op jit(solution)/shard_map/ppermute | solution.py:46
  27.1 1.9 %collective-permute-start.3 = (bf16[256,384]{1,0:T(8,128)(2,1)}, bf16[256,384]{1,0:T(8,128)(2,1)S(1)}, u32[]{:S(2)}, u32[]{:S(2)}) collective-permute-start(bf16[256,384]{1,0:T(8,128)(2,1)} %param.4), channel_id=1, source_target_pairs={{0,1},{1,2},{2,3},{3,4},{4,5},{5,6},{6,7},{7,0},{8,9},{9,10},{10,1... | collective-permute-start | bytes 589832 | tf_op jit(solution)/shard_map/ppermute | solution.py:29
  29.1 6.5 %collective-permute-start = (bf16[256,384]{1,0:T(8,128)(2,1)}, bf16[256,384]{1,0:T(8,128)(2,1)S(1)}, u32[]{:S(2)}, u32[]{:S(2)}) collective-permute-start(bf16[256,384]{1,0:T(8,128)(2,1)} %param.4), channel_id=1, source_target_pairs={{0,7},{1,0},{2,1},{3,2},{4,3},{5,4},{6,5},{7,6},{8,15},{9,8},{10,9... | collective-permute-start | bytes 589832 | tf_op jit(solution)/shard_map/ppermute | solution.py:32
  35.6 3.8 %collective-permute-done.3 = bf16[256,384]{1,0:T(8,128)(2,1)S(1)} collective-permute-done((bf16[256,384]{1,0:T(8,128)(2,1)}, bf16[256,384]{1,0:T(8,128)(2,1)S(1)}, u32[]{:S(2)}, u32[]{:S(2)}) %collective-permute-start.3) | collective-permute-done | bytes 196640 | tf_op jit(solution)/shard_map/ppermute | solution.py:29
  39.4 1.9 %collective-permute-start.4 = (bf16[256,384]{1,0:T(8,128)(2,1)S(1)}, bf16[256,384]{1,0:T(8,128)(2,1)S(1)}, u32[]{:S(2)}, u32[]{:S(2)}) collective-permute-start(bf16[256,384]{1,0:T(8,128)(2,1)S(1)} %collective-permute-done.3), channel_id=1, source_target_pairs={{0,1},{1,2},{2,3},{3,4},{4,5},{5,6},{6,7},{7,0},{8,9},{9,10},{10,1... | collective-permute-start | bytes 589832 | tf_op jit(solution)/shard_map/ppermute | solution.py:29
  41.3 5.1 %collective-permute-start.1 = (bf16[256,384]{1,0:T(8,128)(2,1)S(1)}, bf16[256,384]{1,0:T(8,128)(2,1)S(1)}, u32[]{:S(2)}, u32[]{:S(2)}) collective-permute-start(bf16[256,384]{1,0:T(8,128)(2,1)S(1)} %collective-permute-done), channel_id=1, source_target_pairs={{0,7},{1,0},{2,1},{3,2},{4,3},{5,4},{6,5},{7,6},{8,15},{9,8},{10,9... | collective-permute-start | bytes 589832 | tf_op jit(solution)/shard_map/ppermute | solution.py:32
  46.5 2.7 %collective-permute-done.4 = bf16[256,384]{1,0:T(8,128)(2,1)S(1)} collective-permute-done((bf16[256,384]{1,0:T(8,128)(2,1)S(1)}, bf16[256,384]{1,0:T(8,128)(2,1)S(1)}, u32[]{:S(2)}, u32[]{:S(2)}) %collective-permute-start.4) | collective-permute-done | bytes 196640 | tf_op jit(solution)/shard_map/ppermute | solution.py:29
  49.2 1.9 %collective-permute-start.5 = (bf16[256,384]{1,0:T(8,128)(2,1)S(1)}, bf16[256,384]{1,0:T(8,128)(2,1)S(1)}, u32[]{:S(2)}, u32[]{:S(2)}) collective-permute-start(bf16[256,384]{1,0:T(8,128)(2,1)S(1)} %collective-permute-done.4), channel_id=1, source_target_pairs={{0,1},{1,2},{2,3},{3,4},{4,5},{5,6},{6,7},{7,0},{8,9},{9,10},{10,1... | collective-permute-start | bytes 589832 | tf_op jit(solution)/shard_map/ppermute | solution.py:29
  51.2 5.1 %collective-permute-start.2 = (bf16[256,384]{1,0:T(8,128)(2,1)S(1)}, bf16[256,384]{1,0:T(8,128)(2,1)S(1)}, u32[]{:S(2)}, u32[]{:S(2)}) collective-permute-start(bf16[256,384]{1,0:T(8,128)(2,1)S(1)} %collective-permute-done.1), channel_id=1, source_target_pairs={{0,7},{1,0},{2,1},{3,2},{4,3},{5,4},{6,5},{7,6},{8,15},{9,8},{10,9... | collective-permute-start | bytes 589832 | tf_op jit(solution)/shard_map/ppermute | solution.py:32
  56.3 2.0 %collective-permute-done.5 = bf16[256,384]{1,0:T(8,128)(2,1)S(1)} collective-permute-done((bf16[256,384]{1,0:T(8,128)(2,1)S(1)}, bf16[256,384]{1,0:T(8,128)(2,1)S(1)}, u32[]{:S(2)}, u32[]{:S(2)}) %collective-permute-start.5) | collective-permute-done | bytes 196640 | tf_op jit(solution)/shard_map/ppermute | solution.py:29
  58.3 1.9 %collective-permute-start.6 = (bf16[256,384]{1,0:T(8,128)(2,1)S(1)}, bf16[256,384]{1,0:T(8,128)(2,1)S(1)}, u32[]{:S(2)}, u32[]{:S(2)}) collective-permute-start(bf16[256,384]{1,0:T(8,128)(2,1)S(1)} %collective-permute-done.5), channel_id=1, source_target_pairs={{0,1},{1,2},{2,3},{3,4},{4,5},{5,6},{6,7},{7,0},{8,9},{9,10},{10,1... | collective-permute-start | bytes 589832 | tf_op jit(solution)/shard_map/ppermute | solution.py:29
  60.2 12.5 %all-gather.4.cloned.1.call-done = bf16[4,256,1536]{2,1,0:T(8,128)(2,1)} async-done(((bf16[4,32,1536]{2,1,0:T(8,128)(2,1)}), bf16[4,256,1536]{2,1,0:T(8,128)(2,1)}) %all-gather.4.cloned.1.call-update) | async-done | bytes 3145744 | tf_op jit(solution)/shard_map/all_gather | solution.py:48
  72.7 4.2 %fusion.6 = bf16[1,1024,384]{2,1,0:T(8,128)(2,1)S(1)} fusion(bf16[1024,1536]{1,0:T(8,128)(2,1)} %bitcast.58, bf16[384,1536]{1,0:T(8,128)(2,1)} %param.5), kind=kOutput, calls=%fused_computation.15 | convolution fusion | flops 1208352768 | bytes 5111808 | tf_op jit(solution)/shard_map/dot_general | solution.py:53
  76.9 1.8 %fusion.7 = bf16[1,1024,384]{2,1,0:T(8,128)(2,1)S(1)} fusion(bf16[1024,1536]{1,0:T(8,128)(2,1)S(1)} %bitcast.60, bf16[384,1536]{1,0:T(8,128)(2,1)S(1)} %collective-permute-done.7), kind=kOutput, calls=%fused_computation.16 | convolution fusion | flops 1208352768 | bytes 5111808 | tf_op jit(solution)/shard_map/dot_general | solution.py:54
  78.7 1.3 pad_maximum_fusion
  80.1 1.9 %collective-permute-start.8 = (bf16[4,8,32,1536]{3,2,1,0:T(8,128)(2,1)}, bf16[4,8,32,1536]{3,2,1,0:T(8,128)(2,1)S(1)}, u32[]{:S(2)}, u32[]{:S(2)}) collective-permute-start(bf16[4,8,32,1536]{3,2,1,0:T(8,128)(2,1)} %bitcast.59), channel_id=1, source_target_pairs={{0,8},{8,0},{1,9},{9,1},{2,10},{10,2},{3,11},{11,3},{4,12},{12,4},... | collective-permute-start | bytes 9437192 | tf_op jit(solution)/shard_map/ppermute | solution.py:58
  82.7 1.1 fusion.1
  84.5 1.4 %fusion.17 = f32[384,1536]{1,0:T(8,128)S(1)} fusion(bf16[1024,384]{1,0:T(8,128)(2,1)S(1)} %bitcast.55, bf16[1024,1536]{1,0:T(8,128)(2,1)S(1)} %bitcast.61), kind=kOutput, calls=%fused_computation.53 | convolution fusion | flops 1207959552 | bytes 6291456 | tf_op jit(solution)/shard_map/dot_general | solution.py:70
  86.0 1.9 %collective-permute-done.8 = bf16[4,8,32,1536]{3,2,1,0:T(8,128)(2,1)S(1)} collective-permute-done((bf16[4,8,32,1536]{3,2,1,0:T(8,128)(2,1)}, bf16[4,8,32,1536]{3,2,1,0:T(8,128)(2,1)S(1)}, u32[]{:S(2)}, u32[]{:S(2)}) %collective-permute-start.8) | collective-permute-done | bytes 3145760 | tf_op jit(solution)/shard_map/ppermute | solution.py:58
  87.9 2.5 %fusion.5 = bf16[384,1536]{1,0:T(8,128)(2,1)} fusion(f32[384,1536]{1,0:T(8,128)S(1)} %fusion.17, bf16[1024,384]{1,0:T(8,128)(2,1)S(1)} %bitcast.53, bf16[1024,1536]{1,0:T(8,128)(2,1)S(1)} %bitcast.52), kind=kOutput, calls=%fused_computation.11 | convolution fusion | flops 1209139200 | bytes 7471104 | tf_op jit(solution)/shard_map/dot_general | solution.py:71
  90.3 33.0 %reduce-scatter.2.cloned.1.call-done = bf16[2,128,384]{2,1,0:T(8,128)(2,1)} async-done(((bf16[2,1024,384]{2,1,0:T(8,128)(2,1)}), bf16[2,128,384]{2,1,0:T(8,128)(2,1)}) %reduce-scatter.2.cloned.1.call-update) | async-done | bytes 196624 | tf_op jit(solution)/shard_map/reduce_scatter | solution.py:57
  123.3 1.9 %collective-permute-start.9 = (bf16[2,128,384]{2,1,0:T(8,128)(2,1)}, bf16[2,128,384]{2,1,0:T(8,128)(2,1)S(1)}, u32[]{:S(2)}, u32[]{:S(2)}) collective-permute-start(bf16[2,128,384]{2,1,0:T(8,128)(2,1)} %reduce-scatter.2.cloned.1.call-done), channel_id=1, source_target_pairs={{0,8},{8,0},{1,9},{9,1},{2,10},{10,2},{3,11},{11,3},{4,12},{12,4},... | collective-permute-start | bytes 589832 | tf_op jit(solution)/shard_map/ppermute | solution.py:75
  126.8 1.0 fusion.15
  (38 shorter events, 3.0 us)
Async XLA Ops:
  7.2 65.5 %all-gather.4.cloned.1.call-start = ((), (), s32[]{:S(2)}) async-start(), calls=%async_computation.2 | async-start | bytes 3538944 | tf_op jit(solution)/shard_map/all_gather | solution.py:48
  25.2 98.1 %reduce-scatter.2.cloned.1.call-start = ((), (), s32[]{:S(2)}) async-start(), calls=%async_computation.1 | async-start | bytes 1769472 | tf_op jit(solution)/shard_map/reduce_scatter | solution.py:57
  25.2 51.7 %collective-permute-start.7 = (bf16[384,1536]{1,0:T(8,128)(2,1)}, bf16[384,1536]{1,0:T(8,128)(2,1)S(1)}, u32[]{:S(2)}, u32[]{:S(2)}) collective-permute-start(bf16[384,1536]{1,0:T(8,128)(2,1)} %param.5), channel_id=1, source_target_pairs={{0,8},{8,0},{1,9},{9,1},{2,10},{10,2},{3,11},{11,3},{4,12},{12,4},... | collective-permute-start | bytes 3538952 | tf_op jit(solution)/shard_map/ppermute | solution.py:46
  27.1 12.2 %collective-permute-start.3 = (bf16[256,384]{1,0:T(8,128)(2,1)}, bf16[256,384]{1,0:T(8,128)(2,1)S(1)}, u32[]{:S(2)}, u32[]{:S(2)}) collective-permute-start(bf16[256,384]{1,0:T(8,128)(2,1)} %param.4), channel_id=1, source_target_pairs={{0,1},{1,2},{2,3},{3,4},{4,5},{5,6},{6,7},{7,0},{8,9},{9,10},{10,1... | collective-permute-start | bytes 589832 | tf_op jit(solution)/shard_map/ppermute | solution.py:29
  29.1 12.2 %collective-permute-start = (bf16[256,384]{1,0:T(8,128)(2,1)}, bf16[256,384]{1,0:T(8,128)(2,1)S(1)}, u32[]{:S(2)}, u32[]{:S(2)}) collective-permute-start(bf16[256,384]{1,0:T(8,128)(2,1)} %param.4), channel_id=1, source_target_pairs={{0,7},{1,0},{2,1},{3,2},{4,3},{5,4},{6,5},{7,6},{8,15},{9,8},{10,9... | collective-permute-start | bytes 589832 | tf_op jit(solution)/shard_map/ppermute | solution.py:32
  39.4 9.8 %collective-permute-start.4 = (bf16[256,384]{1,0:T(8,128)(2,1)S(1)}, bf16[256,384]{1,0:T(8,128)(2,1)S(1)}, u32[]{:S(2)}, u32[]{:S(2)}) collective-permute-start(bf16[256,384]{1,0:T(8,128)(2,1)S(1)} %collective-permute-done.3), channel_id=1, source_target_pairs={{0,1},{1,2},{2,3},{3,4},{4,5},{5,6},{6,7},{7,0},{8,9},{9,10},{10,1... | collective-permute-start | bytes 589832 | tf_op jit(solution)/shard_map/ppermute | solution.py:29
  41.3 9.8 %collective-permute-start.1 = (bf16[256,384]{1,0:T(8,128)(2,1)S(1)}, bf16[256,384]{1,0:T(8,128)(2,1)S(1)}, u32[]{:S(2)}, u32[]{:S(2)}) collective-permute-start(bf16[256,384]{1,0:T(8,128)(2,1)S(1)} %collective-permute-done), channel_id=1, source_target_pairs={{0,7},{1,0},{2,1},{3,2},{4,3},{5,4},{6,5},{7,6},{8,15},{9,8},{10,9... | collective-permute-start | bytes 589832 | tf_op jit(solution)/shard_map/ppermute | solution.py:32
  49.2 9.1 %collective-permute-start.5 = (bf16[256,384]{1,0:T(8,128)(2,1)S(1)}, bf16[256,384]{1,0:T(8,128)(2,1)S(1)}, u32[]{:S(2)}, u32[]{:S(2)}) collective-permute-start(bf16[256,384]{1,0:T(8,128)(2,1)S(1)} %collective-permute-done.4), channel_id=1, source_target_pairs={{0,1},{1,2},{2,3},{3,4},{4,5},{5,6},{6,7},{7,0},{8,9},{9,10},{10,1... | collective-permute-start | bytes 589832 | tf_op jit(solution)/shard_map/ppermute | solution.py:29
  51.2 28.9 %collective-permute-start.2 = (bf16[256,384]{1,0:T(8,128)(2,1)S(1)}, bf16[256,384]{1,0:T(8,128)(2,1)S(1)}, u32[]{:S(2)}, u32[]{:S(2)}) collective-permute-start(bf16[256,384]{1,0:T(8,128)(2,1)S(1)} %collective-permute-done.1), channel_id=1, source_target_pairs={{0,7},{1,0},{2,1},{3,2},{4,3},{5,4},{6,5},{7,6},{8,15},{9,8},{10,9... | collective-permute-start | bytes 589832 | tf_op jit(solution)/shard_map/ppermute | solution.py:32
  58.3 21.8 %collective-permute-start.6 = (bf16[256,384]{1,0:T(8,128)(2,1)S(1)}, bf16[256,384]{1,0:T(8,128)(2,1)S(1)}, u32[]{:S(2)}, u32[]{:S(2)}) collective-permute-start(bf16[256,384]{1,0:T(8,128)(2,1)S(1)} %collective-permute-done.5), channel_id=1, source_target_pairs={{0,1},{1,2},{2,3},{3,4},{4,5},{5,6},{6,7},{7,0},{8,9},{9,10},{10,1... | collective-permute-start | bytes 589832 | tf_op jit(solution)/shard_map/ppermute | solution.py:29
  72.7 4.2 %copy-start.1 = (bf16[4,256,1536]{2,1,0:T(8,128)(2,1)S(1)}, bf16[4,256,1536]{2,1,0:T(8,128)(2,1)}, u32[]{:S(2)}) copy-start(bf16[4,256,1536]{2,1,0:T(8,128)(2,1)} %all-gather.4.cloned.1.call-done) | copy-start | bytes 9437188
  78.7 1.4 %copy-start = (bf16[256,384]{1,0:T(8,128)(2,1)S(1)}, bf16[256,384]{1,0:T(8,128)(2,1)}, u32[]{:S(2)}) copy-start(bf16[256,384]{1,0:T(8,128)(2,1)} %param.4) | copy-start | bytes 589828
  80.1 7.8 %collective-permute-start.8 = (bf16[4,8,32,1536]{3,2,1,0:T(8,128)(2,1)}, bf16[4,8,32,1536]{3,2,1,0:T(8,128)(2,1)S(1)}, u32[]{:S(2)}, u32[]{:S(2)}) collective-permute-start(bf16[4,8,32,1536]{3,2,1,0:T(8,128)(2,1)} %bitcast.59), channel_id=1, source_target_pairs={{0,8},{8,0},{1,9},{9,1},{2,10},{10,2},{3,11},{11,3},{4,12},{12,4},... | collective-permute-start | bytes 9437192 | tf_op jit(solution)/shard_map/ppermute | solution.py:58
  82.7 1.9 %copy-start.2 = (bf16[4,256,1536]{2,1,0:T(8,128)(2,1)S(1)}, bf16[4,256,1536]{2,1,0:T(8,128)(2,1)}, u32[]{:S(2)}) copy-start(bf16[4,256,1536]{2,1,0:T(8,128)(2,1)} %all-gather.4.cloned.1.call-done) | copy-start | bytes 9437188
  123.3 3.5 %collective-permute-start.9 = (bf16[2,128,384]{2,1,0:T(8,128)(2,1)}, bf16[2,128,384]{2,1,0:T(8,128)(2,1)S(1)}, u32[]{:S(2)}, u32[]{:S(2)}) collective-permute-start(bf16[2,128,384]{2,1,0:T(8,128)(2,1)} %reduce-scatter.2.cloned.1.call-done), channel_id=1, source_target_pairs={{0,8},{8,0},{1,9},{9,1},{2,10},{10,2},{3,11},{11,3},{4,12},{12,4},... | collective-permute-start | bytes 589832 | tf_op jit(solution)/shard_map/ppermute | solution.py:75
Sparse Core Ops, SparseCore 0:
  25.3 47.3 all-gather.3
  80.2 43.0 reduce-scatter.1

commit v11 on v10

--- a/solution.py
+++ b/solution.py
@@ -44,17 +44,17 @@
         c = lax.axis_index("col")
         tok_blk, width = grad_out.shape
         w_partner = lax.ppermute(down_weight, "rc", shift_pairs(n_core, 1))
+        w_both = jnp.concatenate([down_weight, w_partner], axis=0)
         abs_x = lax.all_gather(grad_out, "rx", axis=0, tiled=False)
         g_own = lax.all_gather(abs_x, "ry", axis=1, tiled=False)
         rel = ring_gather(pre_act, "col", n_col)
         n_y = g_own.shape[1]
         go = g_own.reshape(-1, width)
         dn2 = (((1,), (1,)), ((), ()))
-        p_mine = lax.dot_general(go, down_weight, dn2, preferred_element_type=jnp.float32)
-        p_part = lax.dot_general(go, w_partner, dn2, preferred_element_type=jnp.float32)
-        p_both = jnp.stack([p_mine, p_part]).astype(jnp.bfloat16)
+        p_both = lax.dot_general(go, w_both, dn2, preferred_element_type=jnp.float32)
+        p_both = p_both.astype(jnp.bfloat16).reshape(go.shape[0], n_core, -1)
         g_late, rel, p_both = lax.optimization_barrier((g_own, rel, p_both))
-        red = lax.psum_scatter(p_both, "col", scatter_dimension=1, tiled=True)
+        red = lax.psum_scatter(p_both, "col", scatter_dimension=0, tiled=True)
         g_other = lax.ppermute(g_late, "rc", shift_pairs(n_core, 1))
         rel = jnp.stack(rel)
         both = jnp.concatenate([rel, rel], axis=0)
@@ -73,8 +73,8 @@
         sub = pre_act.shape[0] // (tok_blk * n_core)
         grad_weight, red = lax.optimization_barrier((grad_weight, red))
         got = lax.ppermute(red, "rc", shift_pairs(n_core, 1))
-        mine = red[0].reshape(sub, 1, tok_blk, hid)
-        theirs = got[1].reshape(sub, 1, tok_blk, hid)
+        mine = red[:, 0].reshape(sub, 1, tok_blk, hid)
+        theirs = got[:, 1].reshape(sub, 1, tok_blk, hid)
         slot = lax.broadcasted_iota(jnp.int32, (sub, n_core, tok_blk, hid), 1)
         gh = jnp.where(slot == rc, mine, theirs).astype(jnp.float32)
         gg = gelu_grad(pre_act.astype(jnp.float32)).reshape(sub, n_core, tok_blk, hid)

time: 136 us -> 136 us (level)
  local copies, waits for them, and re-layouts: 2.38 us -> 3.96 us
    optimization_barrier x0 -> x1, local copies, waits for them, and re-layouts: none -> 1.58 us  [body(): g_late, rel, p_both = lax.optimization_barrier((g_own, rel, p_both))]
    dot_general x2 -> x1, matrix products: 5.96 us -> 5.24 us  [body(): lax.dot_general(go, w_both, dn2, preferred_element_type=jnp.float32)]
  transfers between devices with their start and end apart: 12 -> 12, of which waited for: 7 -> 7; matrix products, arithmetic and copies ran while one was open for 10% -> 9% of each run, Pallas kernels for 0% -> 0%
where the time goes in v11:
time: 136 us; the launch traced here: 134 us
  waiting for transfers between devices  56.4 us (41%)
  starting transfers between devices  30.2 us (22%)
  blocking collectives  17.9 us (13%)
  between operations  14.4 us (11%)
  matrix products  9.09 us (7%)
  local copies, waits for them, and re-layouts  3.96 us (3%)
  other arithmetic  2.09 us (2%)
    reduce_scatter x1, waiting for transfers between devices, body(): red = lax.psum_scatter(p_both, 'col', scatter_dimension=0, tiled=True)  32.9 us
    all_gather x1, blocking collectives, body(): abs_x = lax.all_gather(grad_out, 'rx', axis=0, tiled=False)  17.9 us
    ppermute x3, starting transfers between devices, ring_gather(): bwd = lax.ppermute(bwd, axis, [(i, (i - 1) % n) for i in range(n)])  16.7 us
    all_gather x1, waiting for transfers between devices, body(): g_own = lax.all_gather(abs_x, 'ry', axis=1, tiled=False)  12.5 us
    ppermute x4, waiting for transfers between devices, ring_gather(): fwd = lax.ppermute(fwd, axis, [(i, (i + 1) % n) for i in range(n)])  8.55 us
    ppermute x4, starting transfers between devices, ring_gather(): fwd = lax.ppermute(fwd, axis, [(i, (i + 1) % n) for i in range(n)])  7.65 us
    dot_general x1, matrix products, body(): lax.dot_general(go, w_both, dn2, preferred_element_type=jnp.float32)  5.24 us
  transfers between devices with their start and end apart: 12, of which 7 were waited for; matrix products, arithmetic and copies ran while one was open for 9% of the time, Pallas kernels for 0%

profile of v11, /device:TPU:6, one launch (start us, length us, event | category | flops | bytes accessed | tf_op | source)
XLA Modules:
  0.0 134.1 jit_solution(1755239508681621750)
XLA Ops:
  7.2 17.9 %all-gather = bf16[128,1536]{1,0:T(8,128)(2,1)} all-gather(bf16[32,1536]{1,0:T(8,128)(2,1)} %param.3), channel_id=2, replica_groups=mesh['rx'=4,'ry'=8,'rc'=2,'col'=8] {'rx'}, dimensions={0}, use_global_device_ids=true | all-gather | bytes 491520 | tf_op jit(solution)/shard_map/all_gather | solution.py:48
  25.2 1.9 %collective-permute-start.7 = (bf16[384,1536]{1,0:T(8,128)(2,1)}, bf16[384,1536]{1,0:T(8,128)(2,1)S(1)}, u32[]{:S(2)}, u32[]{:S(2)}) collective-permute-start(bf16[384,1536]{1,0:T(8,128)(2,1)} %param.5), channel_id=1, source_target_pairs={{0,8},{8,0},{1,9},{9,1},{2,10},{10,2},{3,11},{11,3},{4,12},{12,4},... | collective-permute-start | bytes 3538952 | tf_op jit(solution)/shard_map/ppermute | solution.py:46
  27.1 1.9 %collective-permute-start.3 = (bf16[256,384]{1,0:T(8,128)(2,1)}, bf16[256,384]{1,0:T(8,128)(2,1)S(1)}, u32[]{:S(2)}, u32[]{:S(2)}) collective-permute-start(bf16[256,384]{1,0:T(8,128)(2,1)} %param.4), channel_id=1, source_target_pairs={{0,1},{1,2},{2,3},{3,4},{4,5},{5,6},{6,7},{7,0},{8,9},{9,10},{10,1... | collective-permute-start | bytes 589832 | tf_op jit(solution)/shard_map/ppermute | solution.py:29
  29.1 6.5 %collective-permute-start = (bf16[256,384]{1,0:T(8,128)(2,1)}, bf16[256,384]{1,0:T(8,128)(2,1)S(1)}, u32[]{:S(2)}, u32[]{:S(2)}) collective-permute-start(bf16[256,384]{1,0:T(8,128)(2,1)} %param.4), channel_id=1, source_target_pairs={{0,7},{1,0},{2,1},{3,2},{4,3},{5,4},{6,5},{7,6},{8,15},{9,8},{10,9... | collective-permute-start | bytes 589832 | tf_op jit(solution)/shard_map/ppermute | solution.py:32
  35.6 3.8 %collective-permute-done.3 = bf16[256,384]{1,0:T(8,128)(2,1)S(1)} collective-permute-done((bf16[256,384]{1,0:T(8,128)(2,1)}, bf16[256,384]{1,0:T(8,128)(2,1)S(1)}, u32[]{:S(2)}, u32[]{:S(2)}) %collective-permute-start.3) | collective-permute-done | bytes 196640 | tf_op jit(solution)/shard_map/ppermute | solution.py:29
  39.4 1.9 %collective-permute-start.4 = (bf16[256,384]{1,0:T(8,128)(2,1)S(1)}, bf16[256,384]{1,0:T(8,128)(2,1)S(1)}, u32[]{:S(2)}, u32[]{:S(2)}) collective-permute-start(bf16[256,384]{1,0:T(8,128)(2,1)S(1)} %collective-permute-done.3), channel_id=1, source_target_pairs={{0,1},{1,2},{2,3},{3,4},{4,5},{5,6},{6,7},{7,0},{8,9},{9,10},{10,1... | collective-permute-start | bytes 589832 | tf_op jit(solution)/shard_map/ppermute | solution.py:29
  41.3 5.1 %collective-permute-start.1 = (bf16[256,384]{1,0:T(8,128)(2,1)S(1)}, bf16[256,384]{1,0:T(8,128)(2,1)S(1)}, u32[]{:S(2)}, u32[]{:S(2)}) collective-permute-start(bf16[256,384]{1,0:T(8,128)(2,1)S(1)} %collective-permute-done), channel_id=1, source_target_pairs={{0,7},{1,0},{2,1},{3,2},{4,3},{5,4},{6,5},{7,6},{8,15},{9,8},{10,9... | collective-permute-start | bytes 589832 | tf_op jit(solution)/shard_map/ppermute | solution.py:32
  46.5 2.7 %collective-permute-done.4 = bf16[256,384]{1,0:T(8,128)(2,1)S(1)} collective-permute-done((bf16[256,384]{1,0:T(8,128)(2,1)S(1)}, bf16[256,384]{1,0:T(8,128)(2,1)S(1)}, u32[]{:S(2)}, u32[]{:S(2)}) %collective-permute-start.4) | collective-permute-done | bytes 196640 | tf_op jit(solution)/shard_map/ppermute | solution.py:29
  49.2 1.9 %collective-permute-start.5 = (bf16[256,384]{1,0:T(8,128)(2,1)S(1)}, bf16[256,384]{1,0:T(8,128)(2,1)S(1)}, u32[]{:S(2)}, u32[]{:S(2)}) collective-permute-start(bf16[256,384]{1,0:T(8,128)(2,1)S(1)} %collective-permute-done.4), channel_id=1, source_target_pairs={{0,1},{1,2},{2,3},{3,4},{4,5},{5,6},{6,7},{7,0},{8,9},{9,10},{10,1... | collective-permute-start | bytes 589832 | tf_op jit(solution)/shard_map/ppermute | solution.py:29
  51.2 5.1 %collective-permute-start.2 = (bf16[256,384]{1,0:T(8,128)(2,1)S(1)}, bf16[256,384]{1,0:T(8,128)(2,1)S(1)}, u32[]{:S(2)}, u32[]{:S(2)}) collective-permute-start(bf16[256,384]{1,0:T(8,128)(2,1)S(1)} %collective-permute-done.1), channel_id=1, source_target_pairs={{0,7},{1,0},{2,1},{3,2},{4,3},{5,4},{6,5},{7,6},{8,15},{9,8},{10,9... | collective-permute-start | bytes 589832 | tf_op jit(solution)/shard_map/ppermute | solution.py:32
  56.3 2.0 %collective-permute-done.5 = bf16[256,384]{1,0:T(8,128)(2,1)S(1)} collective-permute-done((bf16[256,384]{1,0:T(8,128)(2,1)S(1)}, bf16[256,384]{1,0:T(8,128)(2,1)S(1)}, u32[]{:S(2)}, u32[]{:S(2)}) %collective-permute-start.5) | collective-permute-done | bytes 196640 | tf_op jit(solution)/shard_map/ppermute | solution.py:29
  58.3 1.9 %collective-permute-start.6 = (bf16[256,384]{1,0:T(8,128)(2,1)S(1)}, bf16[256,384]{1,0:T(8,128)(2,1)S(1)}, u32[]{:S(2)}, u32[]{:S(2)}) collective-permute-start(bf16[256,384]{1,0:T(8,128)(2,1)S(1)} %collective-permute-done.5), channel_id=1, source_target_pairs={{0,1},{1,2},{2,3},{3,4},{4,5},{5,6},{6,7},{7,0},{8,9},{9,10},{10,1... | collective-permute-start | bytes 589832 | tf_op jit(solution)/shard_map/ppermute | solution.py:29
  60.2 12.5 %all-gather.4.cloned.1.call-done = bf16[4,256,1536]{2,1,0:T(8,128)(2,1)} async-done(((bf16[4,32,1536]{2,1,0:T(8,128)(2,1)}), bf16[4,256,1536]{2,1,0:T(8,128)(2,1)}) %all-gather.4.cloned.1.call-update) | async-done | bytes 3145744 | tf_op jit(solution)/shard_map/all_gather | solution.py:49
  72.7 5.2 %fusion.10 = bf16[768,1024]{1,0:T(8,128)(2,1)S(1)} fusion(bf16[1024,1536]{1,0:T(8,128)(2,1)} %bitcast.55, bf16[384,1536]{1,0:T(8,128)(2,1)} %copy-done.2, bf16[384,1536]{1,0:T(8,128)(2,1)} %param.5), kind=kOutput, calls=%fused_computation.16 | convolution fusion | flops 2421424128 | bytes 7077888 | tf_op jit(solution)/shard_map/dot_general | solution.py:54
  78.0 1.6 %copy.7 = bf16[1024,2,384]{2,0,1:T(8,128)(2,1)} copy(bf16[1024,2,384]{0,2,1:T(8,128)(2,1)S(1)} %bitcast.50) | data formatting | bytes 3145728 | tf_op jit(solution)/shard_map/optimization_barrier | solution.py:56
  79.6 1.9 %collective-permute-start.8 = (bf16[4,8,32,1536]{3,2,1,0:T(8,128)(2,1)}, bf16[4,8,32,1536]{3,2,1,0:T(8,128)(2,1)S(1)}, u32[]{:S(2)}, u32[]{:S(2)}) collective-permute-start(bf16[4,8,32,1536]{3,2,1,0:T(8,128)(2,1)} %bitcast.56), channel_id=1, source_target_pairs={{0,8},{8,0},{1,9},{9,1},{2,10},{10,2},{3,11},{11,3},{4,12},{12,4},... | collective-permute-start | bytes 9437192 | tf_op jit(solution)/shard_map/ppermute | solution.py:58
  82.2 1.1 fusion.1
  84.1 1.4 %fusion.23 = f32[384,1536]{1,0:T(8,128)S(1)} fusion(bf16[1024,384]{1,0:T(8,128)(2,1)S(1)} %bitcast.52, bf16[1024,1536]{1,0:T(8,128)(2,1)S(1)} %bitcast.57), kind=kOutput, calls=%fused_computation.54 | convolution fusion | flops 1207959552 | bytes 6291456 | tf_op jit(solution)/shard_map/dot_general | solution.py:70
  85.5 1.9 %collective-permute-done.8 = bf16[4,8,32,1536]{3,2,1,0:T(8,128)(2,1)S(1)} collective-permute-done((bf16[4,8,32,1536]{3,2,1,0:T(8,128)(2,1)}, bf16[4,8,32,1536]{3,2,1,0:T(8,128)(2,1)S(1)}, u32[]{:S(2)}, u32[]{:S(2)}) %collective-permute-start.8) | collective-permute-done | bytes 3145760 | tf_op jit(solution)/shard_map/ppermute | solution.py:58
  87.4 2.5 %fusion.5 = bf16[384,1536]{1,0:T(8,128)(2,1)} fusion(f32[384,1536]{1,0:T(8,128)S(1)} %fusion.23, bf16[1024,384]{1,0:T(8,128)(2,1)S(1)} %bitcast.49, bf16[1024,1536]{1,0:T(8,128)(2,1)S(1)} %bitcast.48), kind=kOutput, calls=%fused_computation.11 | convolution fusion | flops 1209139200 | bytes 7471104 | tf_op jit(solution)/shard_map/dot_general | solution.py:71
  89.8 32.9 %reduce-scatter.2.cloned.1.call-done = bf16[128,2,384]{2,0,1:T(8,128)(2,1)} async-done(((bf16[1024,2,384]{2,0,1:T(8,128)(2,1)}), bf16[128,2,384]{2,0,1:T(8,128)(2,1)}) %reduce-scatter.2.cloned.1.call-update) | async-done | bytes 196624 | tf_op jit(solution)/shard_map/reduce_scatter | solution.py:57
  122.7 1.9 %collective-permute-start.9 = (bf16[128,2,384]{2,0,1:T(8,128)(2,1)}, bf16[128,2,384]{2,0,1:T(8,128)(2,1)S(1)}, u32[]{:S(2)}, u32[]{:S(2)}) collective-permute-start(bf16[128,2,384]{2,0,1:T(8,128)(2,1)} %reduce-scatter.2.cloned.1.call-done), channel_id=1, source_target_pairs={{0,8},{8,0},{1,9},{9,1},{2,10},{10,2},{3,11},{11,3},{4,12},{12,4},... | collective-permute-start | bytes 589832 | tf_op jit(solution)/shard_map/ppermute | solution.py:75
  124.8 0.9 slice.6
  126.3 1.0 fusion.20
  (37 shorter events, 2.1 us)
Async XLA Ops:
  7.2 65.5 %all-gather.4.cloned.1.call-start = ((), (), s32[]{:S(2)}) async-start(), calls=%async_computation.2 | async-start | bytes 3538944 | tf_op jit(solution)/shard_map/all_gather | solution.py:49
  25.2 97.5 %reduce-scatter.2.cloned.1.call-start = ((), (), s32[]{:S(2)}) async-start(), calls=%async_computation.1 | async-start | bytes 1769472 | tf_op jit(solution)/shard_map/reduce_scatter | solution.py:57
  25.2 35.0 %collective-permute-start.7 = (bf16[384,1536]{1,0:T(8,128)(2,1)}, bf16[384,1536]{1,0:T(8,128)(2,1)S(1)}, u32[]{:S(2)}, u32[]{:S(2)}) collective-permute-start(bf16[384,1536]{1,0:T(8,128)(2,1)} %param.5), channel_id=1, source_target_pairs={{0,8},{8,0},{1,9},{9,1},{2,10},{10,2},{3,11},{11,3},{4,12},{12,4},... | collective-permute-start | bytes 3538952 | tf_op jit(solution)/shard_map/ppermute | solution.py:46
  27.1 12.2 %collective-permute-start.3 = (bf16[256,384]{1,0:T(8,128)(2,1)}, bf16[256,384]{1,0:T(8,128)(2,1)S(1)}, u32[]{:S(2)}, u32[]{:S(2)}) collective-permute-start(bf16[256,384]{1,0:T(8,128)(2,1)} %param.4), channel_id=1, source_target_pairs={{0,1},{1,2},{2,3},{3,4},{4,5},{5,6},{6,7},{7,0},{8,9},{9,10},{10,1... | collective-permute-start | bytes 589832 | tf_op jit(solution)/shard_map/ppermute | solution.py:29
  29.1 12.2 %collective-permute-start = (bf16[256,384]{1,0:T(8,128)(2,1)}, bf16[256,384]{1,0:T(8,128)(2,1)S(1)}, u32[]{:S(2)}, u32[]{:S(2)}) collective-permute-start(bf16[256,384]{1,0:T(8,128)(2,1)} %param.4), channel_id=1, source_target_pairs={{0,7},{1,0},{2,1},{3,2},{4,3},{5,4},{6,5},{7,6},{8,15},{9,8},{10,9... | collective-permute-start | bytes 589832 | tf_op jit(solution)/shard_map/ppermute | solution.py:32
  39.4 9.8 %collective-permute-start.4 = (bf16[256,384]{1,0:T(8,128)(2,1)S(1)}, bf16[256,384]{1,0:T(8,128)(2,1)S(1)}, u32[]{:S(2)}, u32[]{:S(2)}) collective-permute-start(bf16[256,384]{1,0:T(8,128)(2,1)S(1)} %collective-permute-done.3), channel_id=1, source_target_pairs={{0,1},{1,2},{2,3},{3,4},{4,5},{5,6},{6,7},{7,0},{8,9},{9,10},{10,1... | collective-permute-start | bytes 589832 | tf_op jit(solution)/shard_map/ppermute | solution.py:29
  41.3 9.8 %collective-permute-start.1 = (bf16[256,384]{1,0:T(8,128)(2,1)S(1)}, bf16[256,384]{1,0:T(8,128)(2,1)S(1)}, u32[]{:S(2)}, u32[]{:S(2)}) collective-permute-start(bf16[256,384]{1,0:T(8,128)(2,1)S(1)} %collective-permute-done), channel_id=1, source_target_pairs={{0,7},{1,0},{2,1},{3,2},{4,3},{5,4},{6,5},{7,6},{8,15},{9,8},{10,9... | collective-permute-start | bytes 589832 | tf_op jit(solution)/shard_map/ppermute | solution.py:32
  49.2 9.1 %collective-permute-start.5 = (bf16[256,384]{1,0:T(8,128)(2,1)S(1)}, bf16[256,384]{1,0:T(8,128)(2,1)S(1)}, u32[]{:S(2)}, u32[]{:S(2)}) collective-permute-start(bf16[256,384]{1,0:T(8,128)(2,1)S(1)} %collective-permute-done.4), channel_id=1, source_target_pairs={{0,1},{1,2},{2,3},{3,4},{4,5},{5,6},{6,7},{7,0},{8,9},{9,10},{10,1... | collective-permute-start | bytes 589832 | tf_op jit(solution)/shard_map/ppermute | solution.py:29
  51.2 26.8 %collective-permute-start.2 = (bf16[256,384]{1,0:T(8,128)(2,1)S(1)}, bf16[256,384]{1,0:T(8,128)(2,1)S(1)}, u32[]{:S(2)}, u32[]{:S(2)}) collective-permute-start(bf16[256,384]{1,0:T(8,128)(2,1)S(1)} %collective-permute-done.1), channel_id=1, source_target_pairs={{0,7},{1,0},{2,1},{3,2},{4,3},{5,4},{6,5},{7,6},{8,15},{9,8},{10,9... | collective-permute-start | bytes 589832 | tf_op jit(solution)/shard_map/ppermute | solution.py:32
  58.3 19.7 %collective-permute-start.6 = (bf16[256,384]{1,0:T(8,128)(2,1)S(1)}, bf16[256,384]{1,0:T(8,128)(2,1)S(1)}, u32[]{:S(2)}, u32[]{:S(2)}) collective-permute-start(bf16[256,384]{1,0:T(8,128)(2,1)S(1)} %collective-permute-done.5), channel_id=1, source_target_pairs={{0,1},{1,2},{2,3},{3,4},{4,5},{5,6},{6,7},{7,0},{8,9},{9,10},{10,1... | collective-permute-start | bytes 589832 | tf_op jit(solution)/shard_map/ppermute | solution.py:29
  60.2 12.5 %copy-start.2 = (bf16[384,1536]{1,0:T(8,128)(2,1)}, bf16[384,1536]{1,0:T(8,128)(2,1)S(1)}, u32[]{:S(2)}) copy-start(bf16[384,1536]{1,0:T(8,128)(2,1)S(1)} %collective-permute-done.7) | copy-start | bytes 3538948
  77.9 1.6 %copy-start = (bf16[256,384]{1,0:T(8,128)(2,1)S(1)}, bf16[256,384]{1,0:T(8,128)(2,1)}, u32[]{:S(2)}) copy-start(bf16[256,384]{1,0:T(8,128)(2,1)} %param.4) | copy-start | bytes 589828
  79.6 7.8 %collective-permute-start.8 = (bf16[4,8,32,1536]{3,2,1,0:T(8,128)(2,1)}, bf16[4,8,32,1536]{3,2,1,0:T(8,128)(2,1)S(1)}, u32[]{:S(2)}, u32[]{:S(2)}) collective-permute-start(bf16[4,8,32,1536]{3,2,1,0:T(8,128)(2,1)} %bitcast.56), channel_id=1, source_target_pairs={{0,8},{8,0},{1,9},{9,1},{2,10},{10,2},{3,11},{11,3},{4,12},{12,4},... | collective-permute-start | bytes 9437192 | tf_op jit(solution)/shard_map/ppermute | solution.py:58
  82.2 1.9 %copy-start.1 = (bf16[4,256,1536]{2,1,0:T(8,128)(2,1)S(1)}, bf16[4,256,1536]{2,1,0:T(8,128)(2,1)}, u32[]{:S(2)}) copy-start(bf16[4,256,1536]{2,1,0:T(8,128)(2,1)} %all-gather.4.cloned.1.call-done) | copy-start | bytes 9437188
  122.7 3.5 %collective-permute-start.9 = (bf16[128,2,384]{2,0,1:T(8,128)(2,1)}, bf16[128,2,384]{2,0,1:T(8,128)(2,1)S(1)}, u32[]{:S(2)}, u32[]{:S(2)}) collective-permute-start(bf16[128,2,384]{2,0,1:T(8,128)(2,1)} %reduce-scatter.2.cloned.1.call-done), channel_id=1, source_target_pairs={{0,8},{8,0},{1,9},{9,1},{2,10},{10,2},{3,11},{11,3},{4,12},{12,4},... | collective-permute-start | bytes 589832 | tf_op jit(solution)/shard_map/ppermute | solution.py:75
Sparse Core Ops, SparseCore 0:
  25.3 47.3 all-gather.3
  79.7 42.9 reduce-scatter.1

commit v12 on v11

--- a/solution.py
+++ b/solution.py
@@ -45,7 +45,8 @@
         tok_blk, width = grad_out.shape
         w_partner = lax.ppermute(down_weight, "rc", shift_pairs(n_core, 1))
         w_both = jnp.concatenate([down_weight, w_partner], axis=0)
-        abs_x = lax.all_gather(grad_out, "rx", axis=0, tiled=False)
+        copies = jnp.broadcast_to(grad_out[None], (n_x,) + grad_out.shape)
+        abs_x = lax.all_to_all(copies, "rx", 0, 0, tiled=False)
         g_own = lax.all_gather(abs_x, "ry", axis=1, tiled=False)
         rel = ring_gather(pre_act, "col", n_col)
         n_y = g_own.shape[1]

time: 136 us -> 134 us (0.985)
  blocking collectives: 17.9 us -> 14.2 us
    all_gather x1 -> x0, blocking collectives: 17.9 us -> none  [body(): abs_x = lax.all_gather(grad_out, 'rx', axis=0, tiled=False)]
    all_to_all x0 -> x1, blocking collectives: none -> 14.2 us  [body(): abs_x = lax.all_to_all(copies, 'rx', 0, 0, tiled=False)]
where the time goes in v12:
time: 134 us; the launch traced here: 132 us
  waiting for transfers between devices  56.4 us (42%)
  starting transfers between devices  31.2 us (23%)
  between operations  14.4 us (11%)
  blocking collectives  14.2 us (11%)
  matrix products  9.09 us (7%)
  local copies, waits for them, and re-layouts  4.88 us (4%)
  other arithmetic  2.09 us (2%)
    reduce_scatter x1, waiting for transfers between devices, body(): red = lax.psum_scatter(p_both, 'col', scatter_dimension=0, tiled=True)  32.9 us
    ppermute x3, starting transfers between devices, ring_gather(): bwd = lax.ppermute(bwd, axis, [(i, (i - 1) % n) for i in range(n)])  17.7 us
    all_to_all x1, blocking collectives, body(): abs_x = lax.all_to_all(copies, 'rx', 0, 0, tiled=False)  14.2 us
    all_gather x1, waiting for transfers between devices, body(): g_own = lax.all_gather(abs_x, 'ry', axis=1, tiled=False)  12.5 us
    ppermute x4, waiting for transfers between devices, ring_gather(): fwd = lax.ppermute(fwd, axis, [(i, (i + 1) % n) for i in range(n)])  8.55 us
    ppermute x4, starting transfers between devices, ring_gather(): fwd = lax.ppermute(fwd, axis, [(i, (i + 1) % n) for i in range(n)])  7.65 us
    dot_general x1, matrix products, body(): lax.dot_general(go, w_both, dn2, preferred_element_type=jnp.float32)  5.24 us
  transfers between devices with their start and end apart: 12, of which 7 were waited for; matrix products, arithmetic and copies ran while one was open for 9% of the time, Pallas kernels for 0%

profile of v12, /device:TPU:6, one launch (start us, length us, event | category | flops | bytes accessed | tf_op | source)
XLA Modules:
  0.0 132.2 jit_solution(7848414621550609859)
XLA Ops:
  7.2 0.9 broadcast_in_dim.30
  8.1 14.2 %all_to_all.5 = bf16[4,32,1536]{2,1,0:T(8,128)(2,1)} all-to-all(bf16[4,32,1536]{2,1,0:T(8,128)(2,1)S(1)} %broadcast_in_dim.30), channel_id=1, replica_groups=mesh['rx'=4,'ry'=8,'rc'=2,'col'=8] {'rx'}, dimensions={0} | all-to-all | bytes 786432 | tf_op jit(solution)/shard_map/all_to_all | solution.py:49
  22.4 1.9 %collective-permute-start.7 = (bf16[384,1536]{1,0:T(8,128)(2,1)}, bf16[384,1536]{1,0:T(8,128)(2,1)S(1)}, u32[]{:S(2)}, u32[]{:S(2)}) collective-permute-start(bf16[384,1536]{1,0:T(8,128)(2,1)} %param.5), channel_id=1, source_target_pairs={{0,8},{8,0},{1,9},{9,1},{2,10},{10,2},{3,11},{11,3},{4,12},{12,4},... | collective-permute-start | bytes 3538952 | tf_op jit(solution)/shard_map/ppermute | solution.py:46
  24.4 1.9 %collective-permute-start.3 = (bf16[256,384]{1,0:T(8,128)(2,1)}, bf16[256,384]{1,0:T(8,128)(2,1)S(1)}, u32[]{:S(2)}, u32[]{:S(2)}) collective-permute-start(bf16[256,384]{1,0:T(8,128)(2,1)} %param.4), channel_id=1, source_target_pairs={{0,1},{1,2},{2,3},{3,4},{4,5},{5,6},{6,7},{7,0},{8,9},{9,10},{10,1... | collective-permute-start | bytes 589832 | tf_op jit(solution)/shard_map/ppermute | solution.py:29
  26.3 7.4 %collective-permute-start = (bf16[256,384]{1,0:T(8,128)(2,1)}, bf16[256,384]{1,0:T(8,128)(2,1)S(1)}, u32[]{:S(2)}, u32[]{:S(2)}) collective-permute-start(bf16[256,384]{1,0:T(8,128)(2,1)} %param.4), channel_id=1, source_target_pairs={{0,7},{1,0},{2,1},{3,2},{4,3},{5,4},{6,5},{7,6},{8,15},{9,8},{10,9... | collective-permute-start | bytes 589832 | tf_op jit(solution)/shard_map/ppermute | solution.py:32
  33.7 3.8 %collective-permute-done.3 = bf16[256,384]{1,0:T(8,128)(2,1)S(1)} collective-permute-done((bf16[256,384]{1,0:T(8,128)(2,1)}, bf16[256,384]{1,0:T(8,128)(2,1)S(1)}, u32[]{:S(2)}, u32[]{:S(2)}) %collective-permute-start.3) | collective-permute-done | bytes 196640 | tf_op jit(solution)/shard_map/ppermute | solution.py:29
  37.5 1.9 %collective-permute-start.4 = (bf16[256,384]{1,0:T(8,128)(2,1)S(1)}, bf16[256,384]{1,0:T(8,128)(2,1)S(1)}, u32[]{:S(2)}, u32[]{:S(2)}) collective-permute-start(bf16[256,384]{1,0:T(8,128)(2,1)S(1)} %collective-permute-done.3), channel_id=1, source_target_pairs={{0,1},{1,2},{2,3},{3,4},{4,5},{5,6},{6,7},{7,0},{8,9},{9,10},{10,1... | collective-permute-start | bytes 589832 | tf_op jit(solution)/shard_map/ppermute | solution.py:29
  39.5 5.1 %collective-permute-start.1 = (bf16[256,384]{1,0:T(8,128)(2,1)S(1)}, bf16[256,384]{1,0:T(8,128)(2,1)S(1)}, u32[]{:S(2)}, u32[]{:S(2)}) collective-permute-start(bf16[256,384]{1,0:T(8,128)(2,1)S(1)} %collective-permute-done), channel_id=1, source_target_pairs={{0,7},{1,0},{2,1},{3,2},{4,3},{5,4},{6,5},{7,6},{8,15},{9,8},{10,9... | collective-permute-start | bytes 589832 | tf_op jit(solution)/shard_map/ppermute | solution.py:32
  44.6 2.7 %collective-permute-done.4 = bf16[256,384]{1,0:T(8,128)(2,1)S(1)} collective-permute-done((bf16[256,384]{1,0:T(8,128)(2,1)S(1)}, bf16[256,384]{1,0:T(8,128)(2,1)S(1)}, u32[]{:S(2)}, u32[]{:S(2)}) %collective-permute-start.4) | collective-permute-done | bytes 196640 | tf_op jit(solution)/shard_map/ppermute | solution.py:29
  47.4 1.9 %collective-permute-start.5 = (bf16[256,384]{1,0:T(8,128)(2,1)S(1)}, bf16[256,384]{1,0:T(8,128)(2,1)S(1)}, u32[]{:S(2)}, u32[]{:S(2)}) collective-permute-start(bf16[256,384]{1,0:T(8,128)(2,1)S(1)} %collective-permute-done.4), channel_id=1, source_target_pairs={{0,1},{1,2},{2,3},{3,4},{4,5},{5,6},{6,7},{7,0},{8,9},{9,10},{10,1... | collective-permute-start | bytes 589832 | tf_op jit(solution)/shard_map/ppermute | solution.py:29
  49.3 5.1 %collective-permute-start.2 = (bf16[256,384]{1,0:T(8,128)(2,1)S(1)}, bf16[256,384]{1,0:T(8,128)(2,1)S(1)}, u32[]{:S(2)}, u32[]{:S(2)}) collective-permute-start(bf16[256,384]{1,0:T(8,128)(2,1)S(1)} %collective-permute-done.1), channel_id=1, source_target_pairs={{0,7},{1,0},{2,1},{3,2},{4,3},{5,4},{6,5},{7,6},{8,15},{9,8},{10,9... | collective-permute-start | bytes 589832 | tf_op jit(solution)/shard_map/ppermute | solution.py:32
  54.5 2.0 %collective-permute-done.5 = bf16[256,384]{1,0:T(8,128)(2,1)S(1)} collective-permute-done((bf16[256,384]{1,0:T(8,128)(2,1)S(1)}, bf16[256,384]{1,0:T(8,128)(2,1)S(1)}, u32[]{:S(2)}, u32[]{:S(2)}) %collective-permute-start.5) | collective-permute-done | bytes 196640 | tf_op jit(solution)/shard_map/ppermute | solution.py:29
  56.4 1.9 %collective-permute-start.6 = (bf16[256,384]{1,0:T(8,128)(2,1)S(1)}, bf16[256,384]{1,0:T(8,128)(2,1)S(1)}, u32[]{:S(2)}, u32[]{:S(2)}) collective-permute-start(bf16[256,384]{1,0:T(8,128)(2,1)S(1)} %collective-permute-done.5), channel_id=1, source_target_pairs={{0,1},{1,2},{2,3},{3,4},{4,5},{5,6},{6,7},{7,0},{8,9},{9,10},{10,1... | collective-permute-start | bytes 589832 | tf_op jit(solution)/shard_map/ppermute | solution.py:29
  58.4 12.5 %all-gather.3.cloned.1.call-done = bf16[4,256,1536]{2,1,0:T(8,128)(2,1)} async-done(((bf16[4,32,1536]{2,1,0:T(8,128)(2,1)}), bf16[4,256,1536]{2,1,0:T(8,128)(2,1)}) %all-gather.3.cloned.1.call-update) | async-done | bytes 3145744 | tf_op jit(solution)/shard_map/all_gather | solution.py:50
  70.8 5.2 %fusion.10 = bf16[768,1024]{1,0:T(8,128)(2,1)S(1)} fusion(bf16[1024,1536]{1,0:T(8,128)(2,1)} %bitcast.53, bf16[384,1536]{1,0:T(8,128)(2,1)} %copy-done.2, bf16[384,1536]{1,0:T(8,128)(2,1)} %param.5), kind=kOutput, calls=%fused_computation.16 | convolution fusion | flops 2421424128 | bytes 7077888 | tf_op jit(solution)/shard_map/dot_general | solution.py:55
  76.1 1.6 %copy.7 = bf16[1024,2,384]{2,0,1:T(8,128)(2,1)} copy(bf16[1024,2,384]{0,2,1:T(8,128)(2,1)S(1)} %bitcast.49) | data formatting | bytes 3145728 | tf_op jit(solution)/shard_map/optimization_barrier | solution.py:57
  77.8 1.9 %collective-permute-start.8 = (bf16[4,8,32,1536]{3,2,1,0:T(8,128)(2,1)}, bf16[4,8,32,1536]{3,2,1,0:T(8,128)(2,1)S(1)}, u32[]{:S(2)}, u32[]{:S(2)}) collective-permute-start(bf16[4,8,32,1536]{3,2,1,0:T(8,128)(2,1)} %bitcast.54), channel_id=1, source_target_pairs={{0,8},{8,0},{1,9},{9,1},{2,10},{10,2},{3,11},{11,3},{4,12},{12,4},... | collective-permute-start | bytes 9437192 | tf_op jit(solution)/shard_map/ppermute | solution.py:59
  80.3 1.1 fusion.1
  82.2 1.4 %fusion.23 = f32[384,1536]{1,0:T(8,128)S(1)} fusion(bf16[1024,384]{1,0:T(8,128)(2,1)S(1)} %bitcast.50, bf16[1024,1536]{1,0:T(8,128)(2,1)S(1)} %bitcast.55), kind=kOutput, calls=%fused_computation.54 | convolution fusion | flops 1207959552 | bytes 6291456 | tf_op jit(solution)/shard_map/dot_general | solution.py:71
  83.6 1.9 %collective-permute-done.8 = bf16[4,8,32,1536]{3,2,1,0:T(8,128)(2,1)S(1)} collective-permute-done((bf16[4,8,32,1536]{3,2,1,0:T(8,128)(2,1)}, bf16[4,8,32,1536]{3,2,1,0:T(8,128)(2,1)S(1)}, u32[]{:S(2)}, u32[]{:S(2)}) %collective-permute-start.8) | collective-permute-done | bytes 3145760 | tf_op jit(solution)/shard_map/ppermute | solution.py:59
  85.5 2.5 %fusion.5 = bf16[384,1536]{1,0:T(8,128)(2,1)} fusion(f32[384,1536]{1,0:T(8,128)S(1)} %fusion.23, bf16[1024,384]{1,0:T(8,128)(2,1)S(1)} %bitcast.48, bf16[1024,1536]{1,0:T(8,128)(2,1)S(1)} %bitcast.47), kind=kOutput, calls=%fused_computation.11 | convolution fusion | flops 1209139200 | bytes 7471104 | tf_op jit(solution)/shard_map/dot_general | solution.py:72
  88.0 32.9 %reduce-scatter.2.cloned.1.call-done = bf16[128,2,384]{2,0,1:T(8,128)(2,1)} async-done(((bf16[1024,2,384]{2,0,1:T(8,128)(2,1)}), bf16[128,2,384]{2,0,1:T(8,128)(2,1)}) %reduce-scatter.2.cloned.1.call-update) | async-done | bytes 196624 | tf_op jit(solution)/shard_map/reduce_scatter | solution.py:58
  120.9 1.9 %collective-permute-start.9 = (bf16[128,2,384]{2,0,1:T(8,128)(2,1)}, bf16[128,2,384]{2,0,1:T(8,128)(2,1)S(1)}, u32[]{:S(2)}, u32[]{:S(2)}) collective-permute-start(bf16[128,2,384]{2,0,1:T(8,128)(2,1)} %reduce-scatter.2.cloned.1.call-done), channel_id=1, source_target_pairs={{0,8},{8,0},{1,9},{9,1},{2,10},{10,2},{3,11},{11,3},{4,12},{12,4},... | collective-permute-start | bytes 589832 | tf_op jit(solution)/shard_map/ppermute | solution.py:76
  124.4 1.0 fusion.20
  (38 shorter events, 3.0 us)
Async XLA Ops:
  7.2 63.7 %all-gather.3.cloned.1.call-start = ((), (), s32[]{:S(2)}) async-start(), calls=%async_computation.3 | async-start | bytes 3538944 | tf_op jit(solution)/shard_map/all_gather | solution.py:50
  22.4 98.5 %reduce-scatter.2.cloned.1.call-start = ((), (), s32[]{:S(2)}) async-start(), calls=%async_computation.2 | async-start | bytes 1769472 | tf_op jit(solution)/shard_map/reduce_scatter | solution.py:58
  22.4 35.9 %collective-permute-start.7 = (bf16[384,1536]{1,0:T(8,128)(2,1)}, bf16[384,1536]{1,0:T(8,128)(2,1)S(1)}, u32[]{:S(2)}, u32[]{:S(2)}) collective-permute-start(bf16[384,1536]{1,0:T(8,128)(2,1)} %param.5), channel_id=1, source_target_pairs={{0,8},{8,0},{1,9},{9,1},{2,10},{10,2},{3,11},{11,3},{4,12},{12,4},... | collective-permute-start | bytes 3538952 | tf_op jit(solution)/shard_map/ppermute | solution.py:46
  24.4 13.2 %collective-permute-start.3 = (bf16[256,384]{1,0:T(8,128)(2,1)}, bf16[256,384]{1,0:T(8,128)(2,1)S(1)}, u32[]{:S(2)}, u32[]{:S(2)}) collective-permute-start(bf16[256,384]{1,0:T(8,128)(2,1)} %param.4), channel_id=1, source_target_pairs={{0,1},{1,2},{2,3},{3,4},{4,5},{5,6},{6,7},{7,0},{8,9},{9,10},{10,1... | collective-permute-start | bytes 589832 | tf_op jit(solution)/shard_map/ppermute | solution.py:29
  26.3 13.2 %collective-permute-start = (bf16[256,384]{1,0:T(8,128)(2,1)}, bf16[256,384]{1,0:T(8,128)(2,1)S(1)}, u32[]{:S(2)}, u32[]{:S(2)}) collective-permute-start(bf16[256,384]{1,0:T(8,128)(2,1)} %param.4), channel_id=1, source_target_pairs={{0,7},{1,0},{2,1},{3,2},{4,3},{5,4},{6,5},{7,6},{8,15},{9,8},{10,9... | collective-permute-start | bytes 589832 | tf_op jit(solution)/shard_map/ppermute | solution.py:32
  37.5 9.8 %collective-permute-start.4 = (bf16[256,384]{1,0:T(8,128)(2,1)S(1)}, bf16[256,384]{1,0:T(8,128)(2,1)S(1)}, u32[]{:S(2)}, u32[]{:S(2)}) collective-permute-start(bf16[256,384]{1,0:T(8,128)(2,1)S(1)} %collective-permute-done.3), channel_id=1, source_target_pairs={{0,1},{1,2},{2,3},{3,4},{4,5},{5,6},{6,7},{7,0},{8,9},{9,10},{10,1... | collective-permute-start | bytes 589832 | tf_op jit(solution)/shard_map/ppermute | solution.py:29
  39.5 9.8 %collective-permute-start.1 = (bf16[256,384]{1,0:T(8,128)(2,1)S(1)}, bf16[256,384]{1,0:T(8,128)(2,1)S(1)}, u32[]{:S(2)}, u32[]{:S(2)}) collective-permute-start(bf16[256,384]{1,0:T(8,128)(2,1)S(1)} %collective-permute-done), channel_id=1, source_target_pairs={{0,7},{1,0},{2,1},{3,2},{4,3},{5,4},{6,5},{7,6},{8,15},{9,8},{10,9... | collective-permute-start | bytes 589832 | tf_op jit(solution)/shard_map/ppermute | solution.py:32
  47.4 9.1 %collective-permute-start.5 = (bf16[256,384]{1,0:T(8,128)(2,1)S(1)}, bf16[256,384]{1,0:T(8,128)(2,1)S(1)}, u32[]{:S(2)}, u32[]{:S(2)}) collective-permute-start(bf16[256,384]{1,0:T(8,128)(2,1)S(1)} %collective-permute-done.4), channel_id=1, source_target_pairs={{0,1},{1,2},{2,3},{3,4},{4,5},{5,6},{6,7},{7,0},{8,9},{9,10},{10,1... | collective-permute-start | bytes 589832 | tf_op jit(solution)/shard_map/ppermute | solution.py:29
  49.3 26.8 %collective-permute-start.2 = (bf16[256,384]{1,0:T(8,128)(2,1)S(1)}, bf16[256,384]{1,0:T(8,128)(2,1)S(1)}, u32[]{:S(2)}, u32[]{:S(2)}) collective-permute-start(bf16[256,384]{1,0:T(8,128)(2,1)S(1)} %collective-permute-done.1), channel_id=1, source_target_pairs={{0,7},{1,0},{2,1},{3,2},{4,3},{5,4},{6,5},{7,6},{8,15},{9,8},{10,9... | collective-permute-start | bytes 589832 | tf_op jit(solution)/shard_map/ppermute | solution.py:32
  56.4 19.7 %collective-permute-start.6 = (bf16[256,384]{1,0:T(8,128)(2,1)S(1)}, bf16[256,384]{1,0:T(8,128)(2,1)S(1)}, u32[]{:S(2)}, u32[]{:S(2)}) collective-permute-start(bf16[256,384]{1,0:T(8,128)(2,1)S(1)} %collective-permute-done.5), channel_id=1, source_target_pairs={{0,1},{1,2},{2,3},{3,4},{4,5},{5,6},{6,7},{7,0},{8,9},{9,10},{10,1... | collective-permute-start | bytes 589832 | tf_op jit(solution)/shard_map/ppermute | solution.py:29
  58.3 12.5 %copy-start.2 = (bf16[384,1536]{1,0:T(8,128)(2,1)}, bf16[384,1536]{1,0:T(8,128)(2,1)S(1)}, u32[]{:S(2)}) copy-start(bf16[384,1536]{1,0:T(8,128)(2,1)S(1)} %collective-permute-done.7) | copy-start | bytes 3538948
  76.1 1.6 %copy-start = (bf16[256,384]{1,0:T(8,128)(2,1)S(1)}, bf16[256,384]{1,0:T(8,128)(2,1)}, u32[]{:S(2)}) copy-start(bf16[256,384]{1,0:T(8,128)(2,1)} %param.4) | copy-start | bytes 589828
  77.8 7.8 %collective-permute-start.8 = (bf16[4,8,32,1536]{3,2,1,0:T(8,128)(2,1)}, bf16[4,8,32,1536]{3,2,1,0:T(8,128)(2,1)S(1)}, u32[]{:S(2)}, u32[]{:S(2)}) collective-permute-start(bf16[4,8,32,1536]{3,2,1,0:T(8,128)(2,1)} %bitcast.54), channel_id=1, source_target_pairs={{0,8},{8,0},{1,9},{9,1},{2,10},{10,2},{3,11},{11,3},{4,12},{12,4},... | collective-permute-start | bytes 9437192 | tf_op jit(solution)/shard_map/ppermute | solution.py:59
  80.3 1.9 %copy-start.1 = (bf16[4,256,1536]{2,1,0:T(8,128)(2,1)S(1)}, bf16[4,256,1536]{2,1,0:T(8,128)(2,1)}, u32[]{:S(2)}) copy-start(bf16[4,256,1536]{2,1,0:T(8,128)(2,1)} %all-gather.3.cloned.1.call-done) | copy-start | bytes 9437188
  120.9 3.5 %collective-permute-start.9 = (bf16[128,2,384]{2,0,1:T(8,128)(2,1)}, bf16[128,2,384]{2,0,1:T(8,128)(2,1)S(1)}, u32[]{:S(2)}, u32[]{:S(2)}) collective-permute-start(bf16[128,2,384]{2,0,1:T(8,128)(2,1)} %reduce-scatter.2.cloned.1.call-done), channel_id=1, source_target_pairs={{0,8},{8,0},{1,9},{9,1},{2,10},{10,2},{3,11},{11,3},{4,12},{12,4},... | collective-permute-start | bytes 589832 | tf_op jit(solution)/shard_map/ppermute | solution.py:76
Sparse Core Ops, SparseCore 0:
  22.5 48.2 all-gather.2
  77.8 42.9 reduce-scatter.1

commit v13 on v12

--- a/solution.py
+++ b/solution.py
@@ -73,11 +73,9 @@
         grad_weight = gw.astype(jnp.bfloat16)
         sub = pre_act.shape[0] // (tok_blk * n_core)
         grad_weight, red = lax.optimization_barrier((grad_weight, red))
-        got = lax.ppermute(red, "rc", shift_pairs(n_core, 1))
-        mine = red[:, 0].reshape(sub, 1, tok_blk, hid)
-        theirs = got[:, 1].reshape(sub, 1, tok_blk, hid)
-        slot = lax.broadcasted_iota(jnp.int32, (sub, n_core, tok_blk, hid), 1)
-        gh = jnp.where(slot == rc, mine, theirs).astype(jnp.float32)
+        send = jnp.where(rc == 0, jnp.stack([red[:, 0], red[:, 1]]), jnp.stack([red[:, 1], red[:, 0]]))
+        recv = lax.all_to_all(send, "rc", 0, 0, tiled=False)
+        gh = jnp.transpose(recv.reshape(n_core, sub, tok_blk, hid), (1, 0, 2, 3)).astype(jnp.float32)
         gg = gelu_grad(pre_act.astype(jnp.float32)).reshape(sub, n_core, tok_blk, hid)
         grad_pre = (gh * gg).reshape(pre_act.shape).astype(jnp.bfloat16)
         return (grad_pre, grad_weight)

time: 134 us -> 135 us (level)
  blocking collectives: 14.2 us -> 18.1 us
  starting transfers between devices: 31.2 us -> 29.2 us
  waiting for transfers between devices: 56.4 us -> 54.7 us
    all_to_all x0 -> x1, blocking collectives: none -> 3.89 us  [body(): recv = lax.all_to_all(send, 'rc', 0, 0, tiled=False)]
    ppermute x1 -> x0, starting transfers between devices: 1.91 us -> none  [body(): got = lax.ppermute(red, 'rc', shift_pairs(n_core, 1))]
  transfers between devices with their start and end apart: 12 -> 11, of which waited for: 7 -> 6; matrix products, arithmetic and copies ran while one was open for 9% -> 9% of each run, Pallas kernels for 0% -> 0%
where the time goes in v13:
time: 135 us; the launch traced here: 133 us
  waiting for transfers between devices  54.7 us (41%)
  starting transfers between devices  29.2 us (22%)
  blocking collectives  18.1 us (13%)
  between operations  14.4 us (11%)
  matrix products  9.11 us (7%)
  local copies, waits for them, and re-layouts  5.46 us (4%)
  other arithmetic  2.35 us (2%)
    reduce_scatter x1, waiting for transfers between devices, body(): red = lax.psum_scatter(p_both, 'col', scatter_dimension=0, tiled=True)  32.9 us
    ppermute x3, starting transfers between devices, ring_gather(): bwd = lax.ppermute(bwd, axis, [(i, (i - 1) % n) for i in range(n)])  17.7 us
    all_to_all x1, blocking collectives, body(): abs_x = lax.all_to_all(copies, 'rx', 0, 0, tiled=False)  14.2 us
    all_gather x1, waiting for transfers between devices, body(): g_own = lax.all_gather(abs_x, 'ry', axis=1, tiled=False)  12.5 us
    ppermute x4, starting transfers between devices, ring_gather(): fwd = lax.ppermute(fwd, axis, [(i, (i + 1) % n) for i in range(n)])  7.65 us
    ppermute x4, waiting for transfers between devices, ring_gather(): fwd = lax.ppermute(fwd, axis, [(i, (i + 1) % n) for i in range(n)])  7.37 us
    dot_general x1, matrix products, body(): lax.dot_general(go, w_both, dn2, preferred_element_type=jnp.float32)  5.24 us
    all_to_all x1, blocking collectives, body(): recv = lax.all_to_all(send, 'rc', 0, 0, tiled=False)  3.89 us
  transfers between devices with their start and end apart: 11, of which 6 were waited for; matrix products, arithmetic and copies ran while one was open for 9% of the time, Pallas kernels for 0%

profile of v13, /device:TPU:6, one launch (start us, length us, event | category | flops | bytes accessed | tf_op | source)
XLA Modules:
  0.0 133.3 jit_solution(17438560977016691818)
XLA Ops:
  7.2 0.9 broadcast_in_dim.2
  8.1 14.2 %all_to_all.10 = bf16[4,32,1536]{2,1,0:T(8,128)(2,1)} all-to-all(bf16[4,32,1536]{2,1,0:T(8,128)(2,1)S(1)} %broadcast_in_dim.2), channel_id=1, replica_groups=mesh['rx'=4,'ry'=8,'rc'=2,'col'=8] {'rx'}, dimensions={0} | all-to-all | bytes 786432 | tf_op jit(solution)/shard_map/all_to_all | solution.py:49
  22.4 1.9 %collective-permute-start.7 = (bf16[384,1536]{1,0:T(8,128)(2,1)}, bf16[384,1536]{1,0:T(8,128)(2,1)S(1)}, u32[]{:S(2)}, u32[]{:S(2)}) collective-permute-start(bf16[384,1536]{1,0:T(8,128)(2,1)} %param.5), channel_id=1, source_target_pairs={{0,8},{8,0},{1,9},{9,1},{2,10},{10,2},{3,11},{11,3},{4,12},{12,4},... | collective-permute-start | bytes 3538952 | tf_op jit(solution)/shard_map/ppermute | solution.py:46
  24.4 1.9 %collective-permute-start.3 = (bf16[256,384]{1,0:T(8,128)(2,1)}, bf16[256,384]{1,0:T(8,128)(2,1)S(1)}, u32[]{:S(2)}, u32[]{:S(2)}) collective-permute-start(bf16[256,384]{1,0:T(8,128)(2,1)} %param.4), channel_id=1, source_target_pairs={{0,1},{1,2},{2,3},{3,4},{4,5},{5,6},{6,7},{7,0},{8,9},{9,10},{10,1... | collective-permute-start | bytes 589832 | tf_op jit(solution)/shard_map/ppermute | solution.py:29
  26.3 7.4 %collective-permute-start = (bf16[256,384]{1,0:T(8,128)(2,1)}, bf16[256,384]{1,0:T(8,128)(2,1)S(1)}, u32[]{:S(2)}, u32[]{:S(2)}) collective-permute-start(bf16[256,384]{1,0:T(8,128)(2,1)} %param.4), channel_id=1, source_target_pairs={{0,7},{1,0},{2,1},{3,2},{4,3},{5,4},{6,5},{7,6},{8,15},{9,8},{10,9... | collective-permute-start | bytes 589832 | tf_op jit(solution)/shard_map/ppermute | solution.py:32
  33.7 3.8 %collective-permute-done.3 = bf16[256,384]{1,0:T(8,128)(2,1)S(1)} collective-permute-done((bf16[256,384]{1,0:T(8,128)(2,1)}, bf16[256,384]{1,0:T(8,128)(2,1)S(1)}, u32[]{:S(2)}, u32[]{:S(2)}) %collective-permute-start.3) | collective-permute-done | bytes 196640 | tf_op jit(solution)/shard_map/ppermute | solution.py:29
  37.5 1.9 %collective-permute-start.4 = (bf16[256,384]{1,0:T(8,128)(2,1)S(1)}, bf16[256,384]{1,0:T(8,128)(2,1)S(1)}, u32[]{:S(2)}, u32[]{:S(2)}) collective-permute-start(bf16[256,384]{1,0:T(8,128)(2,1)S(1)} %collective-permute-done.3), channel_id=1, source_target_pairs={{0,1},{1,2},{2,3},{3,4},{4,5},{5,6},{6,7},{7,0},{8,9},{9,10},{10,1... | collective-permute-start | bytes 589832 | tf_op jit(solution)/shard_map/ppermute | solution.py:29
  39.5 5.1 %collective-permute-start.1 = (bf16[256,384]{1,0:T(8,128)(2,1)S(1)}, bf16[256,384]{1,0:T(8,128)(2,1)S(1)}, u32[]{:S(2)}, u32[]{:S(2)}) collective-permute-start(bf16[256,384]{1,0:T(8,128)(2,1)S(1)} %collective-permute-done), channel_id=1, source_target_pairs={{0,7},{1,0},{2,1},{3,2},{4,3},{5,4},{6,5},{7,6},{8,15},{9,8},{10,9... | collective-permute-start | bytes 589832 | tf_op jit(solution)/shard_map/ppermute | solution.py:32
  44.6 2.7 %collective-permute-done.4 = bf16[256,384]{1,0:T(8,128)(2,1)S(1)} collective-permute-done((bf16[256,384]{1,0:T(8,128)(2,1)S(1)}, bf16[256,384]{1,0:T(8,128)(2,1)S(1)}, u32[]{:S(2)}, u32[]{:S(2)}) %collective-permute-start.4) | collective-permute-done | bytes 196640 | tf_op jit(solution)/shard_map/ppermute | solution.py:29
  47.4 1.9 %collective-permute-start.5 = (bf16[256,384]{1,0:T(8,128)(2,1)S(1)}, bf16[256,384]{1,0:T(8,128)(2,1)S(1)}, u32[]{:S(2)}, u32[]{:S(2)}) collective-permute-start(bf16[256,384]{1,0:T(8,128)(2,1)S(1)} %collective-permute-done.4), channel_id=1, source_target_pairs={{0,1},{1,2},{2,3},{3,4},{4,5},{5,6},{6,7},{7,0},{8,9},{9,10},{10,1... | collective-permute-start | bytes 589832 | tf_op jit(solution)/shard_map/ppermute | solution.py:29
  49.3 1.2 fusion.18
  50.5 5.1 %collective-permute-start.2 = (bf16[256,384]{1,0:T(8,128)(2,1)S(1)}, bf16[256,384]{1,0:T(8,128)(2,1)S(1)}, u32[]{:S(2)}, u32[]{:S(2)}) collective-permute-start(bf16[256,384]{1,0:T(8,128)(2,1)S(1)} %collective-permute-done.1), channel_id=1, source_target_pairs={{0,7},{1,0},{2,1},{3,2},{4,3},{5,4},{6,5},{7,6},{8,15},{9,8},{10,9... | collective-permute-start | bytes 589832 | tf_op jit(solution)/shard_map/ppermute | solution.py:32
  56.4 1.9 %collective-permute-start.6 = (bf16[256,384]{1,0:T(8,128)(2,1)S(1)}, bf16[256,384]{1,0:T(8,128)(2,1)S(1)}, u32[]{:S(2)}, u32[]{:S(2)}) collective-permute-start(bf16[256,384]{1,0:T(8,128)(2,1)S(1)} %collective-permute-done.5), channel_id=1, source_target_pairs={{0,1},{1,2},{2,3},{3,4},{4,5},{5,6},{6,7},{7,0},{8,9},{9,10},{10,1... | collective-permute-start | bytes 589832 | tf_op jit(solution)/shard_map/ppermute | solution.py:29
  58.4 12.5 %all-gather.3.cloned.1.call-done = bf16[4,256,1536]{2,1,0:T(8,128)(2,1)} async-done(((bf16[4,32,1536]{2,1,0:T(8,128)(2,1)}), bf16[4,256,1536]{2,1,0:T(8,128)(2,1)}) %all-gather.3.cloned.1.call-update) | async-done | bytes 3145744 | tf_op jit(solution)/shard_map/all_gather | solution.py:50
  70.8 5.2 %fusion.10 = bf16[768,1024]{1,0:T(8,128)(2,1)S(1)} fusion(bf16[1024,1536]{1,0:T(8,128)(2,1)} %bitcast.60, bf16[384,1536]{1,0:T(8,128)(2,1)} %copy-done.2, bf16[384,1536]{1,0:T(8,128)(2,1)} %param.5), kind=kOutput, calls=%fused_computation.16 | convolution fusion | flops 2421424128 | bytes 7077888 | tf_op jit(solution)/shard_map/dot_general | solution.py:55
  76.1 1.6 %copy.7 = bf16[1024,2,384]{2,0,1:T(8,128)(2,1)} copy(bf16[1024,2,384]{0,2,1:T(8,128)(2,1)S(1)} %bitcast.55) | data formatting | bytes 3145728 | tf_op jit(solution)/shard_map/optimization_barrier | solution.py:57
  77.7 1.9 %collective-permute-start.8 = (bf16[4,8,32,1536]{3,2,1,0:T(8,128)(2,1)}, bf16[4,8,32,1536]{3,2,1,0:T(8,128)(2,1)S(1)}, u32[]{:S(2)}, u32[]{:S(2)}) collective-permute-start(bf16[4,8,32,1536]{3,2,1,0:T(8,128)(2,1)} %bitcast.61), channel_id=1, source_target_pairs={{0,8},{8,0},{1,9},{9,1},{2,10},{10,2},{3,11},{11,3},{4,12},{12,4},... | collective-permute-start | bytes 9437192 | tf_op jit(solution)/shard_map/ppermute | solution.py:59
  80.3 1.1 fusion.1
  82.2 1.4 %fusion.23 = f32[384,1536]{1,0:T(8,128)S(1)} fusion(bf16[1024,384]{1,0:T(8,128)(2,1)S(1)} %bitcast.58, bf16[1024,1536]{1,0:T(8,128)(2,1)S(1)} %bitcast.62), kind=kOutput, calls=%fused_computation.56 | convolution fusion | flops 1207959552 | bytes 6291456 | tf_op jit(solution)/shard_map/dot_general | solution.py:71
  83.6 1.9 %collective-permute-done.8 = bf16[4,8,32,1536]{3,2,1,0:T(8,128)(2,1)S(1)} collective-permute-done((bf16[4,8,32,1536]{3,2,1,0:T(8,128)(2,1)}, bf16[4,8,32,1536]{3,2,1,0:T(8,128)(2,1)S(1)}, u32[]{:S(2)}, u32[]{:S(2)}) %collective-permute-start.8) | collective-permute-done | bytes 3145760 | tf_op jit(solution)/shard_map/ppermute | solution.py:59
  85.5 2.5 %fusion.5 = bf16[384,1536]{1,0:T(8,128)(2,1)} fusion(f32[384,1536]{1,0:T(8,128)S(1)} %fusion.23, bf16[1024,384]{1,0:T(8,128)(2,1)S(1)} %bitcast.54, bf16[1024,1536]{1,0:T(8,128)(2,1)S(1)} %bitcast.53), kind=kOutput, calls=%fused_computation.11 | convolution fusion | flops 1209139200 | bytes 7471104 | tf_op jit(solution)/shard_map/dot_general | solution.py:72
  88.0 32.9 %reduce-scatter.2.cloned.1.call-done = bf16[128,2,384]{2,0,1:T(8,128)(2,1)} async-done(((bf16[1024,2,384]{2,0,1:T(8,128)(2,1)}), bf16[128,2,384]{2,0,1:T(8,128)(2,1)}) %reduce-scatter.2.cloned.1.call-update) | async-done | bytes 196624 | tf_op jit(solution)/shard_map/reduce_scatter | solution.py:58
  120.8 1.0 slice_bitcast_fusion.1
  121.8 3.9 %all_to_all.11 = bf16[2,128,384]{2,1,0:T(8,128)(2,1)S(1)} all-to-all(bf16[2,128,384]{2,1,0:T(8,128)(2,1)S(1)} %maximum_select_fusion), channel_id=1, replica_groups=mesh['rx'=4,'ry'=8,'rc'=2,'col'=8] {'rc'}, dimensions={0} | all-to-all | bytes 393216 | tf_op jit(solution)/shard_map/all_to_all | solution.py:77
  (36 shorter events, 3.0 us)
Async XLA Ops:
  7.2 63.7 %all-gather.3.cloned.1.call-start = ((), (), s32[]{:S(2)}) async-start(), calls=%async_computation.4 | async-start | bytes 3538944 | tf_op jit(solution)/shard_map/all_gather | solution.py:50
  22.4 98.5 %reduce-scatter.2.cloned.1.call-start = ((), (), s32[]{:S(2)}) async-start(), calls=%async_computation.3 | async-start | bytes 1769472 | tf_op jit(solution)/shard_map/reduce_scatter | solution.py:58
  22.4 35.9 %collective-permute-start.7 = (bf16[384,1536]{1,0:T(8,128)(2,1)}, bf16[384,1536]{1,0:T(8,128)(2,1)S(1)}, u32[]{:S(2)}, u32[]{:S(2)}) collective-permute-start(bf16[384,1536]{1,0:T(8,128)(2,1)} %param.5), channel_id=1, source_target_pairs={{0,8},{8,0},{1,9},{9,1},{2,10},{10,2},{3,11},{11,3},{4,12},{12,4},... | collective-permute-start | bytes 3538952 | tf_op jit(solution)/shard_map/ppermute | solution.py:46
  24.4 13.2 %collective-permute-start.3 = (bf16[256,384]{1,0:T(8,128)(2,1)}, bf16[256,384]{1,0:T(8,128)(2,1)S(1)}, u32[]{:S(2)}, u32[]{:S(2)}) collective-permute-start(bf16[256,384]{1,0:T(8,128)(2,1)} %param.4), channel_id=1, source_target_pairs={{0,1},{1,2},{2,3},{3,4},{4,5},{5,6},{6,7},{7,0},{8,9},{9,10},{10,1... | collective-permute-start | bytes 589832 | tf_op jit(solution)/shard_map/ppermute | solution.py:29
  26.3 13.2 %collective-permute-start = (bf16[256,384]{1,0:T(8,128)(2,1)}, bf16[256,384]{1,0:T(8,128)(2,1)S(1)}, u32[]{:S(2)}, u32[]{:S(2)}) collective-permute-start(bf16[256,384]{1,0:T(8,128)(2,1)} %param.4), channel_id=1, source_target_pairs={{0,7},{1,0},{2,1},{3,2},{4,3},{5,4},{6,5},{7,6},{8,15},{9,8},{10,9... | collective-permute-start | bytes 589832 | tf_op jit(solution)/shard_map/ppermute | solution.py:32
  37.5 9.8 %collective-permute-start.4 = (bf16[256,384]{1,0:T(8,128)(2,1)S(1)}, bf16[256,384]{1,0:T(8,128)(2,1)S(1)}, u32[]{:S(2)}, u32[]{:S(2)}) collective-permute-start(bf16[256,384]{1,0:T(8,128)(2,1)S(1)} %collective-permute-done.3), channel_id=1, source_target_pairs={{0,1},{1,2},{2,3},{3,4},{4,5},{5,6},{6,7},{7,0},{8,9},{9,10},{10,1... | collective-permute-start | bytes 589832 | tf_op jit(solution)/shard_map/ppermute | solution.py:29
  39.5 11.0 %collective-permute-start.1 = (bf16[256,384]{1,0:T(8,128)(2,1)S(1)}, bf16[256,384]{1,0:T(8,128)(2,1)S(1)}, u32[]{:S(2)}, u32[]{:S(2)}) collective-permute-start(bf16[256,384]{1,0:T(8,128)(2,1)S(1)} %collective-permute-done), channel_id=1, source_target_pairs={{0,7},{1,0},{2,1},{3,2},{4,3},{5,4},{6,5},{7,6},{8,15},{9,8},{10,9... | collective-permute-start | bytes 589832 | tf_op jit(solution)/shard_map/ppermute | solution.py:32
  47.4 9.1 %collective-permute-start.5 = (bf16[256,384]{1,0:T(8,128)(2,1)S(1)}, bf16[256,384]{1,0:T(8,128)(2,1)S(1)}, u32[]{:S(2)}, u32[]{:S(2)}) collective-permute-start(bf16[256,384]{1,0:T(8,128)(2,1)S(1)} %collective-permute-done.4), channel_id=1, source_target_pairs={{0,1},{1,2},{2,3},{3,4},{4,5},{5,6},{6,7},{7,0},{8,9},{9,10},{10,1... | collective-permute-start | bytes 589832 | tf_op jit(solution)/shard_map/ppermute | solution.py:29
  50.5 25.6 %collective-permute-start.2 = (bf16[256,384]{1,0:T(8,128)(2,1)S(1)}, bf16[256,384]{1,0:T(8,128)(2,1)S(1)}, u32[]{:S(2)}, u32[]{:S(2)}) collective-permute-start(bf16[256,384]{1,0:T(8,128)(2,1)S(1)} %collective-permute-done.1), channel_id=1, source_target_pairs={{0,7},{1,0},{2,1},{3,2},{4,3},{5,4},{6,5},{7,6},{8,15},{9,8},{10,9... | collective-permute-start | bytes 589832 | tf_op jit(solution)/shard_map/ppermute | solution.py:32
  56.4 19.7 %collective-permute-start.6 = (bf16[256,384]{1,0:T(8,128)(2,1)S(1)}, bf16[256,384]{1,0:T(8,128)(2,1)S(1)}, u32[]{:S(2)}, u32[]{:S(2)}) collective-permute-start(bf16[256,384]{1,0:T(8,128)(2,1)S(1)} %collective-permute-done.5), channel_id=1, source_target_pairs={{0,1},{1,2},{2,3},{3,4},{4,5},{5,6},{6,7},{7,0},{8,9},{9,10},{10,1... | collective-permute-start | bytes 589832 | tf_op jit(solution)/shard_map/ppermute | solution.py:29
  58.3 12.5 %copy-start.2 = (bf16[384,1536]{1,0:T(8,128)(2,1)}, bf16[384,1536]{1,0:T(8,128)(2,1)S(1)}, u32[]{:S(2)}) copy-start(bf16[384,1536]{1,0:T(8,128)(2,1)S(1)} %collective-permute-done.7) | copy-start | bytes 3538948
  76.1 1.6 %copy-start = (bf16[256,384]{1,0:T(8,128)(2,1)S(1)}, bf16[256,384]{1,0:T(8,128)(2,1)}, u32[]{:S(2)}) copy-start(bf16[256,384]{1,0:T(8,128)(2,1)} %param.4) | copy-start | bytes 589828
  77.7 7.8 %collective-permute-start.8 = (bf16[4,8,32,1536]{3,2,1,0:T(8,128)(2,1)}, bf16[4,8,32,1536]{3,2,1,0:T(8,128)(2,1)S(1)}, u32[]{:S(2)}, u32[]{:S(2)}) collective-permute-start(bf16[4,8,32,1536]{3,2,1,0:T(8,128)(2,1)} %bitcast.61), channel_id=1, source_target_pairs={{0,8},{8,0},{1,9},{9,1},{2,10},{10,2},{3,11},{11,3},{4,12},{12,4},... | collective-permute-start | bytes 9437192 | tf_op jit(solution)/shard_map/ppermute | solution.py:59
  80.3 1.9 %copy-start.1 = (bf16[4,256,1536]{2,1,0:T(8,128)(2,1)S(1)}, bf16[4,256,1536]{2,1,0:T(8,128)(2,1)}, u32[]{:S(2)}) copy-start(bf16[4,256,1536]{2,1,0:T(8,128)(2,1)} %all-gather.3.cloned.1.call-done) | copy-start | bytes 9437188
Sparse Core Ops, SparseCore 0:
  22.5 48.2 all-gather.2
  77.8 42.9 reduce-scatter.1
